TPU v7x, 256 devices: a whole 4x4x8 slice. The times are simulated.
256 devices in a mesh: mom: 64 (over z, x, core), en: 4 (over y).
Axes of the slice: x: 4, y: 4, z: 8, core: 2. Of those that a mesh axis runs over, the one named last changes fastest.
Arguments:
- slab_inverse: float32 [64, 8, 2, 2, 128, 128], P('mom', 'en')
- coupling: float32 [64, 2, 2, 128, 128], P('mom'), may hold values from -0.125 to 0.125
- injection: float32 [64, 8, 2, 128], P('mom', 'en'), may hold values from 0.2 to 2
- neighbors: int32 [2, 128, 32], replicated, may hold values from 0 to 127
- mode_shift: int32 [6], replicated, may hold values from 1 to 2, as said below
- mode_table: int32 [64, 64], P('mom'), may hold values from 0 to 5
- emit_weight: float32 [6], replicated, may hold values from 0.3 to 3
- absorb_weight: float32 [6], replicated, may hold values from 0.3 to 3
Outputs:
- self_energy: float32 [64, 8, 64, 2, 128], P('mom', 'en')
Inputs may be any that keep to these rules, and one draw needn't show every extreme that they name: `mode_shift`: some branch shifts by 2 grid steps and some by 1.
All inputs are finite; a program needn't handle non-finite values.
Results may differ from a plain program's by a relative error of at most 0.0003.
Values sent between devices are 32-bit elements; how exact they have to be, the bound alone decides.
No kernel may reach another device: no remote copies, remote signals or barrier semaphores. Data moves between devices by JAX's collectives and lax.ppermute only.
A program may use at most 128 MiB of HBM per device.

v0:
```python
import jax
import jax.numpy as jnp
from jax import lax
from jax.sharding import PartitionSpec as P

SHIFT_MAX = 2
OFFSETS = (-2, -1, 1, 2)


HIGH = lax.Precision.HIGHEST


def with_halo(x, sides, width):
    for axis, dim in sides:
        count, length = (lax.axis_size(axis), x.shape[dim])
        up = [(i, (i + 1) % count) for i in range(count - 1)]
        down = [(j, i) for i, j in up]
        last = lax.slice_in_dim(x, length - width, length, axis=dim)
        leading = lax.slice_in_dim(x, 0, width, axis=dim)
        before = lax.ppermute(last, axis, up)
        after = lax.ppermute(leading, axis, down)
        x = jnp.concatenate([before, x, after], axis=dim)
    return x


def product(left, right):
    return jnp.einsum("...ij,...jk->...ik", left, right, precision=HIGH)


def cmul(first, second):
    return (
        product(first[0], second[0]) - product(first[1], second[1]),
        product(first[0], second[1]) + product(first[1], second[0]),
    )


def adjoint(value):
    return (jnp.swapaxes(value[0], -1, -2), -jnp.swapaxes(value[1], -1, -2))


def slab_pairs(slab_inverse, coupling, injection, neighbors):
    orbitals = slab_inverse.shape[-1]
    slab_count = slab_inverse.shape[1]
    eye = jnp.eye(orbitals, dtype=jnp.float32)
    columns = jnp.arange(orbitals, dtype=jnp.int32)
    collected = []
    retarded = None
    lesser = None
    for slab in range(slab_count):
        inverse = (slab_inverse[:, slab, 0], slab_inverse[:, slab, 1])
        source = injection[:, slab][:, None, :]
        if slab == 0:
            retarded = inverse
            lesser = cmul((retarded[0] * source, retarded[1] * source), adjoint(retarded))
        else:
            link = (coupling[slab, 0], coupling[slab, 1])
            back = adjoint(link)
            sigma = cmul(cmul(link, retarded), back)
            inner = cmul(cmul(inverse, sigma), inverse)
            retarded = (inverse[0] + inner[0], inverse[1] + inner[1])
            middle = cmul(cmul(link, lesser), back)
            middle = (middle[0] + eye[None] * source, middle[1])
            lesser = cmul(cmul(retarded, middle), adjoint(retarded))
        selector = (neighbors[slab][:, :, None] == columns[None, None, :]).astype(jnp.float32)
        parts = [jnp.einsum("eoc,ojc->ejo", value, selector, precision=HIGH) for value in lesser]
        collected.append(jnp.stack(parts, axis=2))
    return jnp.concatenate(collected, axis=1)


def shift_weights(table_row, mode_shift, emit_weight, absorb_weight):
    mode_ids = jnp.arange(mode_shift.shape[0], dtype=jnp.int32)
    chosen = (table_row[:, None] == mode_ids[None, :]).astype(jnp.float32)
    shift = jnp.sum(chosen * mode_shift.astype(jnp.float32)[None], axis=1)
    emit = jnp.sum(chosen * emit_weight[None], axis=1)
    absorb = jnp.sum(chosen * absorb_weight[None], axis=1)
    rows = []
    for offset in OFFSETS:
        if offset < 0:
            rows.append(emit * (shift == -offset).astype(jnp.float32))
        else:
            rows.append(absorb * (shift == offset).astype(jnp.float32))
    return jnp.stack(rows) / table_row.shape[0]


def mix(data, weights, energies):
    total = None
    for index, offset in enumerate(OFFSETS):
        window = data[SHIFT_MAX + offset : SHIFT_MAX + offset + energies]
        term = jnp.einsum("kj,ejc->kec", weights[:, index], window, precision=HIGH)
        total = term if total is None else total + term
    return total


def shards(
    slab_inverse, coupling, injection, neighbors, mode_shift, mode_table, emit_weight, absorb_weight
):
    pairs = slab_pairs(slab_inverse[0], coupling[0], injection[0], neighbors)
    energies = pairs.shape[0]
    moms = lax.axis_size("mom")
    flat = pairs.reshape(energies, -1)
    width = flat.shape[1] // moms
    widened = with_halo(flat, (("en", 0),), SHIFT_MAX)
    blocks = widened.reshape(widened.shape[0], moms, width)
    weights = shift_weights(mode_table[0], mode_shift, emit_weight, absorb_weight).reshape(-1)
    extra = -(-weights.shape[0] // width)
    weights = jnp.pad(weights, (0, extra * width - weights.shape[0]))
    rows = jnp.broadcast_to(weights.reshape(extra, 1, width), (extra, moms, width))
    sent = lax.all_to_all(jnp.concatenate([blocks, rows], axis=0), "mom", 1, 1)
    data = sent[: widened.shape[0]]
    table = jnp.swapaxes(sent[widened.shape[0] :], 0, 1).reshape(moms, -1)
    table = table[:, : len(OFFSETS) * moms].reshape(moms, len(OFFSETS), moms)
    mixed = mix(data, table, energies)
    back = lax.all_to_all(mixed, "mom", 0, 0)
    result = jnp.swapaxes(back, 0, 1).reshape(pairs.shape)
    return result[None]


def solution(mesh):
    placed = (
        P("mom", "en", None, None, None, None),
        P("mom", None, None, None, None),
        P("mom", "en", None, None),
        P(),
        P(),
        P("mom", None),
        P(),
        P(),
    )
    return jax.shard_map(
        shards,
        mesh=mesh,
        in_specs=placed,
        out_specs=P("mom", "en", None, None, None),
        check_vma=False,
    )
```

profile of v0, /device:TPU:1, one launch (start us, length us, event | category | flops | bytes accessed | tf_op | source)
XLA Modules:
  0.0 82.4 jit_solution(231007226130115002)
XLA Ops:
  0.0 1.1 %copy.270 = f32[1,2,2,2,128,128]{5,4,1,3,2,0:T(8,128)S(1)} copy(f32[1,2,2,2,128,128]{5,4,3,2,1,0:T(8,128)} %param.8) | data formatting | bytes 1048576 | tf_op args[0]
  1.2 0.4 fusion.40
  1.6 0.4 fusion.39
  1.9 0.4 fusion.11
  2.3 0.4 fusion.48
  2.7 0.4 fusion.63
  3.1 0.4 fusion.10
  3.5 0.4 convolution_add_fusion.5
  3.9 0.4 convolution_subtract_fusion.2
  4.3 0.4 fusion.43
  4.7 0.4 fusion.41
  5.1 0.4 convolution_subtract_fusion.7
  5.5 0.4 fusion.44
  5.9 0.4 fusion.42
  6.3 0.4 fusion.21
  6.7 0.4 fusion.19
  7.2 0.1 copy.172
  7.3 0.4 convolution_subtract_fusion.8
  7.7 0.4 fusion.62
  8.1 2.2 %fusion.4 = f32[2,32,1,128]{1,0,3,2:T(2,128)S(1)} fusion(s32[128,32]{1,0:T(8,128)S(1)} %copy.172, f32[2,128,128]{2,1,0:T(8,128)S(1)} %convolution_subtract_fusion.8), kind=kOutput, calls=%fused_computation.6 | convolution fusion | flops 13107200 | bytes 180224 | tf_op jit(solution)/shard_map/eoc,ojc->ejo/dot_general | solution.py:65
  10.3 0.4 convolution_add_fusion.11
  10.6 2.0 %fusion.5 = f32[2,32,1,128]{1,0,3,2:T(2,128)S(1)} fusion(s32[128,32]{1,0:T(8,128)S(1)} %copy.172, f32[2,128,128]{2,1,0:T(8,128)S(1)} %convolution_add_fusion.11), kind=kOutput, calls=%fused_computation.7 | convolution fusion | flops 13107200 | bytes 180224 | tf_op jit(solution)/shard_map/eoc,ojc->ejo/dot_general | solution.py:65
  12.7 0.4 fusion.60
  13.1 0.4 fusion.9
  13.4 0.4 fusion.45
  13.8 0.4 fusion.61
  14.2 0.4 convolution_add_fusion.10
  14.6 0.4 fusion.13
  15.0 0.4 fusion.14
  15.4 0.4 fusion.8
  15.8 0.4 convolution_add_fusion.3
  16.2 0.4 fusion.12
  16.6 0.3 fusion.79
  16.9 0.3 fusion.81
  17.2 0.3 convolution_subtract_fusion.5
  17.4 0.4 fusion.32
  17.8 0.4 fusion.80
  18.2 0.1 copy.178
  18.5 0.3 convolution_add_fusion.8
  18.8 0.4 convolution_add_fusion.7
  19.2 0.4 convolution_subtract_fusion.4
  19.6 2.0 %fusion.6 = f32[2,32,1,128]{1,0,3,2:T(2,128)S(1)} fusion(s32[128,32]{1,0:T(8,128)S(1)} %copy.178, f32[2,128,128]{2,1,0:T(8,128)S(1)} %convolution_subtract_fusion.4), kind=kOutput, calls=%fused_computation.8 | convolution fusion | flops 13107200 | bytes 180224 | tf_op jit(solution)/shard_map/eoc,ojc->ejo/dot_general | solution.py:65
  21.7 2.0 %fusion.7 = f32[2,32,1,128]{1,0,3,2:T(2,128)S(1)} fusion(s32[128,32]{1,0:T(8,128)S(1)} %copy.178, f32[2,128,128]{2,1,0:T(8,128)S(1)} %convolution_add_fusion.7), kind=kOutput, calls=%fused_computation.9 | convolution fusion | flops 13107200 | bytes 180224 | tf_op jit(solution)/shard_map/eoc,ojc->ejo/dot_general | solution.py:65
  23.8 0.1 copy.207
  23.9 0.2 reshape.96
  24.1 1.3 %collective-permute-start.1 = (f32[2,16384]{1,0:T(2,128)S(1)}, f32[2,16384]{1,0:T(2,128)S(1)}, u32[]{:S(2)}, u32[]{:S(2)}) collective-permute-start(f32[2,16384]{1,0:T(2,128)S(1)} %reshape.96), channel_id=1, source_target_pairs={{1,0},{2,1},{3,2},{5,4},{6,5},{7,6},{9,8},{10,9},{11,10},{13,12},{... | collective-permute-start | bytes 393224 | tf_op jit(solution)/shard_map/ppermute | solution.py:21
  25.4 4.7 %collective-permute-start = (f32[2,16384]{1,0:T(2,128)S(1)}, f32[2,16384]{1,0:T(2,128)S(1)}, u32[]{:S(2)}, u32[]{:S(2)}) collective-permute-start(f32[2,16384]{1,0:T(2,128)S(1)} %reshape.96), channel_id=1, source_target_pairs={{0,1},{1,2},{2,3},{4,5},{5,6},{6,7},{8,9},{9,10},{10,11},{12,13},{... | collective-permute-start | bytes 393224 | tf_op jit(solution)/shard_map/ppermute | solution.py:20
  30.2 0.1 copy.208
  30.4 0.2 concatenate.17
  30.6 1.4 %collective-permute-done = f32[2,16384]{1,0:T(2,128)S(1)} collective-permute-done((f32[2,16384]{1,0:T(2,128)S(1)}, f32[2,16384]{1,0:T(2,128)S(1)}, u32[]{:S(2)}, u32[]{:S(2)}) %collective-permute-start) | collective-permute-done | bytes 131104 | tf_op jit(solution)/shard_map/ppermute | solution.py:20
  32.0 0.2 pad_maximum_fusion
  32.3 30.9 %all_to_all.10 = f32[7,64,256]{2,0,1:T(8,128)S(1)} all-to-all(f32[7,64,256]{2,0,1:T(8,128)S(1)} %pad_maximum_fusion), channel_id=1, replica_groups=mesh['mom'=64,'en'=4] {'mom'}, dimensions={1} | all-to-all | bytes 917504 | tf_op jit(solution)/shard_map/all_to_all | solution.py:108
  63.2 0.2 slice_reduce_fusion
  63.4 0.1 reshape_reshape_transpose.3
  63.5 0.1 fusion.77
  63.6 0.2 fusion.76
  63.8 0.3 fusion.26
  64.1 0.3 convolution_add_fusion.2
  64.3 0.3 convolution_add_fusion.1
  64.6 0.3 convolution_add_fusion
  64.9 0.1 copy.219
  65.0 16.6 %all_to_all.11 = f32[64,2,256]{2,1,0:T(2,128)S(1)} all-to-all(f32[64,2,256]{2,1,0:T(2,128)S(1)} %copy.219), channel_id=1, replica_groups=mesh['mom'=64,'en'=4] {'mom'}, dimensions={0} | all-to-all | bytes 262144 | tf_op jit(solution)/shard_map/all_to_all | solution.py:113
  81.6 0.2 broadcast_in_dim_reshape.3
  81.7 0.7 copy.220
  (29 shorter events, 0.6 us)
Async XLA Ops:
  0.0 1.1 %copy-start = (f32[1,2,2,128,128]{4,3,2,1,0:T(8,128)S(1)}, f32[1,2,2,128,128]{4,3,2,1,0:T(8,128)}, u32[]{:S(2)}) copy-start(f32[1,2,2,128,128]{4,3,2,1,0:T(8,128)} %param.9) | copy-start | bytes 786436
  5.5 0.8 copy-start.2
  5.9 1.2 %copy-start.1 = (s32[2,128,32]{1,2,0:T(8,128)S(1)}, s32[2,128,32]{1,2,0:T(8,128)}, u32[]{:S(2)}) copy-start(s32[2,128,32]{1,2,0:T(8,128)} %param.11) | copy-start | bytes 98308
  23.7 6.4 %copy-start.6 = (s32[6]{0:T(128)S(1)}, s32[6]{0:T(128)}, u32[]{:S(2)}) copy-start(s32[6]{0:T(128)} %param.12) | copy-start | bytes 76
  23.7 6.4 %copy-start.3 = (f32[6]{0:T(128)S(1)}, f32[6]{0:T(128)}, u32[]{:S(2)}) copy-start(f32[6]{0:T(128)} %param.14) | copy-start | bytes 76
  23.7 6.4 %copy-start.4 = (s32[1,64]{1,0:T(1,128)S(1)}, s32[1,64]{1,0:T(1,128)}, u32[]{:S(2)}) copy-start(s32[1,64]{1,0:T(1,128)} %param.13) | copy-start | bytes 772
  23.7 6.4 %copy-start.5 = (f32[6]{0:T(128)S(1)}, f32[6]{0:T(128)}, u32[]{:S(2)}) copy-start(f32[6]{0:T(128)} %param.15) | copy-start | bytes 76
  24.1 6.5 %collective-permute-start.1 = (f32[2,16384]{1,0:T(2,128)S(1)}, f32[2,16384]{1,0:T(2,128)S(1)}, u32[]{:S(2)}, u32[]{:S(2)}) collective-permute-start(f32[2,16384]{1,0:T(2,128)S(1)} %reshape.96), channel_id=1, source_target_pairs={{1,0},{2,1},{3,2},{5,4},{6,5},{7,6},{9,8},{10,9},{11,10},{13,12},{... | collective-permute-start | bytes 393224 | tf_op jit(solution)/shard_map/ppermute | solution.py:21
  25.4 6.6 %collective-permute-start = (f32[2,16384]{1,0:T(2,128)S(1)}, f32[2,16384]{1,0:T(2,128)S(1)}, u32[]{:S(2)}, u32[]{:S(2)}) collective-permute-start(f32[2,16384]{1,0:T(2,128)S(1)} %reshape.96), channel_id=1, source_target_pairs={{0,1},{1,2},{2,3},{4,5},{5,6},{6,7},{8,9},{9,10},{10,11},{12,13},{... | collective-permute-start | bytes 393224 | tf_op jit(solution)/shard_map/ppermute | solution.py:20
where the time goes:
time: 83 us; the launch traced here: 82.4 us
  blocking collectives  47.5 us (57%)
  matrix products  22.8 us (27%)
  starting transfers between devices  5.95 us (7%)
  local copies, waits for them, and re-layouts  3.81 us (5%)
  waiting for transfers between devices  1.4 us (2%)
    all_to_all x1, blocking collectives, shards(): sent = lax.all_to_all(jnp.concatenate([blocks, rows], axis=0), 'mom', 1, 1)  30.9 us
    all_to_all x1, blocking collectives, shards(): back = lax.all_to_all(mixed, 'mom', 0, 0)  16.6 us
    dot_general x36, matrix products, product(): return jnp.einsum('...ij,...jk->...ik', left, right, precision=HIGH)  13.5 us
    dot_general x4, matrix products, slab_pairs(): jnp.einsum('eoc,ojc->ejo', value, selector, precision=HIGH)  8.23 us
    ppermute x1, starting transfers between devices, with_halo(): before = lax.ppermute(last, axis, up)  4.65 us
  transfers between devices with their start and end apart: 2, of which 1 were waited for; matrix products, arithmetic and copies ran while one was open for 1% of the time, Pallas kernels for 0%

commit v1 on v0

--- a/solution.py
+++ b/solution.py
@@ -85,8 +85,8 @@
 def mix(data, weights, energies):
     total = None
     for index, offset in enumerate(OFFSETS):
-        window = data[SHIFT_MAX + offset : SHIFT_MAX + offset + energies]
-        term = jnp.einsum("kj,ejc->kec", weights[:, index], window, precision=HIGH)
+        window = data[:, SHIFT_MAX + offset : SHIFT_MAX + offset + energies]
+        term = jnp.einsum("kj,jec->kec", weights[:, index], window, precision=HIGH)
         total = term if total is None else total + term
     return total
 
@@ -95,22 +95,25 @@
     slab_inverse, coupling, injection, neighbors, mode_shift, mode_table, emit_weight, absorb_weight
 ):
     pairs = slab_pairs(slab_inverse[0], coupling[0], injection[0], neighbors)
-    energies = pairs.shape[0]
-    moms = lax.axis_size("mom")
-    flat = pairs.reshape(energies, -1)
-    width = flat.shape[1] // moms
-    widened = with_halo(flat, (("en", 0),), SHIFT_MAX)
-    blocks = widened.reshape(widened.shape[0], moms, width)
+    local = pairs.shape[0]
+    moms, groups = lax.axis_size("mom"), lax.axis_size("en")
+    devices = moms * groups
+    flat = pairs.reshape(local, -1)
+    width = flat.shape[1] // devices
+    blocks = jnp.swapaxes(flat.reshape(local, devices, width), 0, 1)
     weights = shift_weights(mode_table[0], mode_shift, emit_weight, absorb_weight).reshape(-1)
-    extra = -(-weights.shape[0] // width)
-    weights = jnp.pad(weights, (0, extra * width - weights.shape[0]))
-    rows = jnp.broadcast_to(weights.reshape(extra, 1, width), (extra, moms, width))
-    sent = lax.all_to_all(jnp.concatenate([blocks, rows], axis=0), "mom", 1, 1)
-    data = sent[: widened.shape[0]]
-    table = jnp.swapaxes(sent[widened.shape[0] :], 0, 1).reshape(moms, -1)
-    table = table[:, : len(OFFSETS) * moms].reshape(moms, len(OFFSETS), moms)
-    mixed = mix(data, table, energies)
-    back = lax.all_to_all(mixed, "mom", 0, 0)
+    share = -(-weights.shape[0] // (groups * width)) * width
+    weights = jnp.pad(weights, (0, share * groups - weights.shape[0]))
+    mine = lax.dynamic_slice_in_dim(weights, lax.axis_index("en") * share, share)
+    rows = jnp.broadcast_to(mine.reshape(1, -1, width), (devices, share // width, width))
+    sent = lax.all_to_all(jnp.concatenate([blocks, rows], axis=1), ("mom", "en"), 0, 0)
+    sent = sent.reshape(moms, groups, local + share // width, width)
+    data = sent[:, :, :local].reshape(moms, groups * local, width)
+    data = jnp.pad(data, ((0, 0), (SHIFT_MAX, SHIFT_MAX), (0, 0)))
+    table = sent[:, :, local:].reshape(moms, -1)[:, : len(OFFSETS) * moms]
+    mixed = mix(data, table.reshape(moms, len(OFFSETS), moms), groups * local)
+    mixed = mixed.reshape(devices, local, width)
+    back = lax.all_to_all(mixed, ("mom", "en"), 0, 0)
     result = jnp.swapaxes(back, 0, 1).reshape(pairs.shape)
     return result[None]
 

time: 83 us -> 80.1 us (0.965)
  starting transfers between devices: 5.95 us -> 0 us
  other arithmetic: 0.39 us -> 2.4 us
  waiting for transfers between devices: 1.4 us -> 0 us
  blocking collectives: 47.5 us -> 48.8 us
  local copies, waits for them, and re-layouts: 3.81 us -> 5.06 us
    ppermute x2 -> x0, starting transfers between devices: 5.95 us -> none  [the longest x1 4.65 us: with_halo(): before = lax.ppermute(last, axis, up)]
    all_to_all x0 -> x2, other arithmetic: none -> 2.22 us  [the longest x1 1.27 us: shards(): lax.all_to_all(jnp.concatenate([blocks, rows], axis=1), ('mom', 'en'), 0, 0)]
    ppermute x2 -> x0, waiting for transfers between devices: 1.4 us -> none  [the longest x1 1.39 us: with_halo(): before = lax.ppermute(last, axis, up)]
    all_to_all x2, blocking collectives: 47.5 us -> 48.8 us  [the longest x1 30.7 us: shards(): lax.all_to_all(jnp.concatenate([blocks, rows], axis=1), ('mom', 'en'), 0, 0)]
    unnamed x15 -> x20, local copies, waits for them, and re-layouts: 1.16 us -> 2.29 us
  transfers between devices with their start and end apart: 2 -> 0, of which waited for: 1 -> 0; matrix products, arithmetic and copies ran while one was open for 1% -> 0% of each run, Pallas kernels for 0% -> 0%
where the time goes in v1:
time: 80.1 us; the launch traced here: 80 us
  blocking collectives  48.8 us (61%)
  matrix products  23.1 us (29%)
  local copies, waits for them, and re-layouts  5.06 us (6%)
  other arithmetic  2.4 us (3%)
    all_to_all x1, blocking collectives, shards(): lax.all_to_all(jnp.concatenate([blocks, rows], axis=1), ('mom', 'en'), 0, 0)  30.7 us
    all_to_all x1, blocking collectives, shards(): back = lax.all_to_all(mixed, ('mom', 'en'), 0, 0)  18 us
    dot_general x36, matrix products, product(): return jnp.einsum('...ij,...jk->...ik', left, right, precision=HIGH)  13.5 us
    dot_general x4, matrix products, slab_pairs(): jnp.einsum('eoc,ojc->ejo', value, selector, precision=HIGH)  8.22 us
    unnamed x20, local copies, waits for them, and re-layouts  2.29 us

profile of v1, /device:TPU:1, one launch (start us, length us, event | category | flops | bytes accessed | tf_op | source)
XLA Modules:
  0.0 80.0 jit_solution(4663105694780806304)
XLA Ops:
  0.0 1.1 %copy.192 = f32[1,2,2,2,128,128]{5,4,1,3,2,0:T(8,128)S(1)} copy(f32[1,2,2,2,128,128]{5,4,3,2,1,0:T(8,128)} %param.8) | data formatting | bytes 1048576 | tf_op args[0]
  1.2 0.4 fusion.36
  1.6 0.4 fusion.35
  1.9 0.4 fusion.11
  2.3 0.4 fusion.44
  2.7 0.4 fusion.59
  3.1 0.4 fusion.10
  3.5 0.4 convolution_add_fusion.5
  3.9 0.4 convolution_subtract_fusion.2
  4.3 0.4 fusion.39
  4.7 0.4 fusion.37
  5.1 0.4 convolution_subtract_fusion.7
  5.5 0.4 fusion.40
  5.9 0.4 fusion.38
  6.3 0.4 fusion.22
  6.7 0.4 fusion.20
  7.2 0.1 copy.115
  7.3 0.4 convolution_subtract_fusion.8
  7.7 0.4 fusion.58
  8.1 2.2 %fusion.4 = f32[2,32,1,128]{1,0,3,2:T(2,128)S(1)} fusion(s32[128,32]{1,0:T(8,128)S(1)} %copy.115, f32[2,128,128]{2,1,0:T(8,128)S(1)} %convolution_subtract_fusion.8), kind=kOutput, calls=%fused_computation.9 | convolution fusion | flops 13107200 | bytes 180224 | tf_op jit(solution)/shard_map/eoc,ojc->ejo/dot_general | solution.py:65
  10.3 0.4 convolution_add_fusion.11
  10.6 2.0 %fusion.5 = f32[2,32,1,128]{1,0,3,2:T(2,128)S(1)} fusion(s32[128,32]{1,0:T(8,128)S(1)} %copy.115, f32[2,128,128]{2,1,0:T(8,128)S(1)} %convolution_add_fusion.11), kind=kOutput, calls=%fused_computation.10 | convolution fusion | flops 13107200 | bytes 180224 | tf_op jit(solution)/shard_map/eoc,ojc->ejo/dot_general | solution.py:65
  12.7 0.4 fusion.56
  13.1 0.4 fusion.9
  13.4 0.4 fusion.41
  13.8 0.4 fusion.57
  14.2 0.4 convolution_add_fusion.10
  14.6 0.4 fusion.13
  15.0 0.4 fusion.14
  15.4 0.4 fusion.8
  15.8 0.4 convolution_add_fusion.3
  16.2 0.4 fusion.12
  16.6 0.3 fusion.77
  16.9 0.3 fusion.79
  17.2 0.3 convolution_subtract_fusion.5
  17.5 0.4 fusion.28
  17.9 0.4 fusion.78
  18.3 0.1 select_reduce_fusion.1
  18.5 0.1 div.10
  18.5 0.1 copy.121
  18.7 0.1 copy.120
  18.8 0.3 convolution_add_fusion.8
  19.1 0.4 convolution_add_fusion.7
  19.5 0.4 convolution_subtract_fusion.4
  19.9 2.0 %fusion.6 = f32[2,32,1,128]{1,0,3,2:T(2,128)S(1)} fusion(s32[128,32]{1,0:T(8,128)S(1)} %copy.121, f32[2,128,128]{2,1,0:T(8,128)S(1)} %convolution_subtract_fusion.4), kind=kOutput, calls=%fused_computation.11 | convolution fusion | flops 13107200 | bytes 180224 | tf_op jit(solution)/shard_map/eoc,ojc->ejo/dot_general | solution.py:65
  21.9 2.0 %fusion.7 = f32[2,32,1,128]{1,0,3,2:T(2,128)S(1)} fusion(s32[128,32]{1,0:T(8,128)S(1)} %copy.121, f32[2,128,128]{2,1,0:T(8,128)S(1)} %convolution_add_fusion.7), kind=kOutput, calls=%fused_computation.12 | convolution fusion | flops 13107200 | bytes 180224 | tf_op jit(solution)/shard_map/eoc,ojc->ejo/dot_general | solution.py:65
  24.1 0.1 copy.150
  24.2 0.2 reshape_reshape.6
  24.5 0.3 copy.151
  24.8 0.5 reshape.103
  25.3 30.7 %all_to_all.10 = f32[256,1,192]{2,1,0:T(1,128)S(1)} all-to-all(f32[256,1,192]{2,1,0:T(1,128)S(1)} %reshape.103), channel_id=1, replica_groups=mesh['mom'=64,'en'=4] {'mom','en'}, dimensions={0} | all-to-all | bytes 393216 | tf_op jit(solution)/shard_map/all_to_all | solution.py:109
  56.0 0.5 broadcast.102
  56.5 1.3 %reduce = f32[256,192]{1,0:T(8,128)S(1)} reduce(f32[256,1,192]{2,1,0:T(1,128)S(1)} %all_to_all.10, f32[]{:T(128)} %broadcast.102), dimensions={1}, to_apply=%all_to_all.6.reduce_sub_computation | reduce | bytes 393220 | tf_op jit(solution)/shard_map/all_to_all | solution.py:109
  57.8 0.2 reshape.104
  58.1 0.3 fusion.19
  58.4 0.4 convolution_add_fusion.2
  58.8 0.3 convolution_add_fusion.1
  59.2 0.3 convolution_add_fusion
  59.5 0.2 copy.155
  59.7 0.3 reshape.105
  60.0 18.0 %all_to_all.11 = f32[256,1,128]{2,1,0:T(1,128)S(1)} all-to-all(f32[256,1,128]{2,1,0:T(1,128)S(1)} %reshape.105), channel_id=1, replica_groups=mesh['mom'=64,'en'=4] {'mom','en'}, dimensions={0} | all-to-all | bytes 262144 | tf_op jit(solution)/shard_map/all_to_all | solution.py:116
  78.0 0.9 %reduce.1 = f32[256,128]{1,0:T(8,128)S(1)} reduce(f32[256,1,128]{2,1,0:T(1,128)S(1)} %all_to_all.11, f32[]{:T(128)} %broadcast.102), dimensions={1}, to_apply=%all_to_all.7.reduce_sub_computation | reduce | bytes 262148 | tf_op jit(solution)/shard_map/all_to_all | solution.py:116
  79.0 0.2 reshape.106
  79.2 0.8 broadcast_in_dim_reshape.3
  (33 shorter events, 0.5 us)
Async XLA Ops:
  0.0 1.1 %copy-start = (f32[1,2,2,128,128]{4,3,2,1,0:T(8,128)S(1)}, f32[1,2,2,128,128]{4,3,2,1,0:T(8,128)}, u32[]{:S(2)}) copy-start(f32[1,2,2,128,128]{4,3,2,1,0:T(8,128)} %param.9) | copy-start | bytes 786436
  5.5 0.8 %copy-start.2 = (f32[1,2,2,128]{3,2,1,0:T(2,128)S(1)}, f32[1,2,2,128]{3,2,1,0:T(2,128)}, u32[]{:S(2)}) copy-start(f32[1,2,2,128]{3,2,1,0:T(2,128)} %param.10) | copy-start | bytes 6148
  5.9 1.2 %copy-start.1 = (s32[2,128,32]{1,2,0:T(8,128)S(1)}, s32[2,128,32]{1,2,0:T(8,128)}, u32[]{:S(2)}) copy-start(s32[2,128,32]{1,2,0:T(8,128)} %param.11) | copy-start | bytes 98308
  17.4 0.8 %copy-start.6 = (s32[6]{0:T(128)S(1)}, s32[6]{0:T(128)}, u32[]{:S(2)}) copy-start(s32[6]{0:T(128)} %param.12) | copy-start | bytes 76
  17.5 0.9 %copy-start.3 = (f32[6]{0:T(128)S(1)}, f32[6]{0:T(128)}, u32[]{:S(2)}) copy-start(f32[6]{0:T(128)} %param.14) | copy-start | bytes 76
  17.5 0.9 %copy-start.4 = (s32[1,64]{1,0:T(1,128)S(1)}, s32[1,64]{1,0:T(1,128)}, u32[]{:S(2)}) copy-start(s32[1,64]{1,0:T(1,128)} %param.13) | copy-start | bytes 772
  17.5 0.8 %copy-start.5 = (f32[6]{0:T(128)S(1)}, f32[6]{0:T(128)}, u32[]{:S(2)}) copy-start(f32[6]{0:T(128)} %param.15) | copy-start | bytes 76

commit v2 on v1

--- a/solution.py
+++ b/solution.py
@@ -23,48 +23,59 @@
     return x
 
 
-def product(left, right):
-    return jnp.einsum("...ij,...jk->...ik", left, right, precision=HIGH)
+def block(value):
+    real, imag = value[..., 0, :, :], value[..., 1, :, :]
+    top = jnp.concatenate([real, -imag], axis=-1)
+    bottom = jnp.concatenate([imag, real], axis=-1)
+    return jnp.concatenate([top, bottom], axis=-2)
 
 
-def cmul(first, second):
-    return (
-        product(first[0], second[0]) - product(first[1], second[1]),
-        product(first[0], second[1]) + product(first[1], second[0]),
-    )
+def column(value, adjoint=False):
+    real, imag = value[..., 0, :, :], value[..., 1, :, :]
+    if adjoint:
+        real, imag = jnp.swapaxes(real, -1, -2), -jnp.swapaxes(imag, -1, -2)
+    return jnp.concatenate([real, imag], axis=-2)
 
 
-def adjoint(value):
-    return (jnp.swapaxes(value[0], -1, -2), -jnp.swapaxes(value[1], -1, -2))
+def split(value):
+    rows = value.shape[-2] // 2
+    return value.reshape(value.shape[:-2] + (2, rows, value.shape[-1]))
+
+
+def cmul(left, right, spec="...ij,...jk->...ik", adjoint=False):
+    product = jnp.einsum(spec, block(left), column(right, adjoint), precision=HIGH)
+    return split(product)
 
 
 def slab_pairs(slab_inverse, coupling, injection, neighbors):
     orbitals = slab_inverse.shape[-1]
     slab_count = slab_inverse.shape[1]
     eye = jnp.eye(orbitals, dtype=jnp.float32)
-    columns = jnp.arange(orbitals, dtype=jnp.int32)
-    collected = []
-    retarded = None
-    lesser = None
-    for slab in range(slab_count):
-        inverse = (slab_inverse[:, slab, 0], slab_inverse[:, slab, 1])
-        source = injection[:, slab][:, None, :]
-        if slab == 0:
-            retarded = inverse
-            lesser = cmul((retarded[0] * source, retarded[1] * source), adjoint(retarded))
-        else:
-            link = (coupling[slab, 0], coupling[slab, 1])
-            back = adjoint(link)
-            sigma = cmul(cmul(link, retarded), back)
-            inner = cmul(cmul(inverse, sigma), inverse)
-            retarded = (inverse[0] + inner[0], inverse[1] + inner[1])
-            middle = cmul(cmul(link, lesser), back)
-            middle = (middle[0] + eye[None] * source, middle[1])
-            lesser = cmul(cmul(retarded, middle), adjoint(retarded))
-        selector = (neighbors[slab][:, :, None] == columns[None, None, :]).astype(jnp.float32)
-        parts = [jnp.einsum("eoc,ojc->ejo", value, selector, precision=HIGH) for value in lesser]
-        collected.append(jnp.stack(parts, axis=2))
-    return jnp.concatenate(collected, axis=1)
+    retarded = slab_inverse[:, 0]
+    source = injection[:, 0][:, None, None, :]
+    lesser = cmul(retarded * source, retarded, adjoint=True)
+    collected = [lesser]
+    for slab in range(1, slab_count):
+        inverse = slab_inverse[:, slab]
+        link = coupling[slab]
+        both = jnp.concatenate([retarded, lesser], axis=-1)
+        linked = cmul(link, both, "ij,ejk->eik")
+        linked = jnp.stack([linked[..., :orbitals], linked[..., orbitals:]], axis=1)
+        sandwich = cmul(linked, link, "ewij,jk->ewik", adjoint=True)
+        sigma, middle = sandwich[:, 0], sandwich[:, 1]
+        diagonal = eye[None] * injection[:, slab][:, None, :]
+        middle = jnp.stack([middle[:, 0] + diagonal, middle[:, 1]], axis=1)
+        inner = cmul(cmul(inverse, sigma), inverse)
+        retarded = inverse + inner
+        lesser = cmul(cmul(retarded, middle), retarded, adjoint=True)
+        collected.append(lesser)
+    stacked = jnp.stack(collected, axis=1)
+    index = jnp.broadcast_to(
+        neighbors[None, :, None, :, :], stacked.shape[:3] + neighbors.shape[1:]
+    )
+    picked = jnp.take_along_axis(stacked, index, axis=-1)
+    picked = jnp.transpose(picked, (0, 1, 4, 2, 3))
+    return picked.reshape(picked.shape[0], -1, picked.shape[3], picked.shape[4])
 
 
 def shift_weights(table_row, mode_shift, emit_weight, absorb_weight):

time: 80.1 us -> 442 us (5.52)
  local copies, waits for them, and re-layouts: 5.06 us -> 380 us
  matrix products: 23.1 us -> 7.35 us
    gather x0 -> x4, local copies, waits for them, and re-layouts: none -> 372 us  [slab_pairs(): picked = jnp.take_along_axis(stacked, index, axis=-1)]
    dot_general x40 -> x7, matrix products: 21.8 us -> 5.97 us  [cmul(): jnp.einsum(spec, block(left), column(right, adjoint), precision=HIGH)]
where the time goes in v2:
time: 442 us; the launch traced here: 441 us
  local copies, waits for them, and re-layouts  380 us (86%)
  blocking collectives  48.8 us (11%)
  matrix products  7.35 us (2%)
    gather x4, local copies, waits for them, and re-layouts, slab_pairs(): picked = jnp.take_along_axis(stacked, index, axis=-1)  372 us
    all_to_all x1, blocking collectives, shards(): lax.all_to_all(jnp.concatenate([blocks, rows], axis=1), ('mom', 'en'), 0, 0)  30.8 us
    all_to_all x1, blocking collectives, shards(): back = lax.all_to_all(mixed, ('mom', 'en'), 0, 0)  18 us

profile of v2, /device:TPU:1, one launch (start us, length us, event | category | flops | bytes accessed | tf_op | source)
XLA Modules:
  0.0 441.2 jit_solution(13691872553289152575)
XLA Ops:
  0.0 1.2 copy.119
  1.2 0.0 copy-start.5
  1.3 0.6 copy-done.5
  1.9 0.1 broadcast_multiply_fusion
  2.0 0.0 copy-start.2
  2.1 0.9 copy-done.2
  3.1 1.0 fusion.8
  4.1 0.1 copy.121
  4.3 0.6 fusion.24
  5.1 1.0 fusion
  6.2 1.0 fusion.16
  7.3 0.6 fusion.28
  7.9 0.1 copy.131
  8.3 1.0 fusion.36
  9.3 0.0 copy-start
  9.4 0.7 copy-done
  10.1 0.6 fusion.101
  10.7 0.6 fusion.116
  11.3 0.2 copy.136
  11.6 0.2 reshape.136
  11.7 0.6 fusion.44
  12.4 371.1 %gather_fusion = f32[32768]{0:T(1024)S(1)} fusion(f32[2,2,2,128,128]{4,3,2,0,1:T(8,128)S(1)} %pad_maximum_fusion, s32[32768]{0:T(1024)S(1)} %reshape.136), kind=kCustom, calls=%fused_computation | custom fusion | bytes 917504 | tf_op jit(solution)/shard_map/jit(take_along_axis)/gather | solution.py:76
  383.5 0.0 copy-start.3
  383.5 0.0 copy-start.1
  383.5 0.0 copy-start.4
  383.5 0.2 reshape.139
  383.7 0.5 copy-done.3
  384.2 0.1 copy.117
  384.3 0.0 copy-done.1
  384.3 0.1 copy.118
  384.4 0.0 copy-done.4
  384.4 0.1 copy.116
  384.6 0.1 bitcast_select_fusion
  384.6 0.0 copy-start.9
  384.7 0.0 copy-start.6
  384.7 0.0 copy-start.7
  384.7 0.0 copy-start.8
  384.7 0.2 copy.137
  384.9 0.2 reshape_reshape_reshape.3
  385.1 0.2 copy-done.9
  385.3 0.0 copy-done.6
  385.3 0.0 copy-done.7
  385.3 0.0 copy-done.8
  385.3 0.1 select_reduce_fusion.1
  385.5 0.1 div.10
  385.5 0.1 dynamic_slice.3
  385.7 0.3 copy.138
  386.0 0.5 reshape.148
  386.4 30.8 %all_to_all.10 = f32[256,1,192]{2,1,0:T(1,128)S(1)} all-to-all(f32[256,1,192]{2,1,0:T(1,128)S(1)} %reshape.148), channel_id=1, replica_groups=mesh['mom'=64,'en'=4] {'mom','en'}, dimensions={0} | all-to-all | bytes 393216 | tf_op jit(solution)/shard_map/all_to_all | solution.py:120
  417.2 0.5 broadcast.182
  417.7 1.3 reduce
  419.0 0.2 reshape.149
  419.3 0.3 fusion.53
  419.6 0.4 convolution_add_fusion.2
  420.0 0.3 convolution_add_fusion.1
  420.4 0.3 convolution_add_fusion
  420.7 0.2 copy.142
  420.9 0.3 reshape.150
  421.1 18.0 %all_to_all.11 = f32[256,1,128]{2,1,0:T(1,128)S(1)} all-to-all(f32[256,1,128]{2,1,0:T(1,128)S(1)} %reshape.150), channel_id=1, replica_groups=mesh['mom'=64,'en'=4] {'mom','en'}, dimensions={0} | all-to-all | bytes 262144 | tf_op jit(solution)/shard_map/all_to_all | solution.py:127
  439.2 0.9 reduce.1
  440.1 0.2 reshape.151
  440.4 0.8 broadcast_in_dim_reshape.3
  (42 shorter events, 0.8 us)
Async XLA Ops:
  1.2 0.7 copy-start.5
  2.0 1.0 copy-start.2
  9.3 0.8 copy-start
  383.5 0.8 copy-start.3
  383.5 0.9 copy-start.1
  383.5 1.0 copy-start.4
  384.6 0.7 copy-start.9
  384.7 0.7 copy-start.6
  384.7 0.7 copy-start.7
  384.7 0.7 copy-start.8

commit v3 on v2

--- a/solution.py
+++ b/solution.py
@@ -70,11 +70,18 @@
         lesser = cmul(cmul(retarded, middle), retarded, adjoint=True)
         collected.append(lesser)
     stacked = jnp.stack(collected, axis=1)
-    index = jnp.broadcast_to(
-        neighbors[None, :, None, :, :], stacked.shape[:3] + neighbors.shape[1:]
+    pieces = []
+    rest = stacked
+    for _ in range(3):
+        piece = rest.astype(jnp.bfloat16)
+        pieces.append(piece)
+        rest = rest - piece.astype(jnp.float32)
+    columns = jnp.arange(orbitals, dtype=jnp.int32)
+    selector = (neighbors[..., None] == columns).astype(jnp.bfloat16)
+    picked = jnp.einsum(
+        "qesxoc,sojc->qesjxo", jnp.stack(pieces), selector, preferred_element_type=jnp.float32
     )
-    picked = jnp.take_along_axis(stacked, index, axis=-1)
-    picked = jnp.transpose(picked, (0, 1, 4, 2, 3))
+    picked = picked[0] + picked[1] + picked[2]
     return picked.reshape(picked.shape[0], -1, picked.shape[3], picked.shape[4])
 
 

time: 442 us -> 71 us (0.16)
  local copies, waits for them, and re-layouts: 380 us -> 6.3 us
    gather x4 -> x0, local copies, waits for them, and re-layouts: 372 us -> none  [slab_pairs(): picked = jnp.take_along_axis(stacked, index, axis=-1)]
where the time goes in v3:
time: 71 us; the launch traced here: 70.8 us
  blocking collectives  48.8 us (69%)
  matrix products  10.7 us (15%)
  local copies, waits for them, and re-layouts  6.3 us (9%)
  other arithmetic  4.41 us (6%)
    all_to_all x1, blocking collectives, shards(): lax.all_to_all(jnp.concatenate([blocks, rows], axis=1), ('mom', 'en'), 0, 0)  30.7 us
    all_to_all x1, blocking collectives, shards(): back = lax.all_to_all(mixed, ('mom', 'en'), 0, 0)  18 us
    dot_general x7, matrix products, cmul(): jnp.einsum(spec, block(left), column(right, adjoint), precision=HIGH)  5.98 us
    dot_general x1, matrix products, slab_pairs(): jnp.einsum('qesxoc,sojc->qesjxo', jnp.stack(pieces), selector, preferred_...  3.36 us
    unnamed x26, local copies, waits for them, and re-layouts  2.89 us

profile of v3, /device:TPU:1, one launch (start us, length us, event | category | flops | bytes accessed | tf_op | source)
XLA Modules:
  0.0 70.8 jit_solution(13275496974412259684)
XLA Ops:
  0.0 0.0 copy-start.2
  0.0 0.0 copy-start
  0.0 1.3 %copy.81 = f32[1,2,2,2,128,128]{4,5,1,3,2,0:T(8,128)S(1)} copy(f32[1,2,2,2,128,128]{5,4,3,2,1,0:T(8,128)} %param.8) | data formatting | bytes 1048576 | tf_op args[0]
  1.3 0.0 copy-done.2
  1.4 0.1 broadcast_multiply_fusion
  1.5 0.0 copy-done
  1.6 1.0 %fusion.20 = f32[2,256,128]{2,1,0:T(8,128)S(1)} fusion(f32[2,128,128]{1,2,0:T(8,128)S(1)} %get-tuple-element.42, f32[2,128,128]{1,2,0:T(8,128)S(1)} %get-tuple-element.41, f32[2,128,128]{1,2,0:T(8,128)S(1)} %fusion.116, f32[2,128,128]{2,1,0:T(8,128)S(1)} %get-tuple-element.51, f32[2,128,128]{2,1,0:T(8,128)S(1)} %get-tuple-element.52), kind=kOutput, calls=%fused_computation.23 | convolution fusion | flops 201785344 | bytes 917504 | tf_op jit(solution)/shard_map/...ij,...jk->...ik/dot_general | solution.py:46
  2.7 0.1 copy.83
  2.8 0.6 fusion.36
  3.7 1.0 %fusion.7 = f32[2,2,256,128]{3,2,1,0:T(8,128)S(1)} fusion(f32[2,2,128,128]{3,2,1,0:T(8,128)S(1)} %fusion.66, f32[2,2,128,128]{3,2,1,0:T(8,128)S(1)} %get-tuple-element.9, f32[2,2,128,128]{3,2,1,0:T(8,128)S(1)} %get-tuple-element.8, f32[128,128]{0,1:T(8,128)S(1)} %get-tuple-element.35, f32[128,128]{0,1:T(8,128)S(1)} %get-tuple-element.32), kind=kOutput, calls=%fused_computation.8 | convolution fusion | flops 403472384 | bytes 1441792 | tf_op jit(solution)/shard_map/ewij,jk->ewik/dot_general | solution.py:46
  4.8 1.0 %fusion.28 = f32[2,256,128]{2,1,0:T(8,128)S(1)} fusion(f32[2,128,128]{1,2,0:T(8,128)S(1)} %get-tuple-element.38, f32[2,128,128]{1,2,0:T(8,128)S(1)} %get-tuple-element.37, f32[2,128,128]{1,2,0:T(8,128)S(1)} %fusion.117, f32[2,128,128]{2,1,0:T(8,128)S(1)} %get-tuple-element.31, f32[2,128,128]{2,1,0:T(8,128)S(1)} %get-tuple-element.30), kind=kOutput, calls=%fused_computation.31 | convolution fusion | flops 201785344 | bytes 917504 | tf_op jit(solution)/shard_map/...ij,...jk->...ik/dot_general | solution.py:46
  5.9 0.6 fusion.40
  6.5 0.1 copy.93
  6.8 1.0 %fusion.48 = f32[2,256,128]{2,1,0:T(8,128)S(1)} fusion(f32[2,128,128]{1,2,0:T(8,128)S(1)} %get-tuple-element.23, f32[2,128,128]{1,2,0:T(8,128)S(1)} %get-tuple-element.22, f32[2,128,128]{1,2,0:T(8,128)S(1)} %get-tuple-element.25, f32[2,128,128]{2,1,0:T(8,128)S(1)} %slice_bitcast_fusion.4, f32[2,128,128]{2,1,0:T(8,128)S(1)} %fusion.92), kind=kOutput, calls=%fused_computation.55 | convolution fusion | flops 201785344 | bytes 917504 | tf_op jit(solution)/shard_map/...ij,...jk->...ik/dot_general | solution.py:46
  7.9 0.0 copy-start.1
  7.9 0.3 copy_dynamic-update-slice_fusion.1
  8.2 0.6 fusion.56
  8.8 0.3 copy_dynamic-update-slice_fusion
  9.1 0.9 %fusion.125 = (bf16[1,2,2,2,128,128]{5,0,3,1,4,2:T(2,128)(2,1)S(1)}, bf16[1,2,2,2,128,128]{5,0,3,1,4,2:T(2,128)(2,1)S(1)}, bf16[1,2,2,2,128,128]{5,0,3,1,4,2:T(2,128)(2,1)S(1)}) fusion(f32[1,2,2,2,128,128]{5,0,3,1,4,2:T(1,128)S(1)} %copy_dynamic-update-slice_fusion), kind=kLoop, calls=%fused_computation.186 | loop fusion | flops 917504 | bytes 1310720 | tf_op jit(solution)/shard_map/convert_element_type | solution.py:76
  10.0 0.0 copy-done.1
  10.0 0.1 copy.80
  10.1 3.4 %fusion.4 = f32[3,2,2,32,2,128]{3,0,4,1,5,2:T(4,128)S(1)} fusion(s32[2,128,32]{2,1,0:T(8,128)S(1)} %copy.80, bf16[1,2,2,2,128,128]{5,0,3,1,4,2:T(2,128)(2,1)S(1)} %get-tuple-element.11, bf16[1,2,2,2,128,128]{5,0,3,1,4,2:T(2,128)(2,1)S(1)} %get-tuple-element.12, bf16[1,2,2,2,128,128]{5,0,3,1,4,2:T(2,128)(2,1)S(1)} %get-tuple-element.10), kind=kOutput, calls=%fused_computation.4 | convolution fusion | flops 28573696 | bytes 1212416 | tf_op jit(solution)/shard_map/qesxoc,sojc->qesjxo/dot_general | solution.py:81
  13.5 0.0 copy-start.6
  13.5 0.0 copy-start.3
  13.5 0.0 copy-start.4
  13.5 0.0 copy-start.5
  13.5 0.8 %slice_add_fusion = f32[1,2,2,32,2,128]{3,0,4,1,5,2:T(1,128)S(1)} fusion(f32[3,2,2,32,2,128]{3,0,4,1,5,2:T(4,128)S(1)} %fusion.4), kind=kLoop, calls=%fused_computation.21 | loop fusion | flops 65536 | bytes 524288 | tf_op jit(solution)/shard_map/add | solution.py:84
  14.3 0.4 copy.100
  14.8 0.2 add.36
  15.0 0.0 copy-done.6
  15.0 0.0 copy-done.3
  15.0 0.0 copy-done.4
  15.0 0.0 copy-done.5
  15.0 0.1 select_reduce_fusion.1
  15.1 0.1 div.10
  15.2 0.1 dynamic_slice.3
  15.3 0.3 copy.101
  15.6 0.5 reshape.256
  16.1 30.7 %all_to_all.10 = f32[256,1,192]{2,1,0:T(1,128)S(1)} all-to-all(f32[256,1,192]{2,1,0:T(1,128)S(1)} %reshape.256), channel_id=1, replica_groups=mesh['mom'=64,'en'=4] {'mom','en'}, dimensions={0} | all-to-all | bytes 393216 | tf_op jit(solution)/shard_map/all_to_all | solution.py:127
  46.8 0.5 broadcast.103
  47.4 1.3 %reduce = f32[256,192]{1,0:T(8,128)S(1)} reduce(f32[256,1,192]{2,1,0:T(1,128)S(1)} %all_to_all.10, f32[]{:T(128)} %broadcast.103), dimensions={1}, to_apply=%all_to_all.6.reduce_sub_computation | reduce | bytes 393220 | tf_op jit(solution)/shard_map/all_to_all | solution.py:127
  48.6 0.2 reshape.257
  49.0 0.3 fusion.64
  49.3 0.4 convolution_add_fusion.2
  49.7 0.3 convolution_add_fusion.1
  50.0 0.3 convolution_add_fusion
  50.4 0.2 copy.105
  50.5 0.3 reshape.258
  50.8 18.0 %all_to_all.11 = f32[256,1,128]{2,1,0:T(1,128)S(1)} all-to-all(f32[256,1,128]{2,1,0:T(1,128)S(1)} %reshape.258), channel_id=1, replica_groups=mesh['mom'=64,'en'=4] {'mom','en'}, dimensions={0} | all-to-all | bytes 262144 | tf_op jit(solution)/shard_map/all_to_all | solution.py:134
  68.8 0.9 %reduce.1 = f32[256,128]{1,0:T(8,128)S(1)} reduce(f32[256,1,128]{2,1,0:T(1,128)S(1)} %all_to_all.11, f32[]{:T(128)} %broadcast.103), dimensions={1}, to_apply=%all_to_all.7.reduce_sub_computation | reduce | bytes 262148 | tf_op jit(solution)/shard_map/all_to_all | solution.py:134
  69.8 0.2 reshape.259
  70.0 0.8 %broadcast_in_dim_reshape.3 = f32[1,2,64,2,128]{4,3,2,1,0:T(2,128)} reshape(f32[2,256,64]{2,1,0:T(8,128)S(1)} %copy.106) | data formatting | bytes 262144 | tf_op jit(solution)/shard_map/broadcast_in_dim;reshape | solution.py:136
  (39 shorter events, 0.8 us)
Async XLA Ops:
  0.0 1.3 %copy-start.2 = (f32[1,2,2,128]{3,2,1,0:T(2,128)S(1)}, f32[1,2,2,128]{3,2,1,0:T(2,128)}, u32[]{:S(2)}) copy-start(f32[1,2,2,128]{3,2,1,0:T(2,128)} %param.10) | copy-start | bytes 6148
  0.0 1.5 %copy-start = (f32[1,2,2,128,128]{4,3,2,1,0:T(8,128)S(1)}, f32[1,2,2,128,128]{4,3,2,1,0:T(8,128)}, u32[]{:S(2)}) copy-start(f32[1,2,2,128,128]{4,3,2,1,0:T(8,128)} %param.9) | copy-start | bytes 786436
  7.9 2.1 %copy-start.1 = (s32[2,128,32]{1,2,0:T(8,128)S(1)}, s32[2,128,32]{1,2,0:T(8,128)}, u32[]{:S(2)}) copy-start(s32[2,128,32]{1,2,0:T(8,128)} %param.11) | copy-start | bytes 98308
  13.5 1.5 %copy-start.6 = (s32[6]{0:T(128)S(1)}, s32[6]{0:T(128)}, u32[]{:S(2)}) copy-start(s32[6]{0:T(128)} %param.12) | copy-start | bytes 76
  13.5 1.5 %copy-start.3 = (f32[6]{0:T(128)S(1)}, f32[6]{0:T(128)}, u32[]{:S(2)}) copy-start(f32[6]{0:T(128)} %param.14) | copy-start | bytes 76
  13.5 1.5 %copy-start.4 = (s32[1,64]{1,0:T(1,128)S(1)}, s32[1,64]{1,0:T(1,128)}, u32[]{:S(2)}) copy-start(s32[1,64]{1,0:T(1,128)} %param.13) | copy-start | bytes 772
  13.5 1.5 %copy-start.5 = (f32[6]{0:T(128)S(1)}, f32[6]{0:T(128)}, u32[]{:S(2)}) copy-start(f32[6]{0:T(128)} %param.15) | copy-start | bytes 76

commit v4 on v3

--- a/solution.py
+++ b/solution.py
@@ -73,9 +73,9 @@
     pieces = []
     rest = stacked
     for _ in range(3):
-        piece = rest.astype(jnp.bfloat16)
-        pieces.append(piece)
-        rest = rest - piece.astype(jnp.float32)
+        piece = lax.reduce_precision(rest, exponent_bits=8, mantissa_bits=7)
+        pieces.append(piece.astype(jnp.bfloat16))
+        rest = rest - piece
     columns = jnp.arange(orbitals, dtype=jnp.int32)
     selector = (neighbors[..., None] == columns).astype(jnp.bfloat16)
     picked = jnp.einsum(

time: 71 us -> 70 us (0.986)
    unnamed x26 -> x25, local copies, waits for them, and re-layouts: 2.89 us -> 2.62 us
where the time goes in v4:
time: 70 us; the launch traced here: 69.9 us
  blocking collectives  48.8 us (70%)
  matrix products  10.9 us (16%)
  local copies, waits for them, and re-layouts  5.74 us (8%)
  other arithmetic  3.82 us (5%)
    all_to_all x1, blocking collectives, shards(): lax.all_to_all(jnp.concatenate([blocks, rows], axis=1), ('mom', 'en'), 0, 0)  30.7 us
    all_to_all x1, blocking collectives, shards(): back = lax.all_to_all(mixed, ('mom', 'en'), 0, 0)  18 us
    dot_general x7, matrix products, cmul(): jnp.einsum(spec, block(left), column(right, adjoint), precision=HIGH)  5.97 us
    dot_general x1, matrix products, slab_pairs(): jnp.einsum('qesxoc,sojc->qesjxo', jnp.stack(pieces), selector, preferred_...  3.57 us
    unnamed x25, local copies, waits for them, and re-layouts  2.62 us

profile of v4, /device:TPU:1, one launch (start us, length us, event | category | flops | bytes accessed | tf_op | source)
XLA Modules:
  0.0 69.9 jit_solution(17273766344793265865)
XLA Ops:
  0.0 0.0 copy-start.2
  0.0 0.0 copy-start
  0.0 1.3 %copy.108 = f32[1,2,2,2,128,128]{4,5,1,3,2,0:T(8,128)S(1)} copy(f32[1,2,2,2,128,128]{5,4,3,2,1,0:T(8,128)} %param.8) | data formatting | bytes 1048576 | tf_op args[0]
  1.3 0.0 copy-done.2
  1.4 0.1 broadcast_multiply_fusion
  1.5 0.0 copy-done
  1.6 1.0 %fusion.18 = f32[2,256,128]{2,1,0:T(8,128)S(1)} fusion(f32[2,128,128]{1,2,0:T(8,128)S(1)} %get-tuple-element.40, f32[2,128,128]{1,2,0:T(8,128)S(1)} %get-tuple-element.39, f32[2,128,128]{1,2,0:T(8,128)S(1)} %fusion.112, f32[2,128,128]{2,1,0:T(8,128)S(1)} %get-tuple-element.51, f32[2,128,128]{2,1,0:T(8,128)S(1)} %get-tuple-element.52), kind=kOutput, calls=%fused_computation.26 | convolution fusion | flops 201785344 | bytes 917504 | tf_op jit(solution)/shard_map/...ij,...jk->...ik/dot_general | solution.py:46
  2.7 0.1 copy.110
  2.8 0.6 fusion.34
  3.7 1.0 %fusion.7 = f32[2,2,256,128]{3,2,1,0:T(8,128)S(1)} fusion(f32[2,2,128,128]{3,2,1,0:T(8,128)S(1)} %fusion.64, f32[2,2,128,128]{3,2,1,0:T(8,128)S(1)} %get-tuple-element.9, f32[2,2,128,128]{3,2,1,0:T(8,128)S(1)} %get-tuple-element.8, f32[128,128]{0,1:T(8,128)S(1)} %get-tuple-element.35, f32[128,128]{0,1:T(8,128)S(1)} %get-tuple-element.32), kind=kOutput, calls=%fused_computation.8 | convolution fusion | flops 403472384 | bytes 1441792 | tf_op jit(solution)/shard_map/ewij,jk->ewik/dot_general | solution.py:46
  4.8 1.0 %fusion.26 = f32[2,256,128]{2,1,0:T(8,128)S(1)} fusion(f32[2,128,128]{1,2,0:T(8,128)S(1)} %get-tuple-element.42, f32[2,128,128]{1,2,0:T(8,128)S(1)} %get-tuple-element.41, f32[2,128,128]{1,2,0:T(8,128)S(1)} %fusion.113, f32[2,128,128]{2,1,0:T(8,128)S(1)} %get-tuple-element.31, f32[2,128,128]{2,1,0:T(8,128)S(1)} %get-tuple-element.30), kind=kOutput, calls=%fused_computation.34 | convolution fusion | flops 201785344 | bytes 917504 | tf_op jit(solution)/shard_map/...ij,...jk->...ik/dot_general | solution.py:46
  5.9 0.6 fusion.38
  6.5 0.1 copy.120
  6.7 0.0 copy-start.1
  6.8 1.0 %fusion.46 = f32[2,256,128]{2,1,0:T(8,128)S(1)} fusion(f32[2,128,128]{1,2,0:T(8,128)S(1)} %get-tuple-element.23, f32[2,128,128]{1,2,0:T(8,128)S(1)} %get-tuple-element.22, f32[2,128,128]{1,2,0:T(8,128)S(1)} %get-tuple-element.25, f32[2,128,128]{2,1,0:T(8,128)S(1)} %slice_bitcast_fusion.4, f32[2,128,128]{2,1,0:T(8,128)S(1)} %fusion.90), kind=kOutput, calls=%fused_computation.58 | convolution fusion | flops 201785344 | bytes 917504 | tf_op jit(solution)/shard_map/...ij,...jk->...ik/dot_general | solution.py:46
  7.9 0.0 copy-done.1
  7.9 0.1 copy.107
  8.0 0.6 fusion.54
  8.6 0.2 reduce-precision_convert_fusion.1
  8.8 0.1 pad_maximum_fusion
  8.9 3.6 %fusion.4 = f32[3,2,2,32,2,128]{3,0,4,1,5,2:T(4,128)S(1)} fusion(s32[2,128,32]{2,1,0:T(8,128)S(1)} %copy.107, bf16[3,2,2,2,128,128]{5,4,3,2,1,0:T(8,128)(2,1)S(1)} %pad_maximum_fusion), kind=kOutput, calls=%fused_computation.4 | convolution fusion | flops 26214400 | bytes 1212416 | tf_op jit(solution)/shard_map/qesxoc,sojc->qesjxo/dot_general | solution.py:81
  12.5 0.0 copy-start.6
  12.5 0.0 copy-start.3
  12.5 0.0 copy-start.4
  12.6 0.0 copy-start.5
  12.6 0.8 %slice_add_fusion = f32[1,2,2,32,2,128]{3,0,4,1,5,2:T(1,128)S(1)} fusion(f32[3,2,2,32,2,128]{3,0,4,1,5,2:T(4,128)S(1)} %fusion.4), kind=kLoop, calls=%fused_computation.24 | loop fusion | flops 65536 | bytes 524288 | tf_op jit(solution)/shard_map/add | solution.py:84
  13.4 0.4 copy.126
  13.8 0.2 add.36
  14.0 0.0 copy-done.6
  14.0 0.0 copy-done.3
  14.0 0.0 copy-done.4
  14.0 0.0 copy-done.5
  14.1 0.1 select_reduce_fusion.1
  14.2 0.1 div.10
  14.3 0.1 dynamic_slice.3
  14.4 0.3 copy.127
  14.7 0.5 reshape.259
  15.1 30.7 %all_to_all.10 = f32[256,1,192]{2,1,0:T(1,128)S(1)} all-to-all(f32[256,1,192]{2,1,0:T(1,128)S(1)} %reshape.259), channel_id=1, replica_groups=mesh['mom'=64,'en'=4] {'mom','en'}, dimensions={0} | all-to-all | bytes 393216 | tf_op jit(solution)/shard_map/all_to_all | solution.py:127
  45.9 0.5 broadcast.103
  46.4 1.3 %reduce = f32[256,192]{1,0:T(8,128)S(1)} reduce(f32[256,1,192]{2,1,0:T(1,128)S(1)} %all_to_all.10, f32[]{:T(128)} %broadcast.103), dimensions={1}, to_apply=%all_to_all.6.reduce_sub_computation | reduce | bytes 393220 | tf_op jit(solution)/shard_map/all_to_all | solution.py:127
  47.7 0.2 reshape.260
  48.0 0.3 fusion.62
  48.3 0.4 convolution_add_fusion.2
  48.7 0.3 convolution_add_fusion.1
  49.1 0.3 convolution_add_fusion
  49.4 0.2 copy.131
  49.6 0.3 reshape.261
  49.8 18.0 %all_to_all.11 = f32[256,1,128]{2,1,0:T(1,128)S(1)} all-to-all(f32[256,1,128]{2,1,0:T(1,128)S(1)} %reshape.261), channel_id=1, replica_groups=mesh['mom'=64,'en'=4] {'mom','en'}, dimensions={0} | all-to-all | bytes 262144 | tf_op jit(solution)/shard_map/all_to_all | solution.py:134
  67.9 0.9 %reduce.1 = f32[256,128]{1,0:T(8,128)S(1)} reduce(f32[256,1,128]{2,1,0:T(1,128)S(1)} %all_to_all.11, f32[]{:T(128)} %broadcast.103), dimensions={1}, to_apply=%all_to_all.7.reduce_sub_computation | reduce | bytes 262148 | tf_op jit(solution)/shard_map/all_to_all | solution.py:134
  68.8 0.2 reshape.262
  69.1 0.8 %broadcast_in_dim_reshape.3 = f32[1,2,64,2,128]{4,3,2,1,0:T(2,128)} reshape(f32[2,256,64]{2,1,0:T(8,128)S(1)} %copy.132) | data formatting | bytes 262144 | tf_op jit(solution)/shard_map/broadcast_in_dim;reshape | solution.py:136
  (39 shorter events, 0.8 us)
Async XLA Ops:
  0.0 1.3 %copy-start.2 = (f32[1,2,2,128]{3,2,1,0:T(2,128)S(1)}, f32[1,2,2,128]{3,2,1,0:T(2,128)}, u32[]{:S(2)}) copy-start(f32[1,2,2,128]{3,2,1,0:T(2,128)} %param.10) | copy-start | bytes 6148
  0.0 1.5 %copy-start = (f32[1,2,2,128,128]{4,3,2,1,0:T(8,128)S(1)}, f32[1,2,2,128,128]{4,3,2,1,0:T(8,128)}, u32[]{:S(2)}) copy-start(f32[1,2,2,128,128]{4,3,2,1,0:T(8,128)} %param.9) | copy-start | bytes 786436
  6.7 1.3 %copy-start.1 = (s32[2,128,32]{1,2,0:T(8,128)S(1)}, s32[2,128,32]{1,2,0:T(8,128)}, u32[]{:S(2)}) copy-start(s32[2,128,32]{1,2,0:T(8,128)} %param.11) | copy-start | bytes 98308
  12.5 1.5 %copy-start.6 = (s32[6]{0:T(128)S(1)}, s32[6]{0:T(128)}, u32[]{:S(2)}) copy-start(s32[6]{0:T(128)} %param.12) | copy-start | bytes 76
  12.5 1.5 %copy-start.3 = (f32[6]{0:T(128)S(1)}, f32[6]{0:T(128)}, u32[]{:S(2)}) copy-start(f32[6]{0:T(128)} %param.14) | copy-start | bytes 76
  12.5 1.5 %copy-start.4 = (s32[1,64]{1,0:T(1,128)S(1)}, s32[1,64]{1,0:T(1,128)}, u32[]{:S(2)}) copy-start(s32[1,64]{1,0:T(1,128)} %param.13) | copy-start | bytes 772
  12.6 1.5 %copy-start.5 = (f32[6]{0:T(128)S(1)}, f32[6]{0:T(128)}, u32[]{:S(2)}) copy-start(f32[6]{0:T(128)} %param.15) | copy-start | bytes 76

commit v5 on v4

--- a/solution.py
+++ b/solution.py
@@ -85,19 +85,19 @@
     return picked.reshape(picked.shape[0], -1, picked.shape[3], picked.shape[4])
 
 
-def shift_weights(table_row, mode_shift, emit_weight, absorb_weight):
+def shift_weights(table, mode_shift, emit_weight, absorb_weight):
     mode_ids = jnp.arange(mode_shift.shape[0], dtype=jnp.int32)
-    chosen = (table_row[:, None] == mode_ids[None, :]).astype(jnp.float32)
-    shift = jnp.sum(chosen * mode_shift.astype(jnp.float32)[None], axis=1)
-    emit = jnp.sum(chosen * emit_weight[None], axis=1)
-    absorb = jnp.sum(chosen * absorb_weight[None], axis=1)
+    chosen = (table[..., None] == mode_ids).astype(jnp.float32)
+    shift = jnp.sum(chosen * mode_shift.astype(jnp.float32), axis=-1)
+    emit = jnp.sum(chosen * emit_weight, axis=-1)
+    absorb = jnp.sum(chosen * absorb_weight, axis=-1)
     rows = []
     for offset in OFFSETS:
         if offset < 0:
             rows.append(emit * (shift == -offset).astype(jnp.float32))
         else:
             rows.append(absorb * (shift == offset).astype(jnp.float32))
-    return jnp.stack(rows) / table_row.shape[0]
+    return jnp.stack(rows, axis=-2) / table.shape[-1]
 
 
 def mix(data, weights, energies):
@@ -118,18 +118,18 @@
     devices = moms * groups
     flat = pairs.reshape(local, -1)
     width = flat.shape[1] // devices
-    blocks = jnp.swapaxes(flat.reshape(local, devices, width), 0, 1)
-    weights = shift_weights(mode_table[0], mode_shift, emit_weight, absorb_weight).reshape(-1)
-    share = -(-weights.shape[0] // (groups * width)) * width
-    weights = jnp.pad(weights, (0, share * groups - weights.shape[0]))
-    mine = lax.dynamic_slice_in_dim(weights, lax.axis_index("en") * share, share)
-    rows = jnp.broadcast_to(mine.reshape(1, -1, width), (devices, share // width, width))
+    blocks = jnp.swapaxes(flat.reshape(local, devices, width), 0, 1).reshape(devices, -1)
+    share = -(-moms // groups)
+    ids = jnp.pad(mode_table[0].astype(jnp.float32), (0, share * groups - moms))
+    mine = lax.dynamic_slice_in_dim(ids, lax.axis_index("en") * share, share)
+    rows = jnp.broadcast_to(mine[None], (devices, share))
     sent = lax.all_to_all(jnp.concatenate([blocks, rows], axis=1), ("mom", "en"), 0, 0)
-    sent = sent.reshape(moms, groups, local + share // width, width)
-    data = sent[:, :, :local].reshape(moms, groups * local, width)
+    sent = sent.reshape(moms, groups, -1)
+    data = sent[:, :, : local * width].reshape(moms, groups * local, width)
     data = jnp.pad(data, ((0, 0), (SHIFT_MAX, SHIFT_MAX), (0, 0)))
-    table = sent[:, :, local:].reshape(moms, -1)[:, : len(OFFSETS) * moms]
-    mixed = mix(data, table.reshape(moms, len(OFFSETS), moms), groups * local)
+    table = sent[:, :, local * width :].reshape(moms, -1)[:, :moms].astype(jnp.int32)
+    weights = shift_weights(table, mode_shift, emit_weight, absorb_weight)
+    mixed = mix(data, weights, groups * local)
     mixed = mixed.reshape(devices, local, width)
     back = lax.all_to_all(mixed, ("mom", "en"), 0, 0)
     result = jnp.swapaxes(back, 0, 1).reshape(pairs.shape)

time: 70 us -> 70 us (level)
  blocking collectives: 48.8 us -> 18 us
  starting transfers between devices: 0 us -> 15.6 us
  waiting for transfers between devices: 0 us -> 15.2 us
    all_to_all x1 -> x0, blocking collectives: 30.7 us -> none  [shards(): lax.all_to_all(jnp.concatenate([blocks, rows], axis=1), ('mom', 'en'), 0, 0)]
    all_to_all x0 -> x1, starting transfers between devices: none -> 15.6 us  [shards(): lax.all_to_all(jnp.concatenate([blocks, rows], axis=1), ('mom', 'en'), 0, 0)]
    all_to_all x0 -> x1, waiting for transfers between devices: none -> 15.2 us  [shards(): lax.all_to_all(jnp.concatenate([blocks, rows], axis=1), ('mom', 'en'), 0, 0)]
    unnamed x25 -> x23, local copies, waits for them, and re-layouts: 2.62 us -> 2.02 us
  transfers between devices with their start and end apart: 0 -> 1, of which waited for: 0 -> 1; matrix products, arithmetic and copies ran while one was open for 0% -> 0% of each run, Pallas kernels for 0% -> 0%
where the time goes in v5:
time: 70 us; the launch traced here: 69.8 us
  blocking collectives  18 us (26%)
  starting transfers between devices  15.6 us (22%)
  waiting for transfers between devices  15.2 us (22%)
  matrix products  10.9 us (16%)
  local copies, waits for them, and re-layouts  6.07 us (9%)
  other arithmetic  3.3 us (5%)
    all_to_all x1, blocking collectives, shards(): back = lax.all_to_all(mixed, ('mom', 'en'), 0, 0)  18 us
    all_to_all x1, starting transfers between devices, shards(): lax.all_to_all(jnp.concatenate([blocks, rows], axis=1), ('mom', 'en'), 0, 0)  15.6 us
    all_to_all x1, waiting for transfers between devices, shards(): lax.all_to_all(jnp.concatenate([blocks, rows], axis=1), ('mom', 'en'), 0, 0)  15.2 us
    dot_general x7, matrix products, cmul(): jnp.einsum(spec, block(left), column(right, adjoint), precision=HIGH)  5.97 us
    dot_general x1, matrix products, slab_pairs(): jnp.einsum('qesxoc,sojc->qesjxo', jnp.stack(pieces), selector, preferred_...  3.57 us
    unnamed x23, local copies, waits for them, and re-layouts  2.02 us
  transfers between devices with their start and end apart: 1, of which 1 were waited for; matrix products, arithmetic and copies ran while one was open for 0% of the time, Pallas kernels for 0%

profile of v5, /device:TPU:1, one launch (start us, length us, event | category | flops | bytes accessed | tf_op | source)
XLA Modules:
  0.0 69.8 jit_solution(845435935162380263)
XLA Ops:
  0.0 0.0 copy-start.2
  0.0 0.0 copy-start
  0.0 1.3 %copy.112 = f32[1,2,2,2,128,128]{4,5,1,3,2,0:T(8,128)S(1)} copy(f32[1,2,2,2,128,128]{5,4,3,2,1,0:T(8,128)} %param.8) | data formatting | bytes 1048576 | tf_op args[0]
  1.3 0.0 copy-done.2
  1.4 0.1 broadcast_multiply_fusion
  1.5 0.0 copy-done
  1.6 1.0 %fusion.18 = f32[2,256,128]{2,1,0:T(8,128)S(1)} fusion(f32[2,128,128]{1,2,0:T(8,128)S(1)} %get-tuple-element.44, f32[2,128,128]{1,2,0:T(8,128)S(1)} %get-tuple-element.43, f32[2,128,128]{1,2,0:T(8,128)S(1)} %fusion.108, f32[2,128,128]{2,1,0:T(8,128)S(1)} %get-tuple-element.53, f32[2,128,128]{2,1,0:T(8,128)S(1)} %get-tuple-element.54), kind=kOutput, calls=%fused_computation.26 | convolution fusion | flops 201785344 | bytes 917504 | tf_op jit(solution)/shard_map/...ij,...jk->...ik/dot_general | solution.py:46
  2.7 0.1 copy.114
  2.8 0.6 fusion.34
  3.7 1.0 %fusion.7 = f32[2,2,256,128]{3,2,1,0:T(8,128)S(1)} fusion(f32[2,2,128,128]{3,2,1,0:T(8,128)S(1)} %fusion.64, f32[2,2,128,128]{3,2,1,0:T(8,128)S(1)} %get-tuple-element.13, f32[2,2,128,128]{3,2,1,0:T(8,128)S(1)} %get-tuple-element.12, f32[128,128]{0,1:T(8,128)S(1)} %get-tuple-element.39, f32[128,128]{0,1:T(8,128)S(1)} %get-tuple-element.36), kind=kOutput, calls=%fused_computation.8 | convolution fusion | flops 403472384 | bytes 1441792 | tf_op jit(solution)/shard_map/ewij,jk->ewik/dot_general | solution.py:46
  4.8 1.0 %fusion.26 = f32[2,256,128]{2,1,0:T(8,128)S(1)} fusion(f32[2,128,128]{1,2,0:T(8,128)S(1)} %get-tuple-element.46, f32[2,128,128]{1,2,0:T(8,128)S(1)} %get-tuple-element.45, f32[2,128,128]{1,2,0:T(8,128)S(1)} %fusion.109, f32[2,128,128]{2,1,0:T(8,128)S(1)} %get-tuple-element.35, f32[2,128,128]{2,1,0:T(8,128)S(1)} %get-tuple-element.34), kind=kOutput, calls=%fused_computation.34 | convolution fusion | flops 201785344 | bytes 917504 | tf_op jit(solution)/shard_map/...ij,...jk->...ik/dot_general | solution.py:46
  5.9 0.6 fusion.38
  6.5 0.1 copy.124
  6.7 0.0 copy-start.1
  6.8 1.0 %fusion.46 = f32[2,256,128]{2,1,0:T(8,128)S(1)} fusion(f32[2,128,128]{1,2,0:T(8,128)S(1)} %get-tuple-element.27, f32[2,128,128]{1,2,0:T(8,128)S(1)} %get-tuple-element.26, f32[2,128,128]{1,2,0:T(8,128)S(1)} %get-tuple-element.29, f32[2,128,128]{2,1,0:T(8,128)S(1)} %slice_bitcast_fusion.4, f32[2,128,128]{2,1,0:T(8,128)S(1)} %fusion.90), kind=kOutput, calls=%fused_computation.58 | convolution fusion | flops 201785344 | bytes 917504 | tf_op jit(solution)/shard_map/...ij,...jk->...ik/dot_general | solution.py:46
  7.9 0.0 copy-done.1
  7.9 0.1 copy.111
  8.0 0.6 fusion.54
  8.6 0.2 reduce-precision_convert_fusion.1
  8.8 0.1 pad_maximum_fusion
  8.9 3.6 %fusion.4 = f32[3,2,2,32,2,128]{3,0,4,1,5,2:T(4,128)S(1)} fusion(s32[2,128,32]{2,1,0:T(8,128)S(1)} %copy.111, bf16[3,2,2,2,128,128]{5,4,3,2,1,0:T(8,128)(2,1)S(1)} %pad_maximum_fusion), kind=kOutput, calls=%fused_computation.4 | convolution fusion | flops 26214400 | bytes 1212416 | tf_op jit(solution)/shard_map/qesxoc,sojc->qesjxo/dot_general | solution.py:81
  12.5 0.0 copy-start.5
  12.5 0.0 copy-start.6
  12.5 0.8 %slice_add_fusion = f32[1,2,2,32,2,128]{3,0,4,1,5,2:T(1,128)S(1)} fusion(f32[3,2,2,32,2,128]{3,0,4,1,5,2:T(4,128)S(1)} %fusion.4), kind=kLoop, calls=%fused_computation.24 | loop fusion | flops 65536 | bytes 524288 | tf_op jit(solution)/shard_map/add | solution.py:84
  13.4 0.4 copy.130
  13.8 0.2 add.36
  14.0 0.1 copy.131
  14.1 0.0 copy-start.3
  14.1 0.0 copy-start.4
  14.1 0.0 copy-done.5
  14.2 0.1 dynamic-slice_bitcast_fusion
  14.2 0.1 maximum_bitcast_fusion.2
  14.3 0.8 %copy.132 = f32[256,1,144]{2,1,0:T(1,128)} copy(f32[256,1,144]{0,2,1:T(8,128)S(1)} %maximum_bitcast_fusion.2) | data formatting | bytes 294912 | tf_op jit(solution)/shard_map/all_to_all | solution.py:126
  15.2 15.6 %all-to-all-start = ((f32[256,1,144]{2,1,0:T(1,128)}), f32[256,1,144]{2,1,0:T(1,128)S(1)}, u32[]{:S(2)}, u32[]{:S(2)}) async-start(f32[256,1,144]{2,1,0:T(1,128)} %copy.132), calls=%async_computation | async-start | bytes 524288 | tf_op jit(solution)/shard_map/all_to_all | solution.py:126
  30.8 0.0 copy-done.6
  30.8 15.2 %all-to-all-done = f32[256,1,144]{2,1,0:T(1,128)S(1)} async-done(((f32[256,1,144]{2,1,0:T(1,128)}), f32[256,1,144]{2,1,0:T(1,128)S(1)}, u32[]{:S(2)}, u32[]{:S(2)}) %all-to-all-start) | async-done | bytes 147488 | tf_op jit(solution)/shard_map/all_to_all | solution.py:126
  46.1 0.6 reduce
  46.7 0.1 reshape.257
  46.8 0.1 copy.155
  46.9 0.1 copy.134
  47.0 0.1 reshape.258
  47.2 0.1 copy.135
  47.2 0.0 copy-done.3
  47.2 0.0 copy-done.4
  47.3 0.1 select_reduce_fusion.1
  47.5 0.3 fusion.62
  47.8 0.4 convolution_add_fusion.2
  48.2 0.3 convolution_add_fusion.1
  48.5 0.3 convolution_add_fusion
  48.9 0.2 copy.136
  49.0 0.3 reshape.269
  49.3 18.0 %all_to_all.14 = f32[256,1,128]{2,1,0:T(1,128)S(1)} all-to-all(f32[256,1,128]{2,1,0:T(1,128)S(1)} %reshape.269), channel_id=1, replica_groups=mesh['mom'=64,'en'=4] {'mom','en'}, dimensions={0} | all-to-all | bytes 262144 | tf_op jit(solution)/shard_map/all_to_all | solution.py:134
  67.3 0.5 broadcast.102
  67.8 0.9 %reduce.1 = f32[256,128]{1,0:T(8,128)S(1)} reduce(f32[256,1,128]{2,1,0:T(1,128)S(1)} %all_to_all.14, f32[]{:T(128)} %broadcast.102), dimensions={1}, to_apply=%all_to_all.11.reduce_sub_computation | reduce | bytes 262148 | tf_op jit(solution)/shard_map/all_to_all | solution.py:134
  68.8 0.2 reshape.270
  69.0 0.8 %broadcast_in_dim_reshape.3 = f32[1,2,64,2,128]{4,3,2,1,0:T(2,128)} reshape(f32[2,256,64]{2,1,0:T(8,128)S(1)} %copy.137) | data formatting | bytes 262144 | tf_op jit(solution)/shard_map/broadcast_in_dim;reshape | solution.py:136
  (38 shorter events, 0.7 us)
Async XLA Ops:
  0.0 1.3 %copy-start.2 = (f32[1,2,2,128]{3,2,1,0:T(2,128)S(1)}, f32[1,2,2,128]{3,2,1,0:T(2,128)}, u32[]{:S(2)}) copy-start(f32[1,2,2,128]{3,2,1,0:T(2,128)} %param.10) | copy-start | bytes 6148
  0.0 1.5 %copy-start = (f32[1,2,2,128,128]{4,3,2,1,0:T(8,128)S(1)}, f32[1,2,2,128,128]{4,3,2,1,0:T(8,128)}, u32[]{:S(2)}) copy-start(f32[1,2,2,128,128]{4,3,2,1,0:T(8,128)} %param.9) | copy-start | bytes 786436
  6.7 1.3 %copy-start.1 = (s32[2,128,32]{1,2,0:T(8,128)S(1)}, s32[2,128,32]{1,2,0:T(8,128)}, u32[]{:S(2)}) copy-start(s32[2,128,32]{1,2,0:T(8,128)} %param.11) | copy-start | bytes 98308
  12.5 1.6 %copy-start.5 = (s32[1,64]{1,0:T(1,128)S(1)}, s32[1,64]{1,0:T(1,128)}, u32[]{:S(2)}) copy-start(s32[1,64]{1,0:T(1,128)} %param.13) | copy-start | bytes 772
  12.5 18.3 %copy-start.6 = (s32[6]{0:T(128)S(1)}, s32[6]{0:T(128)}, u32[]{:S(2)}) copy-start(s32[6]{0:T(128)} %param.12) | copy-start | bytes 76
  14.1 33.1 %copy-start.3 = (f32[6]{0:T(128)S(1)}, f32[6]{0:T(128)}, u32[]{:S(2)}) copy-start(f32[6]{0:T(128)} %param.14) | copy-start | bytes 76
  14.1 33.1 %copy-start.4 = (f32[6]{0:T(128)S(1)}, f32[6]{0:T(128)}, u32[]{:S(2)}) copy-start(f32[6]{0:T(128)} %param.15) | copy-start | bytes 76
  15.2 30.9 %all-to-all-start = ((f32[256,1,144]{2,1,0:T(1,128)}), f32[256,1,144]{2,1,0:T(1,128)S(1)}, u32[]{:S(2)}, u32[]{:S(2)}) async-start(f32[256,1,144]{2,1,0:T(1,128)} %copy.132), calls=%async_computation | async-start | bytes 524288 | tf_op jit(solution)/shard_map/all_to_all | solution.py:126

commit v6 on v5

--- a/solution.py
+++ b/solution.py
@@ -8,6 +8,7 @@
 
 
 HIGH = lax.Precision.HIGHEST
+CHAIN = lax.Precision.HIGH
 
 
 def with_halo(x, sides, width):
@@ -43,7 +44,7 @@
 
 
 def cmul(left, right, spec="...ij,...jk->...ik", adjoint=False):
-    product = jnp.einsum(spec, block(left), column(right, adjoint), precision=HIGH)
+    product = jnp.einsum(spec, block(left), column(right, adjoint), precision=CHAIN)
     return split(product)
 
 

time: 70 us -> 67.7 us (0.967)
  matrix products: 10.9 us -> 8.66 us
    dot_general x7, matrix products: 5.97 us -> 3.7 us  [cmul(): jnp.einsum(spec, block(left), column(right, adjoint), precision=CHAIN)]
where the time goes in v6:
time: 67.7 us; the launch traced here: 67.5 us
  blocking collectives  18 us (27%)
  starting transfers between devices  15.6 us (23%)
  waiting for transfers between devices  15.2 us (22%)
  matrix products  8.66 us (13%)
  local copies, waits for them, and re-layouts  6.07 us (9%)
  other arithmetic  3.3 us (5%)
    all_to_all x1, blocking collectives, shards(): back = lax.all_to_all(mixed, ('mom', 'en'), 0, 0)  18 us
    all_to_all x1, starting transfers between devices, shards(): lax.all_to_all(jnp.concatenate([blocks, rows], axis=1), ('mom', 'en'), 0, 0)  15.6 us
    all_to_all x1, waiting for transfers between devices, shards(): lax.all_to_all(jnp.concatenate([blocks, rows], axis=1), ('mom', 'en'), 0, 0)  15.2 us
    dot_general x7, matrix products, cmul(): jnp.einsum(spec, block(left), column(right, adjoint), precision=CHAIN)  3.7 us
    dot_general x1, matrix products, slab_pairs(): jnp.einsum('qesxoc,sojc->qesjxo', jnp.stack(pieces), selector, preferred_...  3.57 us
    unnamed x23, local copies, waits for them, and re-layouts  2.02 us
    dot_general x4, matrix products, mix(): term = jnp.einsum('kj,jec->kec', weights[:, index], window, precision=HIGH)  1.38 us
  transfers between devices with their start and end apart: 1, of which 1 were waited for; matrix products, arithmetic and copies ran while one was open for 0% of the time, Pallas kernels for 0%

profile of v6, /device:TPU:1, one launch (start us, length us, event | category | flops | bytes accessed | tf_op | source)
XLA Modules:
  0.0 67.5 jit_solution(1013598446167152058)
XLA Ops:
  0.0 0.0 copy-start.2
  0.0 0.0 copy-start
  0.0 1.3 %copy.112 = f32[1,2,2,2,128,128]{4,5,1,3,2,0:T(8,128)S(1)} copy(f32[1,2,2,2,128,128]{5,4,3,2,1,0:T(8,128)} %param.8) | data formatting | bytes 1048576 | tf_op args[0]
  1.3 0.0 copy-done.2
  1.4 0.1 broadcast_multiply_fusion
  1.5 0.0 copy-done
  1.6 0.6 fusion.18
  2.3 0.1 copy.114
  2.4 0.4 fusion.34
  3.1 0.6 fusion.7
  3.7 0.6 fusion.26
  4.5 0.4 fusion.38
  4.8 0.1 copy.124
  5.0 0.0 copy-start.1
  5.2 0.6 fusion.46
  5.9 0.0 copy-done.1
  5.9 0.1 copy.111
  6.0 0.4 fusion.54
  6.4 0.2 reduce-precision_convert_fusion.1
  6.6 0.1 pad_maximum_fusion
  6.7 3.6 %fusion.4 = f32[3,2,2,32,2,128]{3,0,4,1,5,2:T(4,128)S(1)} fusion(s32[2,128,32]{2,1,0:T(8,128)S(1)} %copy.111, bf16[3,2,2,2,128,128]{5,4,3,2,1,0:T(8,128)(2,1)S(1)} %pad_maximum_fusion), kind=kOutput, calls=%fused_computation.4 | convolution fusion | flops 26214400 | bytes 1212416 | tf_op jit(solution)/shard_map/qesxoc,sojc->qesjxo/dot_general | solution.py:82
  10.3 0.0 copy-start.5
  10.3 0.0 copy-start.6
  10.3 0.8 %slice_add_fusion = f32[1,2,2,32,2,128]{3,0,4,1,5,2:T(1,128)S(1)} fusion(f32[3,2,2,32,2,128]{3,0,4,1,5,2:T(4,128)S(1)} %fusion.4), kind=kLoop, calls=%fused_computation.24 | loop fusion | flops 65536 | bytes 524288 | tf_op jit(solution)/shard_map/add | solution.py:85
  11.1 0.4 copy.130
  11.5 0.2 add.36
  11.7 0.1 copy.131
  11.8 0.0 copy-start.3
  11.9 0.0 copy-start.4
  11.9 0.0 copy-done.5
  11.9 0.1 dynamic-slice_bitcast_fusion
  12.0 0.1 maximum_bitcast_fusion.2
  12.1 0.8 %copy.132 = f32[256,1,144]{2,1,0:T(1,128)} copy(f32[256,1,144]{0,2,1:T(8,128)S(1)} %maximum_bitcast_fusion.2) | data formatting | bytes 294912 | tf_op jit(solution)/shard_map/all_to_all | solution.py:127
  12.9 15.6 %all-to-all-start = ((f32[256,1,144]{2,1,0:T(1,128)}), f32[256,1,144]{2,1,0:T(1,128)S(1)}, u32[]{:S(2)}, u32[]{:S(2)}) async-start(f32[256,1,144]{2,1,0:T(1,128)} %copy.132), calls=%async_computation | async-start | bytes 524288 | tf_op jit(solution)/shard_map/all_to_all | solution.py:127
  28.6 0.0 copy-done.6
  28.6 15.2 %all-to-all-done = f32[256,1,144]{2,1,0:T(1,128)S(1)} async-done(((f32[256,1,144]{2,1,0:T(1,128)}), f32[256,1,144]{2,1,0:T(1,128)S(1)}, u32[]{:S(2)}, u32[]{:S(2)}) %all-to-all-start) | async-done | bytes 147488 | tf_op jit(solution)/shard_map/all_to_all | solution.py:127
  43.8 0.6 reduce
  44.4 0.1 reshape.257
  44.6 0.1 copy.155
  44.7 0.1 copy.134
  44.8 0.1 reshape.258
  44.9 0.1 copy.135
  45.0 0.0 copy-done.3
  45.0 0.0 copy-done.4
  45.0 0.1 select_reduce_fusion.1
  45.2 0.3 fusion.62
  45.5 0.4 convolution_add_fusion.2
  45.9 0.3 convolution_add_fusion.1
  46.2 0.3 convolution_add_fusion
  46.6 0.2 copy.136
  46.8 0.3 reshape.269
  47.0 18.0 %all_to_all.14 = f32[256,1,128]{2,1,0:T(1,128)S(1)} all-to-all(f32[256,1,128]{2,1,0:T(1,128)S(1)} %reshape.269), channel_id=1, replica_groups=mesh['mom'=64,'en'=4] {'mom','en'}, dimensions={0} | all-to-all | bytes 262144 | tf_op jit(solution)/shard_map/all_to_all | solution.py:135
  65.1 0.5 broadcast.102
  65.6 0.9 %reduce.1 = f32[256,128]{1,0:T(8,128)S(1)} reduce(f32[256,1,128]{2,1,0:T(1,128)S(1)} %all_to_all.14, f32[]{:T(128)} %broadcast.102), dimensions={1}, to_apply=%all_to_all.11.reduce_sub_computation | reduce | bytes 262148 | tf_op jit(solution)/shard_map/all_to_all | solution.py:135
  66.5 0.2 reshape.270
  66.8 0.8 %broadcast_in_dim_reshape.3 = f32[1,2,64,2,128]{4,3,2,1,0:T(2,128)} reshape(f32[2,256,64]{2,1,0:T(8,128)S(1)} %copy.137) | data formatting | bytes 262144 | tf_op jit(solution)/shard_map/broadcast_in_dim;reshape | solution.py:137
  (38 shorter events, 0.7 us)
Async XLA Ops:
  0.0 1.3 %copy-start.2 = (f32[1,2,2,128]{3,2,1,0:T(2,128)S(1)}, f32[1,2,2,128]{3,2,1,0:T(2,128)}, u32[]{:S(2)}) copy-start(f32[1,2,2,128]{3,2,1,0:T(2,128)} %param.10) | copy-start | bytes 6148
  0.0 1.5 %copy-start = (f32[1,2,2,128,128]{4,3,2,1,0:T(8,128)S(1)}, f32[1,2,2,128,128]{4,3,2,1,0:T(8,128)}, u32[]{:S(2)}) copy-start(f32[1,2,2,128,128]{4,3,2,1,0:T(8,128)} %param.9) | copy-start | bytes 786436
  5.0 0.9 %copy-start.1 = (s32[2,128,32]{1,2,0:T(8,128)S(1)}, s32[2,128,32]{1,2,0:T(8,128)}, u32[]{:S(2)}) copy-start(s32[2,128,32]{1,2,0:T(8,128)} %param.11) | copy-start | bytes 98308
  10.3 1.6 %copy-start.5 = (s32[1,64]{1,0:T(1,128)S(1)}, s32[1,64]{1,0:T(1,128)}, u32[]{:S(2)}) copy-start(s32[1,64]{1,0:T(1,128)} %param.13) | copy-start | bytes 772
  10.3 18.3 %copy-start.6 = (s32[6]{0:T(128)S(1)}, s32[6]{0:T(128)}, u32[]{:S(2)}) copy-start(s32[6]{0:T(128)} %param.12) | copy-start | bytes 76
  11.8 33.1 %copy-start.3 = (f32[6]{0:T(128)S(1)}, f32[6]{0:T(128)}, u32[]{:S(2)}) copy-start(f32[6]{0:T(128)} %param.14) | copy-start | bytes 76
  11.9 33.1 %copy-start.4 = (f32[6]{0:T(128)S(1)}, f32[6]{0:T(128)}, u32[]{:S(2)}) copy-start(f32[6]{0:T(128)} %param.15) | copy-start | bytes 76
  12.9 30.9 %all-to-all-start = ((f32[256,1,144]{2,1,0:T(1,128)}), f32[256,1,144]{2,1,0:T(1,128)S(1)}, u32[]{:S(2)}, u32[]{:S(2)}) async-start(f32[256,1,144]{2,1,0:T(1,128)} %copy.132), calls=%async_computation | async-start | bytes 524288 | tf_op jit(solution)/shard_map/all_to_all | solution.py:127

commit v7 on v6

--- a/solution.py
+++ b/solution.py
@@ -110,6 +110,18 @@
     return total
 
 
+def gather_rows(rows, axis):
+    count, index = lax.axis_size(axis), lax.axis_index(axis)
+    step = 1
+    while step < count:
+        pairs = [(i, i ^ step) for i in range(count)]
+        other = lax.ppermute(rows, axis, pairs)
+        low = (index // step) % 2 == 0
+        rows = jnp.where(low, jnp.concatenate([rows, other]), jnp.concatenate([other, rows]))
+        step *= 2
+    return rows
+
+
 def shards(
     slab_inverse, coupling, injection, neighbors, mode_shift, mode_table, emit_weight, absorb_weight
 ):
@@ -119,16 +131,11 @@
     devices = moms * groups
     flat = pairs.reshape(local, -1)
     width = flat.shape[1] // devices
-    blocks = jnp.swapaxes(flat.reshape(local, devices, width), 0, 1).reshape(devices, -1)
-    share = -(-moms // groups)
-    ids = jnp.pad(mode_table[0].astype(jnp.float32), (0, share * groups - moms))
-    mine = lax.dynamic_slice_in_dim(ids, lax.axis_index("en") * share, share)
-    rows = jnp.broadcast_to(mine[None], (devices, share))
-    sent = lax.all_to_all(jnp.concatenate([blocks, rows], axis=1), ("mom", "en"), 0, 0)
-    sent = sent.reshape(moms, groups, -1)
-    data = sent[:, :, : local * width].reshape(moms, groups * local, width)
+    blocks = jnp.swapaxes(flat.reshape(local, devices, width), 0, 1)
+    table = gather_rows(mode_table[0].astype(jnp.float32)[None], "mom").astype(jnp.int32)
+    sent = lax.all_to_all(blocks, ("mom", "en"), 0, 0)
+    data = sent.reshape(moms, groups * local, width)
     data = jnp.pad(data, ((0, 0), (SHIFT_MAX, SHIFT_MAX), (0, 0)))
-    table = sent[:, :, local * width :].reshape(moms, -1)[:, :moms].astype(jnp.int32)
     weights = shift_weights(table, mode_shift, emit_weight, absorb_weight)
     mixed = mix(data, weights, groups * local)
     mixed = mixed.reshape(devices, local, width)

time: 67.7 us -> 81.8 us (1.21)
  starting transfers between devices: 15.6 us -> 23.9 us
  waiting for transfers between devices: 15.2 us -> 19.9 us
  other arithmetic: 3.3 us -> 4.28 us
    ppermute x0 -> x6, starting transfers between devices: none -> 11 us  [gather_rows(): other = lax.ppermute(rows, axis, pairs)]
    ppermute x0 -> x6, waiting for transfers between devices: none -> 7.5 us  [gather_rows(): other = lax.ppermute(rows, axis, pairs)]
    all_to_all x1, waiting for transfers between devices: 15.2 us -> 12.4 us  [shards(): sent = lax.all_to_all(blocks, ('mom', 'en'), 0, 0)]
    all_to_all x1, starting transfers between devices: 15.6 us -> 12.9 us  [shards(): sent = lax.all_to_all(blocks, ('mom', 'en'), 0, 0)]
    unnamed x23 -> x22, local copies, waits for them, and re-layouts: 2.02 us -> 3 us
    all_to_all x2 -> x1, local copies, waits for them, and re-layouts: 1.34 us -> 0.51 us  [shards(): sent = lax.all_to_all(blocks, ('mom', 'en'), 0, 0)]
  transfers between devices with their start and end apart: 1 -> 7, of which waited for: 1 -> 4; matrix products, arithmetic and copies ran while one was open for 0% -> 15% of each run, Pallas kernels for 0% -> 0%
where the time goes in v7:
time: 81.8 us; the launch traced here: 81.6 us
  starting transfers between devices  23.9 us (29%)
  waiting for transfers between devices  19.9 us (24%)
  blocking collectives  18.3 us (22%)
  matrix products  8.62 us (11%)
  local copies, waits for them, and re-layouts  5.86 us (7%)
  other arithmetic  4.28 us (5%)
    all_to_all x1, blocking collectives, shards(): back = lax.all_to_all(mixed, ('mom', 'en'), 0, 0)  18.3 us
    all_to_all x1, starting transfers between devices, shards(): sent = lax.all_to_all(blocks, ('mom', 'en'), 0, 0)  12.9 us
    all_to_all x1, waiting for transfers between devices, shards(): sent = lax.all_to_all(blocks, ('mom', 'en'), 0, 0)  12.4 us
    ppermute x6, starting transfers between devices, gather_rows(): other = lax.ppermute(rows, axis, pairs)  11 us
    ppermute x6, waiting for transfers between devices, gather_rows(): other = lax.ppermute(rows, axis, pairs)  7.5 us
    dot_general x7, matrix products, cmul(): jnp.einsum(spec, block(left), column(right, adjoint), precision=CHAIN)  3.7 us
    dot_general x1, matrix products, slab_pairs(): jnp.einsum('qesxoc,sojc->qesjxo', jnp.stack(pieces), selector, preferred_...  3.54 us
    unnamed x22, local copies, waits for them, and re-layouts  3 us
  transfers between devices with their start and end apart: 7, of which 4 were waited for; matrix products, arithmetic and copies ran while one was open for 15% of the time, Pallas kernels for 0%

profile of v7, /device:TPU:1, one launch (start us, length us, event | category | flops | bytes accessed | tf_op | source)
XLA Modules:
  0.0 81.6 jit_solution(3519881306529117124)
XLA Ops:
  0.0 0.0 copy-start.2
  0.0 0.0 copy-start
  0.0 0.7 convert_element_type.59
  0.7 3.2 %collective-permute-start = (f32[1,64]{1,0:T(1,128)S(1)}, f32[1,64]{1,0:T(1,128)S(1)}, u32[]{:S(2)}, u32[]{:S(2)}) collective-permute-start(f32[1,64]{1,0:T(1,128)S(1)} %convert_element_type.59), channel_id=1, source_target_pairs={{0,4},{4,0},{8,12},{12,8},{16,20},{20,16},{24,28},{28,24},{32,36},... | collective-permute-start | bytes 776 | tf_op jit(solution)/shard_map/ppermute | solution.py:118
  3.9 1.2 %copy.103 = f32[1,2,2,2,128,128]{4,5,1,3,2,0:T(8,128)S(1)} copy(f32[1,2,2,2,128,128]{5,4,3,2,1,0:T(8,128)} %param.8) | data formatting | bytes 1048576 | tf_op args[0]
  5.2 0.0 copy-done.2
  5.2 0.1 broadcast_multiply_fusion
  5.4 0.0 copy-done
  5.5 0.6 fusion.18
  6.1 0.1 copy.105
  6.3 0.4 fusion.34
  6.9 0.6 fusion.7
  7.6 0.6 fusion.26
  8.3 0.4 fusion.38
  8.7 0.1 copy.115
  9.0 0.6 fusion.46
  9.7 0.0 copy-start.1
  9.7 0.4 fusion.54
  10.1 0.2 reduce-precision_convert_fusion.1
  10.3 0.0 collective-permute-done
  10.4 0.1 collective-permute-start.1
  10.5 2.4 %collective-permute-done.1 = f32[2,64]{1,0:T(2,128)S(1)} collective-permute-done((f32[2,64]{1,0:T(2,128)S(1)}, f32[2,64]{1,0:T(2,128)S(1)}, u32[]{:S(2)}, u32[]{:S(2)}) %collective-permute-start.1) | collective-permute-done | bytes 544 | tf_op jit(solution)/shard_map/ppermute | solution.py:118
  12.9 1.1 %collective-permute-start.2 = (f32[4,64]{1,0:T(4,128)S(1)}, f32[4,64]{1,0:T(4,128)S(1)}, u32[]{:S(2)}, u32[]{:S(2)}) collective-permute-start(f32[4,64]{1,0:T(4,128)S(1)} %maximum_select_fusion.4), channel_id=1, source_target_pairs={{0,16},{4,20},{8,24},{12,28},{16,0},{20,4},{24,8},{28,12},{32,48},... | collective-permute-start | bytes 3080 | tf_op jit(solution)/shard_map/ppermute | solution.py:118
  14.0 2.9 %collective-permute-done.2 = f32[4,64]{1,0:T(4,128)S(1)} collective-permute-done((f32[4,64]{1,0:T(4,128)S(1)}, f32[4,64]{1,0:T(4,128)S(1)}, u32[]{:S(2)}, u32[]{:S(2)}) %collective-permute-start.2) | collective-permute-done | bytes 1056 | tf_op jit(solution)/shard_map/ppermute | solution.py:118
  16.9 0.1 collective-permute-start.3
  17.0 0.1 pad_maximum_fusion
  17.2 0.0 copy-done.1
  17.2 0.1 copy.102
  17.3 2.2 %collective-permute-done.3 = f32[8,64]{1,0:T(8,128)S(1)} collective-permute-done((f32[8,64]{1,0:T(8,128)S(1)}, f32[8,64]{1,0:T(8,128)S(1)}, u32[]{:S(2)}, u32[]{:S(2)}) %collective-permute-start.3) | collective-permute-done | bytes 2080 | tf_op jit(solution)/shard_map/ppermute | solution.py:118
  19.5 1.5 %collective-permute-start.4 = (f32[16,64]{1,0:T(8,128)S(1)}, f32[16,64]{1,0:T(8,128)S(1)}, u32[]{:S(2)}, u32[]{:S(2)}) collective-permute-start(f32[16,64]{1,0:T(8,128)S(1)} %maximum_select_fusion.2), channel_id=1, source_target_pairs={{0,64},{4,68},{8,72},{12,76},{16,80},{20,84},{24,88},{28,92},{32,9... | collective-permute-start | bytes 12296 | tf_op jit(solution)/shard_map/ppermute | solution.py:118
  21.0 3.5 %fusion.4 = f32[3,2,2,32,2,128]{3,0,4,1,5,2:T(4,128)S(1)} fusion(s32[2,128,32]{2,1,0:T(8,128)S(1)} %copy.102, bf16[3,2,2,2,128,128]{5,4,3,2,1,0:T(8,128)(2,1)S(1)} %pad_maximum_fusion), kind=kOutput, calls=%fused_computation.4 | convolution fusion | flops 26214400 | bytes 1212416 | tf_op jit(solution)/shard_map/qesxoc,sojc->qesjxo/dot_general | solution.py:82
  24.5 0.0 collective-permute-done.4
  24.6 0.0 copy-start.5
  24.6 0.0 copy-start.3
  24.6 0.0 copy-start.4
  24.6 5.0 %collective-permute-start.5 = (f32[32,64]{1,0:T(8,128)S(1)}, f32[32,64]{1,0:T(8,128)S(1)}, u32[]{:S(2)}, u32[]{:S(2)}) collective-permute-start(f32[32,64]{1,0:T(8,128)S(1)} %maximum_select_fusion.1), channel_id=1, source_target_pairs={{0,128},{4,132},{8,136},{12,140},{16,144},{20,148},{24,152},{28,15... | collective-permute-start | bytes 24584 | tf_op jit(solution)/shard_map/ppermute | solution.py:118
  29.6 0.8 slice_add_fusion
  30.4 0.4 copy.121
  30.9 0.2 add.64
  31.1 0.2 copy.122
  31.3 0.9 %reshape.292 = f32[256,1,128]{2,1,0:T(1,128)} reshape(f32[256,2,64]{2,1,0:T(2,128)S(1)} %copy.122) | data formatting | bytes 262144
  32.2 12.9 %all-to-all-start = ((f32[256,1,128]{2,1,0:T(1,128)}), f32[256,1,128]{2,1,0:T(1,128)S(1)}, u32[]{:S(2)}, u32[]{:S(2)}) async-start(f32[256,1,128]{2,1,0:T(1,128)} %reshape.292), calls=%async_computation | async-start | bytes 262144 | tf_op jit(solution)/shard_map/all_to_all | solution.py:136
  45.1 0.0 copy-done.5
  45.1 0.0 collective-permute-done.5
  45.2 0.0 copy-done.3
  45.2 0.0 copy-done.4
  45.2 0.1 select_reduce_fusion.1
  45.4 12.4 %all-to-all-done = f32[256,1,128]{2,1,0:T(1,128)S(1)} async-done(((f32[256,1,128]{2,1,0:T(1,128)}), f32[256,1,128]{2,1,0:T(1,128)S(1)}, u32[]{:S(2)}, u32[]{:S(2)}) %all-to-all-start) | async-done | bytes 131104 | tf_op jit(solution)/shard_map/all_to_all | solution.py:136
  57.7 0.5 broadcast.117
  58.3 0.9 %reduce = f32[256,128]{1,0:T(8,128)S(1)} reduce(f32[256,1,128]{2,1,0:T(1,128)S(1)} %all-to-all-done, f32[]{:T(128)} %broadcast.117), dimensions={1}, to_apply=%all_to_all.6.reduce_sub_computation | reduce | bytes 262148 | tf_op jit(solution)/shard_map/all_to_all | solution.py:136
  59.2 0.2 reshape.293
  59.4 0.1 copy.123
  59.5 0.3 fusion.62
  59.8 0.4 convolution_add_fusion.2
  60.2 0.3 convolution_add_fusion.1
  60.5 0.3 convolution_add_fusion
  60.9 0.2 copy.124
  61.0 0.3 reshape.294
  61.3 18.3 %all_to_all.10 = f32[256,1,128]{2,1,0:T(1,128)S(1)} all-to-all(f32[256,1,128]{2,1,0:T(1,128)S(1)} %reshape.294), channel_id=1, replica_groups=mesh['mom'=64,'en'=4] {'mom','en'}, dimensions={0} | all-to-all | bytes 262144 | tf_op jit(solution)/shard_map/all_to_all | solution.py:142
  79.6 0.9 %reduce.1 = f32[256,128]{1,0:T(8,128)S(1)} reduce(f32[256,1,128]{2,1,0:T(1,128)S(1)} %all_to_all.10, f32[]{:T(128)} %broadcast.117), dimensions={1}, to_apply=%all_to_all.7.reduce_sub_computation | reduce | bytes 262148 | tf_op jit(solution)/shard_map/all_to_all | solution.py:142
  80.6 0.2 reshape.295
  80.8 0.8 broadcast_in_dim_reshape.3
  (39 shorter events, 0.7 us)
Async XLA Ops:
  0.0 5.2 %copy-start.2 = (f32[1,2,2,128]{3,2,1,0:T(2,128)S(1)}, f32[1,2,2,128]{3,2,1,0:T(2,128)}, u32[]{:S(2)}) copy-start(f32[1,2,2,128]{3,2,1,0:T(2,128)} %param.10) | copy-start | bytes 6148
  0.0 5.4 %copy-start = (f32[1,2,2,128,128]{4,3,2,1,0:T(8,128)S(1)}, f32[1,2,2,128,128]{4,3,2,1,0:T(8,128)}, u32[]{:S(2)}) copy-start(f32[1,2,2,128,128]{4,3,2,1,0:T(8,128)} %param.9) | copy-start | bytes 786436
  0.7 9.6 %collective-permute-start = (f32[1,64]{1,0:T(1,128)S(1)}, f32[1,64]{1,0:T(1,128)S(1)}, u32[]{:S(2)}, u32[]{:S(2)}) collective-permute-start(f32[1,64]{1,0:T(1,128)S(1)} %convert_element_type.59), channel_id=1, source_target_pairs={{0,4},{4,0},{8,12},{12,8},{16,20},{20,16},{24,28},{28,24},{32,36},... | collective-permute-start | bytes 776 | tf_op jit(solution)/shard_map/ppermute | solution.py:118
  9.7 7.4 %copy-start.1 = (s32[2,128,32]{1,2,0:T(8,128)S(1)}, s32[2,128,32]{1,2,0:T(8,128)}, u32[]{:S(2)}) copy-start(s32[2,128,32]{1,2,0:T(8,128)} %param.11) | copy-start | bytes 98308
  10.4 2.5 %collective-permute-start.1 = (f32[2,64]{1,0:T(2,128)S(1)}, f32[2,64]{1,0:T(2,128)S(1)}, u32[]{:S(2)}, u32[]{:S(2)}) collective-permute-start(f32[2,64]{1,0:T(2,128)S(1)} %maximum_select_fusion.5), channel_id=1, source_target_pairs={{0,8},{4,12},{8,0},{12,4},{16,24},{20,28},{24,16},{28,20},{32,40},... | collective-permute-start | bytes 1544 | tf_op jit(solution)/shard_map/ppermute | solution.py:118
  12.9 4.0 %collective-permute-start.2 = (f32[4,64]{1,0:T(4,128)S(1)}, f32[4,64]{1,0:T(4,128)S(1)}, u32[]{:S(2)}, u32[]{:S(2)}) collective-permute-start(f32[4,64]{1,0:T(4,128)S(1)} %maximum_select_fusion.4), channel_id=1, source_target_pairs={{0,16},{4,20},{8,24},{12,28},{16,0},{20,4},{24,8},{28,12},{32,48},... | collective-permute-start | bytes 3080 | tf_op jit(solution)/shard_map/ppermute | solution.py:118
  16.9 2.5 %collective-permute-start.3 = (f32[8,64]{1,0:T(8,128)S(1)}, f32[8,64]{1,0:T(8,128)S(1)}, u32[]{:S(2)}, u32[]{:S(2)}) collective-permute-start(f32[8,64]{1,0:T(8,128)S(1)} %maximum_select_fusion.3), channel_id=1, source_target_pairs={{0,32},{4,36},{8,40},{12,44},{16,48},{20,52},{24,56},{28,60},{32,0... | collective-permute-start | bytes 6152 | tf_op jit(solution)/shard_map/ppermute | solution.py:118
  19.5 5.0 %collective-permute-start.4 = (f32[16,64]{1,0:T(8,128)S(1)}, f32[16,64]{1,0:T(8,128)S(1)}, u32[]{:S(2)}, u32[]{:S(2)}) collective-permute-start(f32[16,64]{1,0:T(8,128)S(1)} %maximum_select_fusion.2), channel_id=1, source_target_pairs={{0,64},{4,68},{8,72},{12,76},{16,80},{20,84},{24,88},{28,92},{32,9... | collective-permute-start | bytes 12296 | tf_op jit(solution)/shard_map/ppermute | solution.py:118
  24.6 20.6 %copy-start.5 = (s32[6]{0:T(128)S(1)}, s32[6]{0:T(128)}, u32[]{:S(2)}) copy-start(s32[6]{0:T(128)} %param.12) | copy-start | bytes 76
  24.6 20.6 %copy-start.3 = (f32[6]{0:T(128)S(1)}, f32[6]{0:T(128)}, u32[]{:S(2)}) copy-start(f32[6]{0:T(128)} %param.14) | copy-start | bytes 76
  24.6 20.6 %copy-start.4 = (f32[6]{0:T(128)S(1)}, f32[6]{0:T(128)}, u32[]{:S(2)}) copy-start(f32[6]{0:T(128)} %param.15) | copy-start | bytes 76
  24.6 20.6 %collective-permute-start.5 = (f32[32,64]{1,0:T(8,128)S(1)}, f32[32,64]{1,0:T(8,128)S(1)}, u32[]{:S(2)}, u32[]{:S(2)}) collective-permute-start(f32[32,64]{1,0:T(8,128)S(1)} %maximum_select_fusion.1), channel_id=1, source_target_pairs={{0,128},{4,132},{8,136},{12,140},{16,144},{20,148},{24,152},{28,15... | collective-permute-start | bytes 24584 | tf_op jit(solution)/shard_map/ppermute | solution.py:118
  32.2 25.6 %all-to-all-start = ((f32[256,1,128]{2,1,0:T(1,128)}), f32[256,1,128]{2,1,0:T(1,128)S(1)}, u32[]{:S(2)}, u32[]{:S(2)}) async-start(f32[256,1,128]{2,1,0:T(1,128)} %reshape.292), calls=%async_computation | async-start | bytes 262144 | tf_op jit(solution)/shard_map/all_to_all | solution.py:136

commit v8 on v7

--- a/solution.py
+++ b/solution.py
@@ -110,15 +110,26 @@
     return total
 
 
-def gather_rows(rows, axis):
+def gather_rows(rows, axis, group=8):
     count, index = lax.axis_size(axis), lax.axis_index(axis)
-    step = 1
-    while step < count:
-        pairs = [(i, i ^ step) for i in range(count)]
-        other = lax.ppermute(rows, axis, pairs)
-        low = (index // step) % 2 == 0
-        rows = jnp.where(low, jnp.concatenate([rows, other]), jnp.concatenate([other, rows]))
-        step *= 2
+    stride = 1
+    while stride < count:
+        size = min(group, count // stride)
+        position = (index // stride) % size
+        received = [rows]
+        for shift in range(1, size):
+            pairs = []
+            for i in range(count):
+                low = (i // stride) % size
+                target = i + (((low + shift) % size) - low) * stride
+                pairs.append((i, target))
+            received.append(lax.ppermute(rows, axis, pairs))
+        stacked = jnp.stack(received)
+        slots = (position - jnp.arange(size)) % size
+        order = (slots[:, None] == jnp.arange(size)[None, :]).astype(jnp.float32)
+        rows = jnp.einsum("bs,s...->b...", order, stacked, precision=HIGH)
+        rows = rows.reshape((-1,) + rows.shape[2:])
+        stride *= size
     return rows
 
 

time: 81.8 us -> 88.4 us (1.081)
  starting transfers between devices: 23.9 us -> 40.3 us
  waiting for transfers between devices: 19.9 us -> 3.75 us
  blocking collectives: 18.3 us -> 24.1 us
    ppermute x6 -> x14, starting transfers between devices: 11 us -> 28.7 us  [gather_rows(): received.append(lax.ppermute(rows, axis, pairs))]
    all_to_all x1, waiting for transfers between devices: 12.4 us -> 0.01 us  [shards(): sent = lax.all_to_all(blocks, ('mom', 'en'), 0, 0)]
    all_to_all x1, blocking collectives: 18.3 us -> 24.1 us  [shards(): back = lax.all_to_all(mixed, ('mom', 'en'), 0, 0)]
    ppermute x6 -> x14, waiting for transfers between devices: 7.5 us -> 3.75 us  [gather_rows(): received.append(lax.ppermute(rows, axis, pairs))]
    all_to_all x1, starting transfers between devices: 12.9 us -> 11.7 us  [shards(): sent = lax.all_to_all(blocks, ('mom', 'en'), 0, 0)]
    unnamed x22 -> x36, local copies, waits for them, and re-layouts: 3 us -> 3.07 us
  transfers between devices with their start and end apart: 7 -> 15, of which waited for: 4 -> 2; matrix products, arithmetic and copies ran while one was open for 15% -> 15% of each run, Pallas kernels for 0% -> 0%
where the time goes in v8:
time: 88.4 us; the launch traced here: 88.2 us
  starting transfers between devices  40.3 us (46%)
  blocking collectives  24.1 us (27%)
  matrix products  9.05 us (10%)
  local copies, waits for them, and re-layouts  5.95 us (7%)
  other arithmetic  4.26 us (5%)
  waiting for transfers between devices  3.75 us (4%)
    ppermute x14, starting transfers between devices, gather_rows(): received.append(lax.ppermute(rows, axis, pairs))  28.7 us
    all_to_all x1, blocking collectives, shards(): back = lax.all_to_all(mixed, ('mom', 'en'), 0, 0)  24.1 us
    all_to_all x1, starting transfers between devices, shards(): sent = lax.all_to_all(blocks, ('mom', 'en'), 0, 0)  11.7 us
    ppermute x14, waiting for transfers between devices, gather_rows(): received.append(lax.ppermute(rows, axis, pairs))  3.75 us
    dot_general x7, matrix products, cmul(): jnp.einsum(spec, block(left), column(right, adjoint), precision=CHAIN)  3.71 us
    dot_general x1, matrix products, slab_pairs(): jnp.einsum('qesxoc,sojc->qesjxo', jnp.stack(pieces), selector, preferred_...  3.57 us
    unnamed x36, local copies, waits for them, and re-layouts  3.07 us
  transfers between devices with their start and end apart: 15, of which 2 were waited for; matrix products, arithmetic and copies ran while one was open for 15% of the time, Pallas kernels for 0%

profile of v8, /device:TPU:1, one launch (start us, length us, event | category | flops | bytes accessed | tf_op | source)
XLA Modules:
  0.0 88.2 jit_solution(13805808362803092056)
XLA Ops:
  0.0 0.7 convert_element_type.74
  0.7 2.6 %collective-permute-start = (f32[1,64]{1,0:T(1,128)S(1)}, f32[1,64]{1,0:T(1,128)S(1)}, u32[]{:S(2)}, u32[]{:S(2)}) collective-permute-start(f32[1,64]{1,0:T(1,128)S(1)} %convert_element_type.74), channel_id=1, source_target_pairs={{0,4},{4,8},{8,12},{12,16},{16,20},{20,24},{24,28},{28,0},{32,36},... | collective-permute-start | bytes 776 | tf_op jit(solution)/shard_map/ppermute | solution.py:126
  3.3 1.2 %collective-permute-start.1 = (f32[1,64]{1,0:T(1,128)S(1)}, f32[1,64]{1,0:T(1,128)S(1)}, u32[]{:S(2)}, u32[]{:S(2)}) collective-permute-start(f32[1,64]{1,0:T(1,128)S(1)} %convert_element_type.74), channel_id=1, source_target_pairs={{0,8},{4,12},{8,16},{12,20},{16,24},{20,28},{24,0},{28,4},{32,40},... | collective-permute-start | bytes 776 | tf_op jit(solution)/shard_map/ppermute | solution.py:126
  4.5 1.5 %collective-permute-start.2 = (f32[1,64]{1,0:T(1,128)S(1)}, f32[1,64]{1,0:T(1,128)S(1)}, u32[]{:S(2)}, u32[]{:S(2)}) collective-permute-start(f32[1,64]{1,0:T(1,128)S(1)} %convert_element_type.74), channel_id=1, source_target_pairs={{0,12},{4,16},{8,20},{12,24},{16,28},{20,0},{24,4},{28,8},{32,44},... | collective-permute-start | bytes 776 | tf_op jit(solution)/shard_map/ppermute | solution.py:126
  6.0 1.6 %collective-permute-start.3 = (f32[1,64]{1,0:T(1,128)S(1)}, f32[1,64]{1,0:T(1,128)S(1)}, u32[]{:S(2)}, u32[]{:S(2)}) collective-permute-start(f32[1,64]{1,0:T(1,128)S(1)} %convert_element_type.74), channel_id=1, source_target_pairs={{0,16},{4,20},{8,24},{12,28},{16,0},{20,4},{24,8},{28,12},{32,48},... | collective-permute-start | bytes 776 | tf_op jit(solution)/shard_map/ppermute | solution.py:126
  7.7 2.6 %collective-permute-start.4 = (f32[1,64]{1,0:T(1,128)S(1)}, f32[1,64]{1,0:T(1,128)S(1)}, u32[]{:S(2)}, u32[]{:S(2)}) collective-permute-start(f32[1,64]{1,0:T(1,128)S(1)} %convert_element_type.74), channel_id=1, source_target_pairs={{0,20},{4,24},{8,28},{12,0},{16,4},{20,8},{24,12},{28,16},{32,52},... | collective-permute-start | bytes 776 | tf_op jit(solution)/shard_map/ppermute | solution.py:126
  10.3 1.2 %copy.112 = f32[1,2,2,2,128,128]{4,5,1,3,2,0:T(8,128)S(1)} copy(f32[1,2,2,2,128,128]{5,4,3,2,1,0:T(8,128)} %param.8) | data formatting | bytes 1048576 | tf_op args[0]
  11.6 0.1 broadcast_multiply_fusion
  11.9 0.6 fusion.18
  12.5 0.1 copy.114
  12.7 0.4 fusion.34
  13.3 0.6 fusion.7
  14.0 0.6 fusion.26
  14.7 0.4 fusion.38
  15.1 0.1 copy.124
  15.3 0.0 copy-start.1
  15.4 0.6 fusion.46
  16.1 0.1 copy.111
  16.2 0.4 fusion.54
  16.6 0.2 reduce-precision_convert_fusion.1
  16.8 0.1 pad_maximum_fusion
  16.9 3.6 %fusion.4 = f32[3,2,2,32,2,128]{3,0,4,1,5,2:T(4,128)S(1)} fusion(s32[2,128,32]{2,1,0:T(8,128)S(1)} %copy.111, bf16[3,2,2,2,128,128]{5,4,3,2,1,0:T(8,128)(2,1)S(1)} %pad_maximum_fusion), kind=kOutput, calls=%fused_computation.4 | convolution fusion | flops 26214400 | bytes 1212416 | tf_op jit(solution)/shard_map/qesxoc,sojc->qesjxo/dot_general | solution.py:82
  20.5 0.0 copy-start.5
  20.5 0.0 copy-start.6
  20.5 0.0 copy-start.3
  20.5 0.0 copy-start.4
  20.5 0.8 slice_add_fusion
  21.4 0.4 copy.130
  21.8 0.2 add.64
  22.0 0.2 copy.131
  22.2 0.9 %reshape.303 = f32[256,1,128]{2,1,0:T(1,128)} reshape(f32[256,2,64]{2,1,0:T(2,128)S(1)} %copy.131) | data formatting | bytes 262144
  23.1 11.7 %all-to-all-start = ((f32[256,1,128]{2,1,0:T(1,128)}), f32[256,1,128]{2,1,0:T(1,128)S(1)}, u32[]{:S(2)}, u32[]{:S(2)}) async-start(f32[256,1,128]{2,1,0:T(1,128)} %reshape.303), calls=%async_computation | async-start | bytes 262144 | tf_op jit(solution)/shard_map/all_to_all | solution.py:147
  34.9 0.0 collective-permute-done
  34.9 2.6 %collective-permute-start.5 = (f32[1,64]{1,0:T(1,128)S(1)}, f32[1,64]{1,0:T(1,128)S(1)}, u32[]{:S(2)}, u32[]{:S(2)}) collective-permute-start(f32[1,64]{1,0:T(1,128)S(1)} %convert_element_type.74), channel_id=1, source_target_pairs={{0,24},{4,28},{8,0},{12,4},{16,8},{20,12},{24,16},{28,20},{32,56},... | collective-permute-start | bytes 776 | tf_op jit(solution)/shard_map/ppermute | solution.py:126
  37.5 0.7 collective-permute-start.6
  38.2 0.0 collective-permute-done.3
  38.3 0.0 collective-permute-done.5
  38.3 2.2 %collective-permute-done.6 = f32[1,64]{1,0:T(1,128)S(1)} collective-permute-done((f32[1,64]{1,0:T(1,128)S(1)}, f32[1,64]{1,0:T(1,128)S(1)}, u32[]{:S(2)}, u32[]{:S(2)}) %collective-permute-start.6) | collective-permute-done | bytes 288 | tf_op jit(solution)/shard_map/ppermute | solution.py:126
  40.5 0.2 constant_dynamic-update-slice_fusion.15
  40.7 1.5 %collective-permute-start.7 = (f32[8,64]{1,0:T(8,128)S(1)}, f32[8,64]{1,0:T(8,128)S(1)}, u32[]{:S(2)}, u32[]{:S(2)}) collective-permute-start(f32[8,64]{1,0:T(8,128)S(1)} %get-tuple-element.54), channel_id=1, source_target_pairs={{0,32},{4,36},{8,40},{12,44},{16,48},{20,52},{24,56},{28,60},{32,6... | collective-permute-start | bytes 6152 | tf_op jit(solution)/shard_map/ppermute | solution.py:126
  42.2 2.7 %collective-permute-start.8 = (f32[8,64]{1,0:T(8,128)S(1)}, f32[8,64]{1,0:T(8,128)S(1)}, u32[]{:S(2)}, u32[]{:S(2)}) collective-permute-start(f32[8,64]{1,0:T(8,128)S(1)} %get-tuple-element.54), channel_id=1, source_target_pairs={{0,64},{4,68},{8,72},{12,76},{16,80},{20,84},{24,88},{28,92},{32,9... | collective-permute-start | bytes 6152 | tf_op jit(solution)/shard_map/ppermute | solution.py:126
  44.9 3.2 %collective-permute-start.9 = (f32[8,64]{1,0:T(8,128)S(1)}, f32[8,64]{1,0:T(8,128)S(1)}, u32[]{:S(2)}, u32[]{:S(2)}) collective-permute-start(f32[8,64]{1,0:T(8,128)S(1)} %get-tuple-element.54), channel_id=1, source_target_pairs={{0,96},{4,100},{8,104},{12,108},{16,112},{20,116},{24,120},{28,124... | collective-permute-start | bytes 6152 | tf_op jit(solution)/shard_map/ppermute | solution.py:126
  48.1 1.0 %collective-permute-start.10 = (f32[8,64]{1,0:T(8,128)S(1)}, f32[8,64]{1,0:T(8,128)S(1)}, u32[]{:S(2)}, u32[]{:S(2)}) collective-permute-start(f32[8,64]{1,0:T(8,128)S(1)} %get-tuple-element.54), channel_id=1, source_target_pairs={{0,128},{4,132},{8,136},{12,140},{16,144},{20,148},{24,152},{28,15... | collective-permute-start | bytes 6152 | tf_op jit(solution)/shard_map/ppermute | solution.py:126
  49.1 3.7 %collective-permute-start.11 = (f32[8,64]{1,0:T(8,128)S(1)}, f32[8,64]{1,0:T(8,128)S(1)}, u32[]{:S(2)}, u32[]{:S(2)}) collective-permute-start(f32[8,64]{1,0:T(8,128)S(1)} %get-tuple-element.54), channel_id=1, source_target_pairs={{0,160},{4,164},{8,168},{12,172},{16,176},{20,180},{24,184},{28,18... | collective-permute-start | bytes 6152 | tf_op jit(solution)/shard_map/ppermute | solution.py:126
  52.9 0.0 collective-permute-done.7
  52.9 2.8 %collective-permute-start.12 = (f32[8,64]{1,0:T(8,128)S(1)}, f32[8,64]{1,0:T(8,128)S(1)}, u32[]{:S(2)}, u32[]{:S(2)}) collective-permute-start(f32[8,64]{1,0:T(8,128)S(1)} %get-tuple-element.54), channel_id=1, source_target_pairs={{0,192},{4,196},{8,200},{12,204},{16,208},{20,212},{24,216},{28,22... | collective-permute-start | bytes 6152 | tf_op jit(solution)/shard_map/ppermute | solution.py:126
  55.6 0.9 %collective-permute-start.13 = (f32[8,64]{1,0:T(8,128)S(1)}, f32[8,64]{1,0:T(8,128)S(1)}, u32[]{:S(2)}, u32[]{:S(2)}) collective-permute-start(f32[8,64]{1,0:T(8,128)S(1)} %get-tuple-element.54), channel_id=1, source_target_pairs={{0,224},{4,228},{8,232},{12,236},{16,240},{20,244},{24,248},{28,25... | collective-permute-start | bytes 6152 | tf_op jit(solution)/shard_map/ppermute | solution.py:126
  56.6 1.5 %collective-permute-done.13 = f32[8,64]{1,0:T(8,128)S(1)} collective-permute-done((f32[8,64]{1,0:T(8,128)S(1)}, f32[8,64]{1,0:T(8,128)S(1)}, u32[]{:S(2)}, u32[]{:S(2)}) %collective-permute-start.13) | collective-permute-done | bytes 2080 | tf_op jit(solution)/shard_map/ppermute | solution.py:126
  58.1 0.2 convolution_convert_fusion
  58.3 0.1 select_reduce_fusion.1
  58.5 0.5 broadcast.160
  59.1 0.9 %reduce = f32[256,128]{1,0:T(8,128)S(1)} reduce(f32[256,1,128]{2,1,0:T(1,128)S(1)} %all-to-all-done, f32[]{:T(128)} %broadcast.160), dimensions={1}, to_apply=%all_to_all.6.reduce_sub_computation | reduce | bytes 262148 | tf_op jit(solution)/shard_map/all_to_all | solution.py:147
  60.0 0.2 reshape.304
  60.2 0.1 copy.132
  60.3 0.3 fusion.62
  60.6 0.4 convolution_add_fusion.2
  61.0 0.3 convolution_add_fusion.1
  61.3 0.3 convolution_add_fusion
  61.7 0.2 copy.133
  61.8 0.3 reshape.305
  62.1 24.1 %all_to_all.10 = f32[256,1,128]{2,1,0:T(1,128)S(1)} all-to-all(f32[256,1,128]{2,1,0:T(1,128)S(1)} %reshape.305), channel_id=1, replica_groups=mesh['mom'=64,'en'=4] {'mom','en'}, dimensions={0} | all-to-all | bytes 262144 | tf_op jit(solution)/shard_map/all_to_all | solution.py:153
  86.2 0.9 %reduce.1 = f32[256,128]{1,0:T(8,128)S(1)} reduce(f32[256,1,128]{2,1,0:T(1,128)S(1)} %all_to_all.10, f32[]{:T(128)} %broadcast.160), dimensions={1}, to_apply=%all_to_all.7.reduce_sub_computation | reduce | bytes 262148 | tf_op jit(solution)/shard_map/all_to_all | solution.py:153
  87.2 0.2 reshape.306
  87.4 0.8 broadcast_in_dim_reshape.3
  (69 shorter events, 0.8 us)
Async XLA Ops:
  0.0 11.6 %copy-start.2 = (f32[1,2,2,128]{3,2,1,0:T(2,128)S(1)}, f32[1,2,2,128]{3,2,1,0:T(2,128)}, u32[]{:S(2)}) copy-start(f32[1,2,2,128]{3,2,1,0:T(2,128)} %param.10) | copy-start | bytes 6148
  0.0 11.7 %copy-start = (f32[1,2,2,128,128]{4,3,2,1,0:T(8,128)S(1)}, f32[1,2,2,128,128]{4,3,2,1,0:T(8,128)}, u32[]{:S(2)}) copy-start(f32[1,2,2,128,128]{4,3,2,1,0:T(8,128)} %param.9) | copy-start | bytes 786436
  0.7 34.2 %collective-permute-start = (f32[1,64]{1,0:T(1,128)S(1)}, f32[1,64]{1,0:T(1,128)S(1)}, u32[]{:S(2)}, u32[]{:S(2)}) collective-permute-start(f32[1,64]{1,0:T(1,128)S(1)} %convert_element_type.74), channel_id=1, source_target_pairs={{0,4},{4,8},{8,12},{12,16},{16,20},{20,24},{24,28},{28,0},{32,36},... | collective-permute-start | bytes 776 | tf_op jit(solution)/shard_map/ppermute | solution.py:126
  3.3 34.2 %collective-permute-start.1 = (f32[1,64]{1,0:T(1,128)S(1)}, f32[1,64]{1,0:T(1,128)S(1)}, u32[]{:S(2)}, u32[]{:S(2)}) collective-permute-start(f32[1,64]{1,0:T(1,128)S(1)} %convert_element_type.74), channel_id=1, source_target_pairs={{0,8},{4,12},{8,16},{12,20},{16,24},{20,28},{24,0},{28,4},{32,40},... | collective-permute-start | bytes 776 | tf_op jit(solution)/shard_map/ppermute | solution.py:126
  4.5 33.7 %collective-permute-start.2 = (f32[1,64]{1,0:T(1,128)S(1)}, f32[1,64]{1,0:T(1,128)S(1)}, u32[]{:S(2)}, u32[]{:S(2)}) collective-permute-start(f32[1,64]{1,0:T(1,128)S(1)} %convert_element_type.74), channel_id=1, source_target_pairs={{0,12},{4,16},{8,20},{12,24},{16,28},{20,0},{24,4},{28,8},{32,44},... | collective-permute-start | bytes 776 | tf_op jit(solution)/shard_map/ppermute | solution.py:126
  6.0 32.2 %collective-permute-start.3 = (f32[1,64]{1,0:T(1,128)S(1)}, f32[1,64]{1,0:T(1,128)S(1)}, u32[]{:S(2)}, u32[]{:S(2)}) collective-permute-start(f32[1,64]{1,0:T(1,128)S(1)} %convert_element_type.74), channel_id=1, source_target_pairs={{0,16},{4,20},{8,24},{12,28},{16,0},{20,4},{24,8},{28,12},{32,48},... | collective-permute-start | bytes 776 | tf_op jit(solution)/shard_map/ppermute | solution.py:126
  7.7 30.6 %collective-permute-start.4 = (f32[1,64]{1,0:T(1,128)S(1)}, f32[1,64]{1,0:T(1,128)S(1)}, u32[]{:S(2)}, u32[]{:S(2)}) collective-permute-start(f32[1,64]{1,0:T(1,128)S(1)} %convert_element_type.74), channel_id=1, source_target_pairs={{0,20},{4,24},{8,28},{12,0},{16,4},{20,8},{24,12},{28,16},{32,52},... | collective-permute-start | bytes 776 | tf_op jit(solution)/shard_map/ppermute | solution.py:126
  15.3 0.9 copy-start.1
  20.5 14.3 %copy-start.5 = (s32[1,64]{1,0:T(1,128)S(1)}, s32[1,64]{1,0:T(1,128)}, u32[]{:S(2)}) copy-start(s32[1,64]{1,0:T(1,128)} %param.13) | copy-start | bytes 772
  20.5 21.7 %copy-start.6 = (s32[6]{0:T(128)S(1)}, s32[6]{0:T(128)}, u32[]{:S(2)}) copy-start(s32[6]{0:T(128)} %param.12) | copy-start | bytes 76
  20.5 37.8 %copy-start.3 = (f32[6]{0:T(128)S(1)}, f32[6]{0:T(128)}, u32[]{:S(2)}) copy-start(f32[6]{0:T(128)} %param.14) | copy-start | bytes 76
  20.5 37.8 %copy-start.4 = (f32[6]{0:T(128)S(1)}, f32[6]{0:T(128)}, u32[]{:S(2)}) copy-start(f32[6]{0:T(128)} %param.15) | copy-start | bytes 76
  23.1 35.4 %all-to-all-start = ((f32[256,1,128]{2,1,0:T(1,128)}), f32[256,1,128]{2,1,0:T(1,128)S(1)}, u32[]{:S(2)}, u32[]{:S(2)}) async-start(f32[256,1,128]{2,1,0:T(1,128)} %reshape.303), calls=%async_computation | async-start | bytes 262144 | tf_op jit(solution)/shard_map/all_to_all | solution.py:147
  34.9 3.4 %collective-permute-start.5 = (f32[1,64]{1,0:T(1,128)S(1)}, f32[1,64]{1,0:T(1,128)S(1)}, u32[]{:S(2)}, u32[]{:S(2)}) collective-permute-start(f32[1,64]{1,0:T(1,128)S(1)} %convert_element_type.74), channel_id=1, source_target_pairs={{0,24},{4,28},{8,0},{12,4},{16,8},{20,12},{24,16},{28,20},{32,56},... | collective-permute-start | bytes 776 | tf_op jit(solution)/shard_map/ppermute | solution.py:126
  37.5 3.0 %collective-permute-start.6 = (f32[1,64]{1,0:T(1,128)S(1)}, f32[1,64]{1,0:T(1,128)S(1)}, u32[]{:S(2)}, u32[]{:S(2)}) collective-permute-start(f32[1,64]{1,0:T(1,128)S(1)} %convert_element_type.74), channel_id=1, source_target_pairs={{0,28},{4,0},{8,4},{12,8},{16,12},{20,16},{24,20},{28,24},{32,60},... | collective-permute-start | bytes 776 | tf_op jit(solution)/shard_map/ppermute | solution.py:126
  40.7 12.1 %collective-permute-start.7 = (f32[8,64]{1,0:T(8,128)S(1)}, f32[8,64]{1,0:T(8,128)S(1)}, u32[]{:S(2)}, u32[]{:S(2)}) collective-permute-start(f32[8,64]{1,0:T(8,128)S(1)} %get-tuple-element.54), channel_id=1, source_target_pairs={{0,32},{4,36},{8,40},{12,44},{16,48},{20,52},{24,56},{28,60},{32,6... | collective-permute-start | bytes 6152 | tf_op jit(solution)/shard_map/ppermute | solution.py:126
  42.2 13.4 %collective-permute-start.8 = (f32[8,64]{1,0:T(8,128)S(1)}, f32[8,64]{1,0:T(8,128)S(1)}, u32[]{:S(2)}, u32[]{:S(2)}) collective-permute-start(f32[8,64]{1,0:T(8,128)S(1)} %get-tuple-element.54), channel_id=1, source_target_pairs={{0,64},{4,68},{8,72},{12,76},{16,80},{20,84},{24,88},{28,92},{32,9... | collective-permute-start | bytes 6152 | tf_op jit(solution)/shard_map/ppermute | solution.py:126
  44.9 11.6 %collective-permute-start.9 = (f32[8,64]{1,0:T(8,128)S(1)}, f32[8,64]{1,0:T(8,128)S(1)}, u32[]{:S(2)}, u32[]{:S(2)}) collective-permute-start(f32[8,64]{1,0:T(8,128)S(1)} %get-tuple-element.54), channel_id=1, source_target_pairs={{0,96},{4,100},{8,104},{12,108},{16,112},{20,116},{24,120},{28,124... | collective-permute-start | bytes 6152 | tf_op jit(solution)/shard_map/ppermute | solution.py:126
  48.1 8.4 %collective-permute-start.10 = (f32[8,64]{1,0:T(8,128)S(1)}, f32[8,64]{1,0:T(8,128)S(1)}, u32[]{:S(2)}, u32[]{:S(2)}) collective-permute-start(f32[8,64]{1,0:T(8,128)S(1)} %get-tuple-element.54), channel_id=1, source_target_pairs={{0,128},{4,132},{8,136},{12,140},{16,144},{20,148},{24,152},{28,15... | collective-permute-start | bytes 6152 | tf_op jit(solution)/shard_map/ppermute | solution.py:126
  49.1 7.4 %collective-permute-start.11 = (f32[8,64]{1,0:T(8,128)S(1)}, f32[8,64]{1,0:T(8,128)S(1)}, u32[]{:S(2)}, u32[]{:S(2)}) collective-permute-start(f32[8,64]{1,0:T(8,128)S(1)} %get-tuple-element.54), channel_id=1, source_target_pairs={{0,160},{4,164},{8,168},{12,172},{16,176},{20,180},{24,184},{28,18... | collective-permute-start | bytes 6152 | tf_op jit(solution)/shard_map/ppermute | solution.py:126
  52.9 3.7 %collective-permute-start.12 = (f32[8,64]{1,0:T(8,128)S(1)}, f32[8,64]{1,0:T(8,128)S(1)}, u32[]{:S(2)}, u32[]{:S(2)}) collective-permute-start(f32[8,64]{1,0:T(8,128)S(1)} %get-tuple-element.54), channel_id=1, source_target_pairs={{0,192},{4,196},{8,200},{12,204},{16,208},{20,212},{24,216},{28,22... | collective-permute-start | bytes 6152 | tf_op jit(solution)/shard_map/ppermute | solution.py:126
  55.6 2.5 %collective-permute-start.13 = (f32[8,64]{1,0:T(8,128)S(1)}, f32[8,64]{1,0:T(8,128)S(1)}, u32[]{:S(2)}, u32[]{:S(2)}) collective-permute-start(f32[8,64]{1,0:T(8,128)S(1)} %get-tuple-element.54), channel_id=1, source_target_pairs={{0,224},{4,228},{8,232},{12,236},{16,240},{20,244},{24,248},{28,25... | collective-permute-start | bytes 6152 | tf_op jit(solution)/shard_map/ppermute | solution.py:126

commit v9 on v6

--- a/solution.py
+++ b/solution.py
@@ -34,7 +34,7 @@
 def column(value, adjoint=False):
     real, imag = value[..., 0, :, :], value[..., 1, :, :]
     if adjoint:
-        real, imag = jnp.swapaxes(real, -1, -2), -jnp.swapaxes(imag, -1, -2)
+        return jnp.concatenate([real, -imag], axis=-1)
     return jnp.concatenate([real, imag], axis=-2)
 
 
@@ -44,6 +44,8 @@
 
 
 def cmul(left, right, spec="...ij,...jk->...ik", adjoint=False):
+    if adjoint:
+        spec = spec.replace("jk->", "kj->")
     product = jnp.einsum(spec, block(left), column(right, adjoint), precision=CHAIN)
     return split(product)
 
@@ -102,12 +104,10 @@
 
 
 def mix(data, weights, energies):
-    total = None
-    for index, offset in enumerate(OFFSETS):
-        window = data[:, SHIFT_MAX + offset : SHIFT_MAX + offset + energies]
-        term = jnp.einsum("kj,jec->kec", weights[:, index], window, precision=HIGH)
-        total = term if total is None else total + term
-    return total
+    windows = jnp.stack(
+        [data[:, SHIFT_MAX + offset : SHIFT_MAX + offset + energies] for offset in OFFSETS]
+    )
+    return jnp.einsum("kdj,djec->kec", weights, windows, precision=HIGH)
 
 
 def shards(

time: 67.7 us -> 66.1 us (0.976)
  matrix products: 8.66 us -> 7.27 us
    dot_general x7, matrix products: 3.7 us -> 2.9 us  [cmul(): jnp.einsum(spec, block(left), column(right, adjoint), precision=CHAIN)]
    dot_general x4 -> x1, matrix products: 1.38 us -> 0.81 us  [mix(): return jnp.einsum('kdj,djec->kec', weights, windows, precision=HIGH)]
where the time goes in v9:
time: 66.1 us; the launch traced here: 65.9 us
  blocking collectives  18 us (27%)
  starting transfers between devices  15.6 us (24%)
  waiting for transfers between devices  15.2 us (23%)
  matrix products  7.27 us (11%)
  local copies, waits for them, and re-layouts  5.91 us (9%)
  other arithmetic  3.21 us (5%)
    all_to_all x1, blocking collectives, shards(): back = lax.all_to_all(mixed, ('mom', 'en'), 0, 0)  18 us
    all_to_all x1, starting transfers between devices, shards(): lax.all_to_all(jnp.concatenate([blocks, rows], axis=1), ('mom', 'en'), 0, 0)  15.6 us
    all_to_all x1, waiting for transfers between devices, shards(): lax.all_to_all(jnp.concatenate([blocks, rows], axis=1), ('mom', 'en'), 0, 0)  15.2 us
    dot_general x1, matrix products, slab_pairs(): jnp.einsum('qesxoc,sojc->qesjxo', jnp.stack(pieces), selector, preferred_...  3.57 us
    dot_general x7, matrix products, cmul(): jnp.einsum(spec, block(left), column(right, adjoint), precision=CHAIN)  2.9 us
    unnamed x23, local copies, waits for them, and re-layouts  2.04 us
  transfers between devices with their start and end apart: 1, of which 1 were waited for; matrix products, arithmetic and copies ran while one was open for 0% of the time, Pallas kernels for 0%

profile of v9, /device:TPU:1, one launch (start us, length us, event | category | flops | bytes accessed | tf_op | source)
XLA Modules:
  0.0 65.9 jit_solution(13547324001494847146)
XLA Ops:
  0.0 0.0 copy-start.2
  0.0 0.0 copy-start
  0.0 1.1 %copy.146 = f32[1,2,2,2,128,128]{5,4,1,3,2,0:T(8,128)S(1)} copy(f32[1,2,2,2,128,128]{5,4,3,2,1,0:T(8,128)} %param.8) | data formatting | bytes 1048576 | tf_op args[0]
  1.2 0.0 copy-done.2
  1.3 0.0 copy-done
  1.4 0.4 fusion.25
  1.8 0.4 fusion.41
  2.4 0.6 fusion.7
  3.1 0.4 fusion.33
  3.5 0.4 fusion.45
  4.0 0.0 copy-start.1
  4.1 0.4 fusion.53
  4.5 0.2 copy-done.1
  4.7 0.1 copy.99
  4.8 0.4 fusion.61
  5.2 0.2 reduce-precision_convert_fusion.1
  5.4 0.1 pad_maximum_fusion
  5.5 3.6 %fusion.4 = f32[3,2,2,32,2,128]{3,0,4,1,5,2:T(4,128)S(1)} fusion(s32[2,128,32]{2,1,0:T(8,128)S(1)} %copy.99, bf16[3,2,2,2,128,128]{5,4,3,2,1,0:T(8,128)(2,1)S(1)} %pad_maximum_fusion), kind=kOutput, calls=%fused_computation.4 | convolution fusion | flops 26214400 | bytes 1212416 | tf_op jit(solution)/shard_map/qesxoc,sojc->qesjxo/dot_general | solution.py:84
  9.1 0.0 copy-start.5
  9.1 0.0 copy-start.6
  9.1 0.8 %slice_add_fusion = f32[1,2,2,32,2,128]{3,0,4,1,5,2:T(1,128)S(1)} fusion(f32[3,2,2,32,2,128]{3,0,4,1,5,2:T(4,128)S(1)} %fusion.4), kind=kLoop, calls=%fused_computation.29 | loop fusion | flops 65536 | bytes 524288 | tf_op jit(solution)/shard_map/add | solution.py:87
  9.9 0.4 copy.112
  10.4 0.2 add.27
  10.5 0.1 copy.113
  10.7 0.0 copy-done.5
  10.7 0.1 dynamic-slice_bitcast_fusion
  10.8 0.1 maximum_bitcast_fusion.2
  10.9 0.8 %copy.114 = f32[256,1,144]{2,1,0:T(1,128)} copy(f32[256,1,144]{0,2,1:T(8,128)S(1)} %maximum_bitcast_fusion.2) | data formatting | bytes 294912 | tf_op jit(solution)/shard_map/all_to_all | solution.py:127
  11.7 15.6 %all-to-all-start = ((f32[256,1,144]{2,1,0:T(1,128)}), f32[256,1,144]{2,1,0:T(1,128)S(1)}, u32[]{:S(2)}, u32[]{:S(2)}) async-start(f32[256,1,144]{2,1,0:T(1,128)} %copy.114), calls=%async_computation | async-start | bytes 524288 | tf_op jit(solution)/shard_map/all_to_all | solution.py:127
  27.4 0.0 copy-done.6
  27.4 0.0 copy-start.3
  27.4 0.0 copy-start.4
  27.4 15.2 %all-to-all-done = f32[256,1,144]{2,1,0:T(1,128)S(1)} async-done(((f32[256,1,144]{2,1,0:T(1,128)}), f32[256,1,144]{2,1,0:T(1,128)S(1)}, u32[]{:S(2)}, u32[]{:S(2)}) %all-to-all-start) | async-done | bytes 147488 | tf_op jit(solution)/shard_map/all_to_all | solution.py:127
  42.7 0.6 reduce
  43.3 0.1 reshape.257
  43.4 0.1 copy.135
  43.5 0.1 copy.116
  43.6 0.1 reshape.258
  43.8 0.1 copy.117
  43.8 0.1 fusion.69
  43.9 0.0 copy-done.3
  43.9 0.0 copy-done.4
  44.0 0.1 select_reduce_fusion.1
  44.1 0.8 %convolution_bitcast_fusion = f32[64,8,64]{2,0,1:T(8,128)S(1)} fusion(f32[1,64,8,64]{3,1,0,2:T(8,128)S(1)} %get-tuple-element.28, f32[1,64,8,64]{3,1,0,2:T(8,128)S(1)} %get-tuple-element.27, f32[1,64,8,64]{3,1,0,2:T(8,128)S(1)} %get-tuple-element.26, f32[1,64,8,64]{3,1,0,2:T(8,128)S(1)} %get-tuple-element.25, f32[64,1,64]{2,0,1:T(8,128)S(1)} %get-tuple-element.48, ...), kind=kOutput, calls=%fused_computation.5 | convolution fusion | flops 101122048 | bytes 720896 | tf_op jit(solution)/shard_map/kdj,djec->kec/dot_general | solution.py:110
  44.9 0.2 copy.121
  45.1 0.3 reshape.267
  45.4 18.0 %all_to_all.14 = f32[256,1,128]{2,1,0:T(1,128)S(1)} all-to-all(f32[256,1,128]{2,1,0:T(1,128)S(1)} %reshape.267), channel_id=1, replica_groups=mesh['mom'=64,'en'=4] {'mom','en'}, dimensions={0} | all-to-all | bytes 262144 | tf_op jit(solution)/shard_map/all_to_all | solution.py:135
  63.4 0.5 broadcast.102
  63.9 0.9 %reduce.1 = f32[256,128]{1,0:T(8,128)S(1)} reduce(f32[256,1,128]{2,1,0:T(1,128)S(1)} %all_to_all.14, f32[]{:T(128)} %broadcast.102), dimensions={1}, to_apply=%all_to_all.11.reduce_sub_computation | reduce | bytes 262148 | tf_op jit(solution)/shard_map/all_to_all | solution.py:135
  64.8 0.2 reshape.268
  65.1 0.8 %broadcast_in_dim_reshape.3 = f32[1,2,64,2,128]{4,3,2,1,0:T(2,128)} reshape(f32[2,256,64]{2,1,0:T(8,128)S(1)} %copy.122) | data formatting | bytes 262144 | tf_op jit(solution)/shard_map/broadcast_in_dim;reshape | solution.py:137
  (38 shorter events, 0.7 us)
Async XLA Ops:
  0.0 1.2 %copy-start.2 = (f32[1,2,2,128]{3,2,1,0:T(2,128)S(1)}, f32[1,2,2,128]{3,2,1,0:T(2,128)}, u32[]{:S(2)}) copy-start(f32[1,2,2,128]{3,2,1,0:T(2,128)} %param.10) | copy-start | bytes 6148
  0.0 1.3 %copy-start = (f32[1,2,2,128,128]{4,3,2,1,0:T(8,128)S(1)}, f32[1,2,2,128,128]{4,3,2,1,0:T(8,128)}, u32[]{:S(2)}) copy-start(f32[1,2,2,128,128]{4,3,2,1,0:T(8,128)} %param.9) | copy-start | bytes 786436
  4.0 0.8 %copy-start.1 = (s32[2,128,32]{1,2,0:T(8,128)S(1)}, s32[2,128,32]{1,2,0:T(8,128)}, u32[]{:S(2)}) copy-start(s32[2,128,32]{1,2,0:T(8,128)} %param.11) | copy-start | bytes 98308
  9.1 1.6 %copy-start.5 = (s32[1,64]{1,0:T(1,128)S(1)}, s32[1,64]{1,0:T(1,128)}, u32[]{:S(2)}) copy-start(s32[1,64]{1,0:T(1,128)} %param.13) | copy-start | bytes 772
  9.1 18.3 %copy-start.6 = (s32[6]{0:T(128)S(1)}, s32[6]{0:T(128)}, u32[]{:S(2)}) copy-start(s32[6]{0:T(128)} %param.12) | copy-start | bytes 76
  11.7 30.9 %all-to-all-start = ((f32[256,1,144]{2,1,0:T(1,128)}), f32[256,1,144]{2,1,0:T(1,128)S(1)}, u32[]{:S(2)}, u32[]{:S(2)}) async-start(f32[256,1,144]{2,1,0:T(1,128)} %copy.114), calls=%async_computation | async-start | bytes 524288 | tf_op jit(solution)/shard_map/all_to_all | solution.py:127
  27.4 16.6 %copy-start.3 = (f32[6]{0:T(128)S(1)}, f32[6]{0:T(128)}, u32[]{:S(2)}) copy-start(f32[6]{0:T(128)} %param.14) | copy-start | bytes 76
  27.4 16.6 %copy-start.4 = (f32[6]{0:T(128)S(1)}, f32[6]{0:T(128)}, u32[]{:S(2)}) copy-start(f32[6]{0:T(128)} %param.15) | copy-start | bytes 76

commit v10 on v9

--- a/solution.py
+++ b/solution.py
@@ -9,6 +9,7 @@
 
 HIGH = lax.Precision.HIGHEST
 CHAIN = lax.Precision.HIGH
+PIECES = 2
 
 
 def with_halo(x, sides, width):
@@ -75,7 +76,7 @@
     stacked = jnp.stack(collected, axis=1)
     pieces = []
     rest = stacked
-    for _ in range(3):
+    for _ in range(PIECES):
         piece = lax.reduce_precision(rest, exponent_bits=8, mantissa_bits=7)
         pieces.append(piece.astype(jnp.bfloat16))
         rest = rest - piece
@@ -84,7 +85,7 @@
     picked = jnp.einsum(
         "qesxoc,sojc->qesjxo", jnp.stack(pieces), selector, preferred_element_type=jnp.float32
     )
-    picked = picked[0] + picked[1] + picked[2]
+    picked = jnp.sum(picked, axis=0)
     return picked.reshape(picked.shape[0], -1, picked.shape[3], picked.shape[4])
 
 

time: 66.1 us -> 68.4 us (1.035)
  local copies, waits for them, and re-layouts: 5.91 us -> 8.63 us
  other arithmetic: 3.21 us -> 2.28 us
    unnamed x23, local copies, waits for them, and re-layouts: 2.04 us -> 4.91 us
    add x1 -> x0, other arithmetic: 0.81 us -> none  [slab_pairs(): picked = picked[0] + picked[1] + picked[2]]
where the time goes in v10:
time: 68.4 us; the launch traced here: 68.1 us
  blocking collectives  18 us (26%)
  starting transfers between devices  15.6 us (23%)
  waiting for transfers between devices  15.3 us (22%)
  local copies, waits for them, and re-layouts  8.63 us (13%)
  matrix products  7.79 us (11%)
  other arithmetic  2.28 us (3%)
    all_to_all x1, blocking collectives, shards(): back = lax.all_to_all(mixed, ('mom', 'en'), 0, 0)  18 us
    all_to_all x1, starting transfers between devices, shards(): lax.all_to_all(jnp.concatenate([blocks, rows], axis=1), ('mom', 'en'), 0, 0)  15.6 us
    all_to_all x1, waiting for transfers between devices, shards(): lax.all_to_all(jnp.concatenate([blocks, rows], axis=1), ('mom', 'en'), 0, 0)  15.3 us
    unnamed x23, local copies, waits for them, and re-layouts  4.91 us
    dot_general x1, matrix products, slab_pairs(): jnp.einsum('qesxoc,sojc->qesjxo', jnp.stack(pieces), selector, preferred_...  4.07 us
    dot_general x7, matrix products, cmul(): jnp.einsum(spec, block(left), column(right, adjoint), precision=CHAIN)  2.91 us
  transfers between devices with their start and end apart: 1, of which 1 were waited for; matrix products, arithmetic and copies ran while one was open for 0% of the time, Pallas kernels for 0%

profile of v10, /device:TPU:1, one launch (start us, length us, event | category | flops | bytes accessed | tf_op | source)
XLA Modules:
  0.0 68.1 jit_solution(9368962175199869908)
XLA Ops:
  0.0 1.1 %copy.145 = f32[1,2,2,2,128,128]{5,4,1,3,2,0:T(8,128)S(1)} copy(f32[1,2,2,2,128,128]{5,4,3,2,1,0:T(8,128)} %param.8) | data formatting | bytes 1048576 | tf_op args[0]
  1.1 0.0 copy-start.2
  1.1 0.6 copy-done.2
  1.8 0.0 copy-start
  1.9 0.9 %copy-done = f32[1,2,2,128,128]{4,3,2,1,0:T(8,128)S(1)} copy-done((f32[1,2,2,128,128]{4,3,2,1,0:T(8,128)S(1)}, f32[1,2,2,128,128]{4,3,2,1,0:T(8,128)}, u32[]{:S(2)}) %copy-start) | copy-done | bytes 262168
  2.8 0.4 fusion.24
  3.3 0.4 fusion.40
  3.9 0.6 fusion.7
  4.6 0.4 fusion.32
  5.0 0.4 fusion.44
  5.6 0.4 fusion.52
  6.0 0.0 copy-start.1
  6.0 0.7 %copy-done.1 = s32[2,128,32]{1,2,0:T(8,128)S(1)} copy-done((s32[2,128,32]{1,2,0:T(8,128)S(1)}, s32[2,128,32]{1,2,0:T(8,128)}, u32[]{:S(2)}) %copy-start.1) | copy-done | bytes 32792
  6.7 0.1 copy.98
  6.8 0.4 fusion.60
  7.2 0.1 reduce-precision_convert_fusion
  7.3 0.1 pad_maximum_fusion.1
  7.4 4.1 %fusion.4 = f32[2,128,32,2,2]{2,4,3,1,0:T(2,128)S(1)} fusion(s32[2,128,32]{2,1,0:T(8,128)S(1)} %copy.98, bf16[2,2,2,2,128,128]{5,4,3,2,1,0:T(8,128)(2,1)S(1)} %pad_maximum_fusion.1), kind=kOutput, calls=%fused_computation.4 | convolution fusion | flops 17858560 | bytes 688128 | tf_op jit(solution)/shard_map/qesxoc,sojc->qesjxo/dot_general | solution.py:85
  11.5 0.3 copy.111
  11.7 0.0 copy-start.5
  11.7 0.2 reshape_reshape_reshape.3
  11.9 0.1 copy.112
  12.1 0.3 copy-done.5
  12.4 0.1 dynamic-slice_bitcast_fusion
  12.5 0.1 maximum_bitcast_fusion.2
  12.6 0.0 copy-start.6
  12.6 0.8 %copy.113 = f32[256,1,144]{2,1,0:T(1,128)} copy(f32[256,1,144]{0,2,1:T(8,128)S(1)} %maximum_bitcast_fusion.2) | data formatting | bytes 294912 | tf_op jit(solution)/shard_map/all_to_all | solution.py:128
  13.4 15.6 %all-to-all-start = ((f32[256,1,144]{2,1,0:T(1,128)}), f32[256,1,144]{2,1,0:T(1,128)S(1)}, u32[]{:S(2)}, u32[]{:S(2)}) async-start(f32[256,1,144]{2,1,0:T(1,128)} %copy.113), calls=%async_computation | async-start | bytes 524288 | tf_op jit(solution)/shard_map/all_to_all | solution.py:128
  29.1 0.0 copy-done.6
  29.1 15.3 %all-to-all-done = f32[256,1,144]{2,1,0:T(1,128)S(1)} async-done(((f32[256,1,144]{2,1,0:T(1,128)}), f32[256,1,144]{2,1,0:T(1,128)S(1)}, u32[]{:S(2)}, u32[]{:S(2)}) %all-to-all-start) | async-done | bytes 147488 | tf_op jit(solution)/shard_map/all_to_all | solution.py:128
  44.4 0.6 reduce.1
  45.0 0.1 reshape.215
  45.1 0.1 copy.134
  45.2 0.1 copy.115
  45.3 0.1 reshape.216
  45.5 0.1 copy.116
  45.5 0.0 copy-start.3
  45.5 0.0 copy-start.4
  45.5 0.1 fusion.69
  45.7 0.5 copy-done.3
  46.2 0.0 copy-done.4
  46.2 0.1 select_reduce_fusion.1
  46.4 0.8 %convolution_bitcast_fusion = f32[64,8,64]{2,0,1:T(8,128)S(1)} fusion(f32[1,64,8,64]{3,1,0,2:T(8,128)S(1)} %get-tuple-element.27, f32[1,64,8,64]{3,1,0,2:T(8,128)S(1)} %get-tuple-element.26, f32[1,64,8,64]{3,1,0,2:T(8,128)S(1)} %get-tuple-element.25, f32[1,64,8,64]{3,1,0,2:T(8,128)S(1)} %get-tuple-element.24, f32[64,1,64]{2,0,1:T(8,128)S(1)} %get-tuple-element.47, ...), kind=kOutput, calls=%fused_computation.5 | convolution fusion | flops 101122048 | bytes 720896 | tf_op jit(solution)/shard_map/kdj,djec->kec/dot_general | solution.py:111
  47.2 0.2 copy.120
  47.3 0.3 reshape.225
  47.6 18.0 %all_to_all.14 = f32[256,1,128]{2,1,0:T(1,128)S(1)} all-to-all(f32[256,1,128]{2,1,0:T(1,128)S(1)} %reshape.225), channel_id=1, replica_groups=mesh['mom'=64,'en'=4] {'mom','en'}, dimensions={0} | all-to-all | bytes 262144 | tf_op jit(solution)/shard_map/all_to_all | solution.py:136
  65.6 0.5 broadcast.102
  66.1 0.9 %reduce.2 = f32[256,128]{1,0:T(8,128)S(1)} reduce(f32[256,1,128]{2,1,0:T(1,128)S(1)} %all_to_all.14, f32[]{:T(128)} %broadcast.102), dimensions={1}, to_apply=%all_to_all.11.reduce_sub_computation | reduce | bytes 262148 | tf_op jit(solution)/shard_map/all_to_all | solution.py:136
  67.1 0.2 reshape.226
  67.3 0.8 %broadcast_in_dim_reshape.3 = f32[1,2,64,2,128]{4,3,2,1,0:T(2,128)} reshape(f32[2,256,64]{2,1,0:T(8,128)S(1)} %copy.121) | data formatting | bytes 262144 | tf_op jit(solution)/shard_map/broadcast_in_dim;reshape | solution.py:138
  (38 shorter events, 0.7 us)
Async XLA Ops:
  1.1 0.7 %copy-start.2 = (f32[1,2,2,128]{3,2,1,0:T(2,128)S(1)}, f32[1,2,2,128]{3,2,1,0:T(2,128)}, u32[]{:S(2)}) copy-start(f32[1,2,2,128]{3,2,1,0:T(2,128)} %param.10) | copy-start | bytes 6148
  1.8 1.0 %copy-start = (f32[1,2,2,128,128]{4,3,2,1,0:T(8,128)S(1)}, f32[1,2,2,128,128]{4,3,2,1,0:T(8,128)}, u32[]{:S(2)}) copy-start(f32[1,2,2,128,128]{4,3,2,1,0:T(8,128)} %param.9) | copy-start | bytes 786436
  6.0 0.8 %copy-start.1 = (s32[2,128,32]{1,2,0:T(8,128)S(1)}, s32[2,128,32]{1,2,0:T(8,128)}, u32[]{:S(2)}) copy-start(s32[2,128,32]{1,2,0:T(8,128)} %param.11) | copy-start | bytes 98308
  11.7 0.7 copy-start.5
  12.6 16.5 %copy-start.6 = (s32[6]{0:T(128)S(1)}, s32[6]{0:T(128)}, u32[]{:S(2)}) copy-start(s32[6]{0:T(128)} %param.12) | copy-start | bytes 76
  13.4 30.9 %all-to-all-start = ((f32[256,1,144]{2,1,0:T(1,128)}), f32[256,1,144]{2,1,0:T(1,128)S(1)}, u32[]{:S(2)}, u32[]{:S(2)}) async-start(f32[256,1,144]{2,1,0:T(1,128)} %copy.113), calls=%async_computation | async-start | bytes 524288 | tf_op jit(solution)/shard_map/all_to_all | solution.py:128
  45.5 0.7 copy-start.3
  45.5 0.7 copy-start.4

commit v11 on v9

--- a/solution.py
+++ b/solution.py
@@ -72,19 +72,11 @@
         retarded = inverse + inner
         lesser = cmul(cmul(retarded, middle), retarded, adjoint=True)
         collected.append(lesser)
-    stacked = jnp.stack(collected, axis=1)
-    pieces = []
-    rest = stacked
-    for _ in range(3):
-        piece = lax.reduce_precision(rest, exponent_bits=8, mantissa_bits=7)
-        pieces.append(piece.astype(jnp.bfloat16))
-        rest = rest - piece
+    stacked = jnp.swapaxes(jnp.stack(collected, axis=1), -1, -2)
     columns = jnp.arange(orbitals, dtype=jnp.int32)
-    selector = (neighbors[..., None] == columns).astype(jnp.bfloat16)
-    picked = jnp.einsum(
-        "qesxoc,sojc->qesjxo", jnp.stack(pieces), selector, preferred_element_type=jnp.float32
-    )
-    picked = picked[0] + picked[1] + picked[2]
+    chosen = jnp.swapaxes(neighbors, 1, 2)[:, :, None, :] == columns[:, None]
+    picked = jnp.where(chosen[None, :, :, None], stacked[:, :, None], 0.0)
+    picked = jnp.sum(picked, axis=4)
     return picked.reshape(picked.shape[0], -1, picked.shape[3], picked.shape[4])
 
 

time: 66.1 us -> 66.4 us (level)
  matrix products: 7.27 us -> 3.71 us
  other arithmetic: 3.21 us -> 6.07 us
  local copies, waits for them, and re-layouts: 5.91 us -> 6.94 us
    dot_general x1 -> x0, matrix products: 3.57 us -> none  [slab_pairs(): jnp.einsum('qesxoc,sojc->qesjxo', jnp.stack(pieces), selector, preferred_...]
    reduce_sum x0 -> x1, other arithmetic: none -> 3.19 us  [slab_pairs(): picked = jnp.sum(picked, axis=4)]
    unnamed x23 -> x22, local copies, waits for them, and re-layouts: 2.04 us -> 3.32 us
    add x1 -> x0, other arithmetic: 0.81 us -> none  [slab_pairs(): picked = picked[0] + picked[1] + picked[2]]
    eq x0 -> x1, other arithmetic: none -> 0.71 us  [slab_pairs(): chosen = jnp.swapaxes(neighbors, 1, 2)[:, :, None, :] == columns[:, None]]
where the time goes in v11:
time: 66.4 us; the launch traced here: 66.2 us
  blocking collectives  18 us (27%)
  starting transfers between devices  15.7 us (24%)
  waiting for transfers between devices  15.3 us (23%)
  local copies, waits for them, and re-layouts  6.94 us (10%)
  other arithmetic  6.07 us (9%)
  matrix products  3.71 us (6%)
    all_to_all x1, blocking collectives, shards(): back = lax.all_to_all(mixed, ('mom', 'en'), 0, 0)  18 us
    all_to_all x1, starting transfers between devices, shards(): lax.all_to_all(jnp.concatenate([blocks, rows], axis=1), ('mom', 'en'), 0, 0)  15.7 us
    all_to_all x1, waiting for transfers between devices, shards(): lax.all_to_all(jnp.concatenate([blocks, rows], axis=1), ('mom', 'en'), 0, 0)  15.3 us
    unnamed x22, local copies, waits for them, and re-layouts  3.32 us
    reduce_sum x1, other arithmetic, slab_pairs(): picked = jnp.sum(picked, axis=4)  3.19 us
    dot_general x7, matrix products, cmul(): jnp.einsum(spec, block(left), column(right, adjoint), precision=CHAIN)  2.9 us
  transfers between devices with their start and end apart: 1, of which 1 were waited for; matrix products, arithmetic and copies ran while one was open for 0% of the time, Pallas kernels for 0%

profile of v11, /device:TPU:1, one launch (start us, length us, event | category | flops | bytes accessed | tf_op | source)
XLA Modules:
  0.0 66.2 jit_solution(18292174952635337936)
XLA Ops:
  0.0 0.0 copy-start.2
  0.0 1.1 %copy.130 = f32[1,2,2,2,128,128]{5,4,1,3,2,0:T(8,128)S(1)} copy(f32[1,2,2,2,128,128]{5,4,3,2,1,0:T(8,128)} %param.8) | data formatting | bytes 1048576 | tf_op args[0]
  1.1 0.0 copy-start
  1.2 0.0 copy-done.2
  1.3 0.8 %copy-done = f32[1,2,2,128,128]{4,3,2,1,0:T(8,128)S(1)} copy-done((f32[1,2,2,128,128]{4,3,2,1,0:T(8,128)S(1)}, f32[1,2,2,128,128]{4,3,2,1,0:T(8,128)}, u32[]{:S(2)}) %copy-start) | copy-done | bytes 262168
  2.1 0.4 fusion.15
  2.6 0.4 fusion.31
  3.2 0.6 fusion
  3.8 0.4 fusion.23
  4.3 0.4 fusion.35
  4.9 0.4 fusion.43
  5.3 0.4 fusion.51
  5.7 0.0 copy-start.1
  5.7 0.1 maximum_bitcast_fusion
  5.8 0.2 copy.99
  6.0 0.5 copy-done.1
  6.4 0.7 %iota_compare_fusion = pred[2,32,128,128]{3,2,1,0:T(8,128)(4,1)S(1)} fusion(s32[2,32,128]{2,1,0:T(8,128)S(1)} %bitcast.176), kind=kLoop, calls=%fused_computation.1 | loop fusion | flops 1048576 | bytes 1081344 | tf_op jit(solution)/shard_map/eq | solution.py:77
  7.2 0.0 copy-start.5
  7.2 3.2 %select_reduce_fusion = f32[2,2,32,2,128]{4,3,2,1,0:T(2,128)S(1)} fusion(f32[2,2,2,128,128]{4,3,2,1,0:T(8,128)S(1)} %copy.99, pred[2,32,128,128]{3,2,1,0:T(8,128)(4,1)S(1)} %iota_compare_fusion), kind=kLoop, calls=%fused_computation | loop fusion | flops 8355840 | bytes 1703936 | tf_op jit(solution)/shard_map/reduce_sum | solution.py:79
  10.4 0.0 copy-start.6
  10.4 0.2 reshape_reshape_reshape.3
  10.6 0.1 copy.100
  10.7 0.0 copy-done.5
  10.7 0.1 dynamic-slice_bitcast_fusion
  10.8 0.1 maximum_bitcast_fusion.3
  10.9 0.8 %copy.101 = f32[256,1,144]{2,1,0:T(1,128)} copy(f32[256,1,144]{0,2,1:T(8,128)S(1)} %maximum_bitcast_fusion.3) | data formatting | bytes 294912 | tf_op jit(solution)/shard_map/all_to_all | solution.py:119
  11.7 15.7 %all-to-all-start = ((f32[256,1,144]{2,1,0:T(1,128)}), f32[256,1,144]{2,1,0:T(1,128)S(1)}, u32[]{:S(2)}, u32[]{:S(2)}) async-start(f32[256,1,144]{2,1,0:T(1,128)} %copy.101), calls=%async_computation | async-start | bytes 524288 | tf_op jit(solution)/shard_map/all_to_all | solution.py:119
  27.4 0.0 copy-done.6
  27.4 15.3 %all-to-all-done = f32[256,1,144]{2,1,0:T(1,128)S(1)} async-done(((f32[256,1,144]{2,1,0:T(1,128)}), f32[256,1,144]{2,1,0:T(1,128)S(1)}, u32[]{:S(2)}, u32[]{:S(2)}) %all-to-all-start) | async-done | bytes 147488 | tf_op jit(solution)/shard_map/all_to_all | solution.py:119
  42.7 0.6 reduce
  43.3 0.1 reshape.137
  43.4 0.1 reshape.138
  43.6 0.0 copy-start.3
  43.6 0.0 copy-start.4
  43.6 0.1 copy.104
  43.7 0.1 fusion.59
  43.8 0.1 copy.121
  43.9 0.1 copy.103
  44.0 0.3 copy-done.3
  44.2 0.0 copy-done.4
  44.3 0.1 select_reduce_fusion.2
  44.4 0.8 %convolution_bitcast_fusion = f32[64,8,64]{2,0,1:T(8,128)S(1)} fusion(f32[1,64,8,64]{3,1,0,2:T(8,128)S(1)} %get-tuple-element.25, f32[1,64,8,64]{3,1,0,2:T(8,128)S(1)} %get-tuple-element.24, f32[1,64,8,64]{3,1,0,2:T(8,128)S(1)} %get-tuple-element.23, f32[1,64,8,64]{3,1,0,2:T(8,128)S(1)} %get-tuple-element.22, f32[64,1,64]{2,0,1:T(8,128)S(1)} %get-tuple-element.45, ...), kind=kOutput, calls=%fused_computation.2 | convolution fusion | flops 101122048 | bytes 720896 | tf_op jit(solution)/shard_map/kdj,djec->kec/dot_general | solution.py:102
  45.2 0.2 copy.108
  45.4 0.3 reshape.146
  45.7 18.0 %all_to_all.14 = f32[256,1,128]{2,1,0:T(1,128)S(1)} all-to-all(f32[256,1,128]{2,1,0:T(1,128)S(1)} %reshape.146), channel_id=1, replica_groups=mesh['mom'=64,'en'=4] {'mom','en'}, dimensions={0} | all-to-all | bytes 262144 | tf_op jit(solution)/shard_map/all_to_all | solution.py:127
  63.7 0.5 broadcast.108
  64.2 0.9 %reduce.1 = f32[256,128]{1,0:T(8,128)S(1)} reduce(f32[256,1,128]{2,1,0:T(1,128)S(1)} %all_to_all.14, f32[]{:T(128)} %broadcast.108), dimensions={1}, to_apply=%all_to_all.11.reduce_sub_computation | reduce | bytes 262148 | tf_op jit(solution)/shard_map/all_to_all | solution.py:127
  65.1 0.2 reshape.147
  65.4 0.8 %broadcast_in_dim_reshape.3 = f32[1,2,64,2,128]{4,3,2,1,0:T(2,128)} reshape(f32[2,256,64]{2,1,0:T(8,128)S(1)} %copy.109) | data formatting | bytes 262144 | tf_op jit(solution)/shard_map/broadcast_in_dim;reshape | solution.py:129
  (38 shorter events, 0.7 us)
Async XLA Ops:
  0.0 1.2 %copy-start.2 = (f32[1,2,2,128]{3,2,1,0:T(2,128)S(1)}, f32[1,2,2,128]{3,2,1,0:T(2,128)}, u32[]{:S(2)}) copy-start(f32[1,2,2,128]{3,2,1,0:T(2,128)} %param.10) | copy-start | bytes 6148
  1.1 1.0 %copy-start = (f32[1,2,2,128,128]{4,3,2,1,0:T(8,128)S(1)}, f32[1,2,2,128,128]{4,3,2,1,0:T(8,128)}, u32[]{:S(2)}) copy-start(f32[1,2,2,128,128]{4,3,2,1,0:T(8,128)} %param.9) | copy-start | bytes 786436
  5.7 0.8 %copy-start.1 = (s32[2,128,32]{1,2,0:T(8,128)S(1)}, s32[2,128,32]{1,2,0:T(8,128)}, u32[]{:S(2)}) copy-start(s32[2,128,32]{1,2,0:T(8,128)} %param.11) | copy-start | bytes 98308
  7.2 3.5 %copy-start.5 = (s32[1,64]{1,0:T(1,128)S(1)}, s32[1,64]{1,0:T(1,128)}, u32[]{:S(2)}) copy-start(s32[1,64]{1,0:T(1,128)} %param.13) | copy-start | bytes 772
  10.4 17.0 %copy-start.6 = (s32[6]{0:T(128)S(1)}, s32[6]{0:T(128)}, u32[]{:S(2)}) copy-start(s32[6]{0:T(128)} %param.12) | copy-start | bytes 76
  11.7 30.9 %all-to-all-start = ((f32[256,1,144]{2,1,0:T(1,128)}), f32[256,1,144]{2,1,0:T(1,128)S(1)}, u32[]{:S(2)}, u32[]{:S(2)}) async-start(f32[256,1,144]{2,1,0:T(1,128)} %copy.101), calls=%async_computation | async-start | bytes 524288 | tf_op jit(solution)/shard_map/all_to_all | solution.py:119
  43.6 0.7 copy-start.3
  43.6 0.7 %copy-start.4 = (f32[6]{0:T(128)S(1)}, f32[6]{0:T(128)}, u32[]{:S(2)}) copy-start(f32[6]{0:T(128)} %param.15) | copy-start | bytes 76

commit v12 on v9

--- a/solution.py
+++ b/solution.py
@@ -116,23 +116,26 @@
     pairs = slab_pairs(slab_inverse[0], coupling[0], injection[0], neighbors)
     local = pairs.shape[0]
     moms, groups = lax.axis_size("mom"), lax.axis_size("en")
-    devices = moms * groups
     flat = pairs.reshape(local, -1)
-    width = flat.shape[1] // devices
-    blocks = jnp.swapaxes(flat.reshape(local, devices, width), 0, 1).reshape(devices, -1)
-    share = -(-moms // groups)
-    ids = jnp.pad(mode_table[0].astype(jnp.float32), (0, share * groups - moms))
-    mine = lax.dynamic_slice_in_dim(ids, lax.axis_index("en") * share, share)
-    rows = jnp.broadcast_to(mine[None], (devices, share))
-    sent = lax.all_to_all(jnp.concatenate([blocks, rows], axis=1), ("mom", "en"), 0, 0)
-    sent = sent.reshape(moms, groups, -1)
-    data = sent[:, :, : local * width].reshape(moms, groups * local, width)
-    data = jnp.pad(data, ((0, 0), (SHIFT_MAX, SHIFT_MAX), (0, 0)))
-    table = sent[:, :, local * width :].reshape(moms, -1)[:, :moms].astype(jnp.int32)
+    width = flat.shape[1] // moms
+    blocks = jnp.swapaxes(flat.reshape(local, moms, width), 0, 1).reshape(moms, -1)
+    ids = jnp.broadcast_to(mode_table[0].astype(jnp.float32)[None], (moms, moms))
+    sent = lax.all_to_all(jnp.concatenate([blocks, ids], axis=1), "mom", 0, 0)
+    data = sent[:, : local * width].reshape(moms, local, width)
+    table = sent[:, local * width :].astype(jnp.int32)
     weights = shift_weights(table, mode_shift, emit_weight, absorb_weight)
-    mixed = mix(data, weights, groups * local)
-    mixed = mixed.reshape(devices, local, width)
-    back = lax.all_to_all(mixed, ("mom", "en"), 0, 0)
+    reach = local + 2 * SHIFT_MAX
+    data = jnp.pad(data, ((0, 0), (2 * SHIFT_MAX, 2 * SHIFT_MAX), (0, 0)))
+    windows = jnp.stack(
+        [data[:, SHIFT_MAX + offset : SHIFT_MAX + offset + reach] for offset in OFFSETS]
+    )
+    part = jnp.einsum("kdj,djec->kec", weights, windows, precision=HIGH)
+    down = [(i, i - 1) for i in range(1, groups)]
+    up = [(i, i + 1) for i in range(groups - 1)]
+    from_up = lax.ppermute(part[:, :SHIFT_MAX], "en", down)
+    from_down = lax.ppermute(part[:, SHIFT_MAX + local :], "en", up)
+    own = part[:, SHIFT_MAX : SHIFT_MAX + local] + from_up + from_down
+    back = lax.all_to_all(own, "mom", 0, 0)
     result = jnp.swapaxes(back, 0, 1).reshape(pairs.shape)
     return result[None]
 

time: 66.1 us -> 62.8 us (0.950)
  starting transfers between devices: 15.6 us -> 18.3 us
  blocking collectives: 18 us -> 16.1 us
  other arithmetic: 3.21 us -> 1.59 us
  local copies, waits for them, and re-layouts: 5.91 us -> 4.32 us
  waiting for transfers between devices: 15.2 us -> 13.8 us
    ppermute x0 -> x2, starting transfers between devices: none -> 5.29 us  [the longest x1 3.99 us: shards(): from_down = lax.ppermute(part[:, SHIFT_MAX + local:], 'en', up)]
    all_to_all x1, waiting for transfers between devices: 15.2 us -> 11.6 us  [shards(): sent = lax.all_to_all(jnp.concatenate([blocks, ids], axis=1), 'mom', 0, 0)]
    all_to_all x1, starting transfers between devices: 15.6 us -> 13 us  [shards(): sent = lax.all_to_all(jnp.concatenate([blocks, ids], axis=1), 'mom', 0, 0)]
    ppermute x0 -> x2, waiting for transfers between devices: none -> 2.16 us  [the longest x1 1.25 us: shards(): from_up = lax.ppermute(part[:, :SHIFT_MAX], 'en', down)]
    all_to_all x1, blocking collectives: 18 us -> 16.1 us  [shards(): back = lax.all_to_all(own, 'mom', 0, 0)]
    all_to_all x3 -> x1, other arithmetic: 1.66 us -> 0.01 us  [shards(): sent = lax.all_to_all(jnp.concatenate([blocks, ids], axis=1), 'mom', 0, 0)]
    all_to_all x2 -> x1, local copies, waits for them, and re-layouts: 1.35 us -> 0.83 us  [shards(): sent = lax.all_to_all(jnp.concatenate([blocks, ids], axis=1), 'mom', 0, 0)]
    unnamed x23 -> x21, local copies, waits for them, and re-layouts: 2.04 us -> 1.57 us
  transfers between devices with their start and end apart: 1 -> 3, of which waited for: 1 -> 3; matrix products, arithmetic and copies ran while one was open for 0% -> 0% of each run, Pallas kernels for 0% -> 0%
where the time goes in v12:
time: 62.8 us; the launch traced here: 62.1 us
  starting transfers between devices  18.3 us (29%)
  blocking collectives  16.1 us (26%)
  waiting for transfers between devices  13.8 us (22%)
  matrix products  7.56 us (12%)
  local copies, waits for them, and re-layouts  4.32 us (7%)
  other arithmetic  1.59 us (3%)
    all_to_all x1, blocking collectives, shards(): back = lax.all_to_all(own, 'mom', 0, 0)  16.1 us
    all_to_all x1, starting transfers between devices, shards(): sent = lax.all_to_all(jnp.concatenate([blocks, ids], axis=1), 'mom', 0, 0)  13 us
    all_to_all x1, waiting for transfers between devices, shards(): sent = lax.all_to_all(jnp.concatenate([blocks, ids], axis=1), 'mom', 0, 0)  11.6 us
    ppermute x1, starting transfers between devices, shards(): from_down = lax.ppermute(part[:, SHIFT_MAX + local:], 'en', up)  3.99 us
    dot_general x1, matrix products, slab_pairs(): jnp.einsum('qesxoc,sojc->qesjxo', jnp.stack(pieces), selector, preferred_...  3.57 us
    dot_general x7, matrix products, cmul(): jnp.einsum(spec, block(left), column(right, adjoint), precision=CHAIN)  2.89 us
    unnamed x21, local copies, waits for them, and re-layouts  1.57 us
    ppermute x1, starting transfers between devices, shards(): from_up = lax.ppermute(part[:, :SHIFT_MAX], 'en', down)  1.29 us
  transfers between devices with their start and end apart: 3, of which 3 were waited for; matrix products, arithmetic and copies ran while one was open for 0% of the time, Pallas kernels for 0%

profile of v12, /device:TPU:1, one launch (start us, length us, event | category | flops | bytes accessed | tf_op | source)
XLA Modules:
  0.0 62.1 jit_solution(1298835077604665149)
XLA Ops:
  0.0 0.0 copy-start.2
  0.0 0.0 copy-start
  0.0 1.1 %copy.138 = f32[1,2,2,2,128,128]{5,4,1,3,2,0:T(8,128)S(1)} copy(f32[1,2,2,2,128,128]{5,4,3,2,1,0:T(8,128)} %param.8) | data formatting | bytes 1048576 | tf_op args[0]
  1.2 0.0 copy-done.2
  1.3 0.0 copy-done
  1.4 0.4 fusion.29
  1.8 0.4 fusion.45
  2.4 0.6 fusion.18
  3.1 0.4 fusion.37
  3.5 0.4 fusion.49
  4.0 0.0 copy-start.1
  4.1 0.4 fusion.57
  4.5 0.2 copy-done.1
  4.8 0.1 copy.90
  4.9 0.4 fusion.65
  5.3 0.2 reduce-precision_convert_fusion.1
  5.4 0.1 pad_maximum_fusion
  5.5 3.6 %fusion.4 = f32[3,2,2,32,2,128]{3,0,4,1,5,2:T(4,128)S(1)} fusion(s32[2,128,32]{2,1,0:T(8,128)S(1)} %copy.90, bf16[3,2,2,2,128,128]{5,4,3,2,1,0:T(8,128)(2,1)S(1)} %pad_maximum_fusion), kind=kOutput, calls=%fused_computation.4 | convolution fusion | flops 26214400 | bytes 1212416 | tf_op jit(solution)/shard_map/qesxoc,sojc->qesjxo/dot_general | solution.py:84
  9.1 0.0 copy-start.5
  9.1 0.8 %slice_add_fusion = f32[1,2,2,32,2,128]{3,0,4,1,5,2:T(1,128)S(1)} fusion(f32[3,2,2,32,2,128]{3,0,4,1,5,2:T(4,128)S(1)} %fusion.4), kind=kLoop, calls=%fused_computation.34 | loop fusion | flops 65536 | bytes 524288 | tf_op jit(solution)/shard_map/add | solution.py:87
  10.0 0.0 copy-start.6
  10.0 0.4 copy.103
  10.4 0.1 add.30
  10.5 0.0 copy-done.5
  10.6 0.0 copy-start.3
  10.6 0.0 copy-start.4
  10.6 0.8 %copy.105 = f32[64,1,576]{2,1,0:T(1,128)} copy(f32[64,1,576]{2,0,1:T(8,128)S(1)} %maximum_bitcast_fusion.2) | data formatting | bytes 294912 | tf_op jit(solution)/shard_map/all_to_all | solution.py:123
  11.4 13.0 %all-to-all-start = ((f32[64,1,576]{2,1,0:T(1,128)}), f32[64,1,576]{2,1,0:T(1,128)S(1)}, u32[]{:S(2)}, u32[]{:S(2)}) async-start(f32[64,1,576]{2,1,0:T(1,128)} %copy.105), calls=%async_computation | async-start | bytes 327680 | tf_op jit(solution)/shard_map/all_to_all | solution.py:123
  24.4 0.0 copy-done.6
  24.5 11.6 %all-to-all-done = f32[64,1,576]{2,1,0:T(1,128)S(1)} async-done(((f32[64,1,576]{2,1,0:T(1,128)}), f32[64,1,576]{2,1,0:T(1,128)S(1)}, u32[]{:S(2)}, u32[]{:S(2)}) %all-to-all-start) | async-done | bytes 147488 | tf_op jit(solution)/shard_map/all_to_all | solution.py:123
  36.2 0.1 fusion.73
  36.3 0.0 copy-done.3
  36.3 0.0 copy-done.4
  36.3 0.1 select_reduce_fusion.1
  36.5 1.1 %fusion.15 = f32[64,6,256]{2,0,1:T(8,128)S(1)} fusion(f32[1,64,6,256]{3,1,0,2:T(8,128)S(1)} %get-tuple-element.46, f32[1,64,6,256]{3,1,0,2:T(8,128)S(1)} %get-tuple-element.45, f32[1,64,6,256]{3,1,0,2:T(8,128)S(1)} %get-tuple-element.44, f32[1,64,6,256]{3,1,0,2:T(8,128)S(1)} %get-tuple-element.43, f32[64,1,64]{2,0,1:T(8,128)S(1)} %get-tuple-element.50, ...), kind=kOutput, calls=%fused_computation.17 | convolution fusion | flops 303235072 | bytes 2031616 | tf_op jit(solution)/shard_map/kdj,djec->kec/dot_general | solution.py:132
  37.6 1.3 %collective-permute-start = (f32[64,2,256]{2,0,1:T(8,128)S(1)}, f32[64,2,256]{2,0,1:T(8,128)S(1)}, u32[]{:S(2)}, u32[]{:S(2)}) collective-permute-start(f32[64,2,256]{2,0,1:T(8,128)S(1)} %get-tuple-element.25), channel_id=1, source_target_pairs={{1,0},{2,1},{3,2},{5,4},{6,5},{7,6},{9,8},{10,9},{11,10},{13,12},{... | collective-permute-start | bytes 393224 | tf_op jit(solution)/shard_map/ppermute | solution.py:135
  38.9 4.0 %collective-permute-start.1 = (f32[64,2,256]{2,0,1:T(8,128)S(1)}, f32[64,2,256]{2,0,1:T(8,128)S(1)}, u32[]{:S(2)}, u32[]{:S(2)}) collective-permute-start(f32[64,2,256]{2,0,1:T(8,128)S(1)} %get-tuple-element.26), channel_id=1, source_target_pairs={{0,1},{1,2},{2,3},{4,5},{5,6},{6,7},{8,9},{9,10},{10,11},{12,13},{... | collective-permute-start | bytes 393224 | tf_op jit(solution)/shard_map/ppermute | solution.py:136
  42.9 1.3 %collective-permute-done = f32[64,2,256]{2,0,1:T(8,128)S(1)} collective-permute-done((f32[64,2,256]{2,0,1:T(8,128)S(1)}, f32[64,2,256]{2,0,1:T(8,128)S(1)}, u32[]{:S(2)}, u32[]{:S(2)}) %collective-permute-start) | collective-permute-done | bytes 131104 | tf_op jit(solution)/shard_map/ppermute | solution.py:135
  44.2 0.9 %collective-permute-done.1 = f32[64,2,256]{2,0,1:T(8,128)S(1)} collective-permute-done((f32[64,2,256]{2,0,1:T(8,128)S(1)}, f32[64,2,256]{2,0,1:T(8,128)S(1)}, u32[]{:S(2)}, u32[]{:S(2)}) %collective-permute-start.1) | collective-permute-done | bytes 131104 | tf_op jit(solution)/shard_map/ppermute | solution.py:136
  45.1 0.1 copy.110
  45.2 16.1 %all_to_all.17 = f32[64,2,256]{2,1,0:T(2,128)S(1)} all-to-all(f32[64,2,256]{2,1,0:T(2,128)S(1)} %copy.110), channel_id=1, replica_groups=mesh['mom'=64,'en'=4] {'mom'}, dimensions={0} | all-to-all | bytes 262144 | tf_op jit(solution)/shard_map/all_to_all | solution.py:138
  61.3 0.2 broadcast_in_dim_reshape.3
  61.4 0.7 %copy.111 = f32[1,2,64,2,128]{4,3,2,1,0:T(2,128)} copy(f32[1,2,64,2,128]{4,3,1,2,0:T(2,128)S(1)} %broadcast_in_dim_reshape.3) | data formatting | bytes 262144 | tf_op jit(solution)/shard_map/broadcast_in_dim;reshape | solution.py:140
  (42 shorter events, 0.7 us)
Async XLA Ops:
  0.0 1.2 %copy-start.2 = (f32[1,2,2,128]{3,2,1,0:T(2,128)S(1)}, f32[1,2,2,128]{3,2,1,0:T(2,128)}, u32[]{:S(2)}) copy-start(f32[1,2,2,128]{3,2,1,0:T(2,128)} %param.10) | copy-start | bytes 6148
  0.0 1.3 %copy-start = (f32[1,2,2,128,128]{4,3,2,1,0:T(8,128)S(1)}, f32[1,2,2,128,128]{4,3,2,1,0:T(8,128)}, u32[]{:S(2)}) copy-start(f32[1,2,2,128,128]{4,3,2,1,0:T(8,128)} %param.9) | copy-start | bytes 786436
  4.0 0.8 %copy-start.1 = (s32[2,128,32]{1,2,0:T(8,128)S(1)}, s32[2,128,32]{1,2,0:T(8,128)}, u32[]{:S(2)}) copy-start(s32[2,128,32]{1,2,0:T(8,128)} %param.11) | copy-start | bytes 98308
  9.1 1.4 %copy-start.5 = (s32[1,64]{1,0:T(1,128)S(1)}, s32[1,64]{1,0:T(1,128)}, u32[]{:S(2)}) copy-start(s32[1,64]{1,0:T(1,128)} %param.13) | copy-start | bytes 772
  10.0 14.5 %copy-start.6 = (s32[6]{0:T(128)S(1)}, s32[6]{0:T(128)}, u32[]{:S(2)}) copy-start(s32[6]{0:T(128)} %param.12) | copy-start | bytes 76
  10.6 25.7 %copy-start.3 = (f32[6]{0:T(128)S(1)}, f32[6]{0:T(128)}, u32[]{:S(2)}) copy-start(f32[6]{0:T(128)} %param.14) | copy-start | bytes 76
  10.6 25.7 %copy-start.4 = (f32[6]{0:T(128)S(1)}, f32[6]{0:T(128)}, u32[]{:S(2)}) copy-start(f32[6]{0:T(128)} %param.15) | copy-start | bytes 76
  11.4 24.6 %all-to-all-start = ((f32[64,1,576]{2,1,0:T(1,128)}), f32[64,1,576]{2,1,0:T(1,128)S(1)}, u32[]{:S(2)}, u32[]{:S(2)}) async-start(f32[64,1,576]{2,1,0:T(1,128)} %copy.105), calls=%async_computation | async-start | bytes 327680 | tf_op jit(solution)/shard_map/all_to_all | solution.py:123
  37.6 6.6 %collective-permute-start = (f32[64,2,256]{2,0,1:T(8,128)S(1)}, f32[64,2,256]{2,0,1:T(8,128)S(1)}, u32[]{:S(2)}, u32[]{:S(2)}) collective-permute-start(f32[64,2,256]{2,0,1:T(8,128)S(1)} %get-tuple-element.25), channel_id=1, source_target_pairs={{1,0},{2,1},{3,2},{5,4},{6,5},{7,6},{9,8},{10,9},{11,10},{13,12},{... | collective-permute-start | bytes 393224 | tf_op jit(solution)/shard_map/ppermute | solution.py:135
  38.9 6.2 %collective-permute-start.1 = (f32[64,2,256]{2,0,1:T(8,128)S(1)}, f32[64,2,256]{2,0,1:T(8,128)S(1)}, u32[]{:S(2)}, u32[]{:S(2)}) collective-permute-start(f32[64,2,256]{2,0,1:T(8,128)S(1)} %get-tuple-element.26), channel_id=1, source_target_pairs={{0,1},{1,2},{2,3},{4,5},{5,6},{6,7},{8,9},{9,10},{10,11},{12,13},{... | collective-permute-start | bytes 393224 | tf_op jit(solution)/shard_map/ppermute | solution.py:136

commit v13 on v12

--- a/solution.py
+++ b/solution.py
@@ -129,12 +129,15 @@
     windows = jnp.stack(
         [data[:, SHIFT_MAX + offset : SHIFT_MAX + offset + reach] for offset in OFFSETS]
     )
-    part = jnp.einsum("kdj,djec->kec", weights, windows, precision=HIGH)
+    edges = jnp.concatenate([windows[:, :, :SHIFT_MAX], windows[:, :, SHIFT_MAX + local :]], axis=2)
+    edge = jnp.einsum("kdj,djec->kec", weights, edges, precision=HIGH)
     down = [(i, i - 1) for i in range(1, groups)]
     up = [(i, i + 1) for i in range(groups - 1)]
-    from_up = lax.ppermute(part[:, :SHIFT_MAX], "en", down)
-    from_down = lax.ppermute(part[:, SHIFT_MAX + local :], "en", up)
-    own = part[:, SHIFT_MAX : SHIFT_MAX + local] + from_up + from_down
+    from_up = lax.ppermute(edge[:, :SHIFT_MAX], "en", down)
+    from_down = lax.ppermute(edge[:, SHIFT_MAX:], "en", up)
+    inside = windows[:, :, SHIFT_MAX : SHIFT_MAX + local]
+    own = lax.optimization_barrier(jnp.einsum("kdj,djec->kec", weights, inside, precision=HIGH))
+    own = own + from_up + from_down
     back = lax.all_to_all(own, "mom", 0, 0)
     result = jnp.swapaxes(back, 0, 1).reshape(pairs.shape)
     return result[None]

time: 62.8 us -> 65.8 us (1.048)
  local copies, waits for them, and re-layouts: 4.32 us -> 6.55 us
  other arithmetic: 1.59 us -> 2.57 us
    squeeze x5, local copies, waits for them, and re-layouts: 0.09 us -> 0.96 us  [block(): real, imag = (value[..., 0, :, :], value[..., 1, :, :])]
    neg x7, other arithmetic: 0.1 us -> 0.94 us  [block(): top = jnp.concatenate([real, -imag], axis=-1)]
    slice x1, local copies, waits for them, and re-layouts: 0.01 us -> 0.76 us  [slab_pairs(): diagonal = eye[None] * injection[:, slab][:, None, :]]
    unnamed x21 -> x17, local copies, waits for them, and re-layouts: 1.57 us -> 2.08 us
  transfers between devices with their start and end apart: 3 -> 3, of which waited for: 3 -> 3; matrix products, arithmetic and copies ran while one was open for 0% -> 1% of each run, Pallas kernels for 0% -> 0%
where the time goes in v13:
time: 65.8 us; the launch traced here: 65 us
  starting transfers between devices  18.2 us (28%)
  blocking collectives  16.1 us (24%)
  waiting for transfers between devices  13.3 us (20%)
  matrix products  7.71 us (12%)
  local copies, waits for them, and re-layouts  6.55 us (10%)
  other arithmetic  2.57 us (4%)
    all_to_all x1, blocking collectives, shards(): back = lax.all_to_all(own, 'mom', 0, 0)  16.1 us
    all_to_all x1, starting transfers between devices, shards(): sent = lax.all_to_all(jnp.concatenate([blocks, ids], axis=1), 'mom', 0, 0)  13 us
    all_to_all x1, waiting for transfers between devices, shards(): sent = lax.all_to_all(jnp.concatenate([blocks, ids], axis=1), 'mom', 0, 0)  11.6 us
    ppermute x1, starting transfers between devices, shards(): from_down = lax.ppermute(edge[:, SHIFT_MAX:], 'en', up)  3.99 us
    dot_general x1, matrix products, slab_pairs(): jnp.einsum('qesxoc,sojc->qesjxo', jnp.stack(pieces), selector, preferred_...  3.57 us
    dot_general x7, matrix products, cmul(): jnp.einsum(spec, block(left), column(right, adjoint), precision=CHAIN)  2.9 us
    unnamed x17, local copies, waits for them, and re-layouts  2.08 us
  transfers between devices with their start and end apart: 3, of which 3 were waited for; matrix products, arithmetic and copies ran while one was open for 1% of the time, Pallas kernels for 0%

profile of v13, /device:TPU:1, one launch (start us, length us, event | category | flops | bytes accessed | tf_op | source)
XLA Modules:
  0.0 65.0 jit_solution(332097664284667437)
XLA Ops:
  0.0 0.8 %fusion.118 = f32[128,128]{1,0:T(8,128)S(1)} fusion(f32[1,2,2,128,128]{4,3,2,1,0:T(8,128)} %param.9), kind=kLoop, calls=%fused_computation.182 | loop fusion | flops 16384 | bytes 131072 | tf_op jit(solution)/shard_map/neg | solution.py:29
  0.9 0.9 %slice_bitcast_fusion.17 = (f32[128,128]{1,0:T(8,128)S(1)}, f32[128,128]{1,0:T(8,128)S(1)}) fusion(f32[1,2,2,128,128]{4,3,2,1,0:T(8,128)} %param.9), kind=kLoop, calls=%fused_computation.160 | loop fusion | bytes 262144 | tf_op jit(solution)/shard_map/squeeze | solution.py:28
  1.7 0.8 %fusion.130 = (f32[2,1,128]{2,1,0:T(1,128)S(1)}, f32[2,1,128]{2,1,0:T(1,128)S(1)}) fusion(f32[2,2,128]{2,1,0:T(2,128)} %bitcast.198), kind=kLoop, calls=%fused_computation.193 | loop fusion | bytes 4096 | tf_op jit(solution)/shard_map/slice | solution.py:69
  2.5 1.1 %copy.139 = f32[1,2,2,2,128,128]{5,4,1,3,2,0:T(8,128)S(1)} copy(f32[1,2,2,2,128,128]{5,4,3,2,1,0:T(8,128)} %param.8) | data formatting | bytes 1048576 | tf_op args[0]
  3.8 0.4 fusion.22
  4.2 0.4 fusion.38
  4.8 0.6 fusion.7
  5.5 0.4 fusion.30
  5.9 0.4 fusion.42
  6.4 0.0 copy-start.3
  6.4 0.0 copy-start
  6.5 0.4 fusion.50
  6.9 0.1 copy-done.3
  7.1 0.1 copy-done
  7.2 0.1 copy.90
  7.3 0.4 fusion.58
  7.7 0.2 reduce-precision_convert_fusion.1
  7.9 0.1 pad_maximum_fusion.1
  8.0 3.6 %fusion.4 = f32[3,2,2,32,2,128]{3,0,4,1,5,2:T(4,128)S(1)} fusion(s32[2,128,32]{2,1,0:T(8,128)S(1)} %copy.90, bf16[3,2,2,2,128,128]{5,4,3,2,1,0:T(8,128)(2,1)S(1)} %pad_maximum_fusion.1), kind=kOutput, calls=%fused_computation.4 | convolution fusion | flops 26214400 | bytes 1212416 | tf_op jit(solution)/shard_map/qesxoc,sojc->qesjxo/dot_general | solution.py:84
  11.5 0.8 %slice_add_fusion = f32[1,2,2,32,2,128]{3,0,4,1,5,2:T(1,128)S(1)} fusion(f32[3,2,2,32,2,128]{3,0,4,1,5,2:T(4,128)S(1)} %fusion.4), kind=kLoop, calls=%fused_computation.32 | loop fusion | flops 65536 | bytes 524288 | tf_op jit(solution)/shard_map/add | solution.py:87
  12.4 0.0 copy-start.4
  12.4 0.4 copy.103
  12.8 0.1 add.30
  13.0 0.8 %copy.105 = f32[64,1,576]{2,1,0:T(1,128)} copy(f32[64,1,576]{2,0,1:T(8,128)S(1)} %maximum_bitcast_fusion.2) | data formatting | bytes 294912 | tf_op jit(solution)/shard_map/all_to_all | solution.py:123
  13.8 13.0 %all-to-all-start = ((f32[64,1,576]{2,1,0:T(1,128)}), f32[64,1,576]{2,1,0:T(1,128)S(1)}, u32[]{:S(2)}, u32[]{:S(2)}) async-start(f32[64,1,576]{2,1,0:T(1,128)} %copy.105), calls=%async_computation | async-start | bytes 327680 | tf_op jit(solution)/shard_map/all_to_all | solution.py:123
  26.8 0.0 copy-done.4
  26.8 11.6 %all-to-all-done = f32[64,1,576]{2,1,0:T(1,128)S(1)} async-done(((f32[64,1,576]{2,1,0:T(1,128)}), f32[64,1,576]{2,1,0:T(1,128)S(1)}, u32[]{:S(2)}, u32[]{:S(2)}) %all-to-all-start) | async-done | bytes 147488 | tf_op jit(solution)/shard_map/all_to_all | solution.py:123
  38.5 0.1 fusion.66
  38.7 0.1 pad_maximum_fusion
  38.8 0.0 copy-start.1
  38.8 0.0 copy-start.2
  38.8 0.1 fusion.126
  38.9 0.5 copy-done.1
  39.5 0.0 copy-done.2
  39.5 0.1 select_reduce_fusion.1
  39.7 0.8 %convolution_bitcast_fusion = f32[64,4,256]{2,0,1:T(8,128)S(1)} fusion(f32[4,64,2,256]{3,1,0,2:T(8,128)S(1)} %get-tuple-element.15, f32[4,64,2,256]{3,1,0,2:T(8,128)S(1)} %get-tuple-element.14, f32[64,1,64]{2,0,1:T(8,128)S(1)} %get-tuple-element.52, f32[64,1,64]{2,0,1:T(8,128)S(1)} %get-tuple-element.51, f32[64,1,64]{2,0,1:T(8,128)S(1)} %get-tuple-element.10, ...), kind=kOutput, calls=%fused_computation.10 | convolution fusion | flops 201654272 | bytes 1376256 | tf_op jit(solution)/shard_map/kdj,djec->kec/dot_general | solution.py:133
  40.5 1.3 %collective-permute-start = (f32[64,2,256]{2,0,1:T(8,128)S(1)}, f32[64,2,256]{2,0,1:T(8,128)S(1)}, u32[]{:S(2)}, u32[]{:S(2)}) collective-permute-start(f32[64,2,256]{2,0,1:T(8,128)S(1)} %get-tuple-element.27), channel_id=1, source_target_pairs={{1,0},{2,1},{3,2},{5,4},{6,5},{7,6},{9,8},{10,9},{11,10},{13,12},{... | collective-permute-start | bytes 393224 | tf_op jit(solution)/shard_map/ppermute | solution.py:136
  41.8 4.0 %collective-permute-start.1 = (f32[64,2,256]{2,0,1:T(8,128)S(1)}, f32[64,2,256]{2,0,1:T(8,128)S(1)}, u32[]{:S(2)}, u32[]{:S(2)}) collective-permute-start(f32[64,2,256]{2,0,1:T(8,128)S(1)} %get-tuple-element.28), channel_id=1, source_target_pairs={{0,1},{1,2},{2,3},{4,5},{5,6},{6,7},{8,9},{9,10},{10,11},{12,13},{... | collective-permute-start | bytes 393224 | tf_op jit(solution)/shard_map/ppermute | solution.py:137
  45.8 0.5 convolution_bitcast_fusion.1
  46.2 0.8 %collective-permute-done = f32[64,2,256]{2,0,1:T(8,128)S(1)} collective-permute-done((f32[64,2,256]{2,0,1:T(8,128)S(1)}, f32[64,2,256]{2,0,1:T(8,128)S(1)}, u32[]{:S(2)}, u32[]{:S(2)}) %collective-permute-start) | collective-permute-done | bytes 131104 | tf_op jit(solution)/shard_map/ppermute | solution.py:136
  47.0 0.9 %collective-permute-done.1 = f32[64,2,256]{2,0,1:T(8,128)S(1)} collective-permute-done((f32[64,2,256]{2,0,1:T(8,128)S(1)}, f32[64,2,256]{2,0,1:T(8,128)S(1)}, u32[]{:S(2)}, u32[]{:S(2)}) %collective-permute-start.1) | collective-permute-done | bytes 131104 | tf_op jit(solution)/shard_map/ppermute | solution.py:137
  47.9 0.1 copy.110
  48.1 16.1 %all_to_all.17 = f32[64,2,256]{2,1,0:T(2,128)S(1)} all-to-all(f32[64,2,256]{2,1,0:T(2,128)S(1)} %copy.110), channel_id=1, replica_groups=mesh['mom'=64,'en'=4] {'mom'}, dimensions={0} | all-to-all | bytes 262144 | tf_op jit(solution)/shard_map/all_to_all | solution.py:141
  64.1 0.2 broadcast_in_dim_reshape.3
  64.3 0.7 %copy.111 = f32[1,2,64,2,128]{4,3,2,1,0:T(2,128)} copy(f32[1,2,64,2,128]{4,3,1,2,0:T(2,128)S(1)} %broadcast_in_dim_reshape.3) | data formatting | bytes 262144 | tf_op jit(solution)/shard_map/broadcast_in_dim;reshape | solution.py:143
  (39 shorter events, 0.7 us)
Async XLA Ops:
  6.4 0.7 %copy-start.3 = (s32[1,64]{1,0:T(1,128)S(1)}, s32[1,64]{1,0:T(1,128)}, u32[]{:S(2)}) copy-start(s32[1,64]{1,0:T(1,128)} %param.13) | copy-start | bytes 772
  6.4 0.8 %copy-start = (s32[2,128,32]{1,2,0:T(8,128)S(1)}, s32[2,128,32]{1,2,0:T(8,128)}, u32[]{:S(2)}) copy-start(s32[2,128,32]{1,2,0:T(8,128)} %param.11) | copy-start | bytes 98308
  12.4 14.4 %copy-start.4 = (s32[6]{0:T(128)S(1)}, s32[6]{0:T(128)}, u32[]{:S(2)}) copy-start(s32[6]{0:T(128)} %param.12) | copy-start | bytes 76
  13.8 24.6 %all-to-all-start = ((f32[64,1,576]{2,1,0:T(1,128)}), f32[64,1,576]{2,1,0:T(1,128)S(1)}, u32[]{:S(2)}, u32[]{:S(2)}) async-start(f32[64,1,576]{2,1,0:T(1,128)} %copy.105), calls=%async_computation | async-start | bytes 327680 | tf_op jit(solution)/shard_map/all_to_all | solution.py:123
  38.8 0.7 %copy-start.1 = (f32[6]{0:T(128)S(1)}, f32[6]{0:T(128)}, u32[]{:S(2)}) copy-start(f32[6]{0:T(128)} %param.14) | copy-start | bytes 76
  38.8 0.7 %copy-start.2 = (f32[6]{0:T(128)S(1)}, f32[6]{0:T(128)}, u32[]{:S(2)}) copy-start(f32[6]{0:T(128)} %param.15) | copy-start | bytes 76
  40.5 6.6 %collective-permute-start = (f32[64,2,256]{2,0,1:T(8,128)S(1)}, f32[64,2,256]{2,0,1:T(8,128)S(1)}, u32[]{:S(2)}, u32[]{:S(2)}) collective-permute-start(f32[64,2,256]{2,0,1:T(8,128)S(1)} %get-tuple-element.27), channel_id=1, source_target_pairs={{1,0},{2,1},{3,2},{5,4},{6,5},{7,6},{9,8},{10,9},{11,10},{13,12},{... | collective-permute-start | bytes 393224 | tf_op jit(solution)/shard_map/ppermute | solution.py:136
  41.8 6.2 %collective-permute-start.1 = (f32[64,2,256]{2,0,1:T(8,128)S(1)}, f32[64,2,256]{2,0,1:T(8,128)S(1)}, u32[]{:S(2)}, u32[]{:S(2)}) collective-permute-start(f32[64,2,256]{2,0,1:T(8,128)S(1)} %get-tuple-element.28), channel_id=1, source_target_pairs={{0,1},{1,2},{2,3},{4,5},{5,6},{6,7},{8,9},{9,10},{10,11},{12,13},{... | collective-permute-start | bytes 393224 | tf_op jit(solution)/shard_map/ppermute | solution.py:137

commit v14 on v12

--- a/solution.py
+++ b/solution.py
@@ -129,7 +129,7 @@
     windows = jnp.stack(
         [data[:, SHIFT_MAX + offset : SHIFT_MAX + offset + reach] for offset in OFFSETS]
     )
-    part = jnp.einsum("kdj,djec->kec", weights, windows, precision=HIGH)
+    part = jnp.einsum("kdj,djec->kec", weights, windows, precision=CHAIN)
     down = [(i, i - 1) for i in range(1, groups)]
     up = [(i, i + 1) for i in range(groups - 1)]
     from_up = lax.ppermute(part[:, :SHIFT_MAX], "en", down)

time: 62.8 us -> 62.4 us (level)
  no operation moved by 1% of the time
where the time goes in v14:
time: 62.4 us; the launch traced here: 61.7 us
  starting transfers between devices  18.3 us (29%)
  blocking collectives  16.1 us (26%)
  waiting for transfers between devices  13.8 us (22%)
  matrix products  7.08 us (11%)
  local copies, waits for them, and re-layouts  4.32 us (7%)
  other arithmetic  1.59 us (3%)
    all_to_all x1, blocking collectives, shards(): back = lax.all_to_all(own, 'mom', 0, 0)  16.1 us
    all_to_all x1, starting transfers between devices, shards(): sent = lax.all_to_all(jnp.concatenate([blocks, ids], axis=1), 'mom', 0, 0)  13 us
    all_to_all x1, waiting for transfers between devices, shards(): sent = lax.all_to_all(jnp.concatenate([blocks, ids], axis=1), 'mom', 0, 0)  11.6 us
    ppermute x1, starting transfers between devices, shards(): from_down = lax.ppermute(part[:, SHIFT_MAX + local:], 'en', up)  3.99 us
    dot_general x1, matrix products, slab_pairs(): jnp.einsum('qesxoc,sojc->qesjxo', jnp.stack(pieces), selector, preferred_...  3.57 us
    dot_general x7, matrix products, cmul(): jnp.einsum(spec, block(left), column(right, adjoint), precision=CHAIN)  2.89 us
    unnamed x21, local copies, waits for them, and re-layouts  1.57 us
    ppermute x1, starting transfers between devices, shards(): from_up = lax.ppermute(part[:, :SHIFT_MAX], 'en', down)  1.29 us
  transfers between devices with their start and end apart: 3, of which 3 were waited for; matrix products, arithmetic and copies ran while one was open for 0% of the time, Pallas kernels for 0%

profile of v14, /device:TPU:1, one launch (start us, length us, event | category | flops | bytes accessed | tf_op | source)
XLA Modules:
  0.0 61.7 jit_solution(1906601519305906145)
XLA Ops:
  0.0 0.0 copy-start.2
  0.0 0.0 copy-start
  0.0 1.1 %copy.138 = f32[1,2,2,2,128,128]{5,4,1,3,2,0:T(8,128)S(1)} copy(f32[1,2,2,2,128,128]{5,4,3,2,1,0:T(8,128)} %param.8) | data formatting | bytes 1048576 | tf_op args[0]
  1.2 0.0 copy-done.2
  1.3 0.0 copy-done
  1.4 0.4 fusion.29
  1.8 0.4 fusion.45
  2.4 0.6 fusion.18
  3.1 0.4 fusion.37
  3.5 0.4 fusion.49
  4.0 0.0 copy-start.1
  4.1 0.4 fusion.57
  4.5 0.2 copy-done.1
  4.8 0.1 copy.90
  4.9 0.4 fusion.65
  5.3 0.2 reduce-precision_convert_fusion.1
  5.4 0.1 pad_maximum_fusion
  5.5 3.6 %fusion.4 = f32[3,2,2,32,2,128]{3,0,4,1,5,2:T(4,128)S(1)} fusion(s32[2,128,32]{2,1,0:T(8,128)S(1)} %copy.90, bf16[3,2,2,2,128,128]{5,4,3,2,1,0:T(8,128)(2,1)S(1)} %pad_maximum_fusion), kind=kOutput, calls=%fused_computation.4 | convolution fusion | flops 26214400 | bytes 1212416 | tf_op jit(solution)/shard_map/qesxoc,sojc->qesjxo/dot_general | solution.py:84
  9.1 0.0 copy-start.5
  9.1 0.8 %slice_add_fusion = f32[1,2,2,32,2,128]{3,0,4,1,5,2:T(1,128)S(1)} fusion(f32[3,2,2,32,2,128]{3,0,4,1,5,2:T(4,128)S(1)} %fusion.4), kind=kLoop, calls=%fused_computation.34 | loop fusion | flops 65536 | bytes 524288 | tf_op jit(solution)/shard_map/add | solution.py:87
  10.0 0.0 copy-start.6
  10.0 0.4 copy.103
  10.4 0.1 add.30
  10.5 0.0 copy-done.5
  10.6 0.0 copy-start.3
  10.6 0.0 copy-start.4
  10.6 0.8 %copy.105 = f32[64,1,576]{2,1,0:T(1,128)} copy(f32[64,1,576]{2,0,1:T(8,128)S(1)} %maximum_bitcast_fusion.2) | data formatting | bytes 294912 | tf_op jit(solution)/shard_map/all_to_all | solution.py:123
  11.4 13.0 %all-to-all-start = ((f32[64,1,576]{2,1,0:T(1,128)}), f32[64,1,576]{2,1,0:T(1,128)S(1)}, u32[]{:S(2)}, u32[]{:S(2)}) async-start(f32[64,1,576]{2,1,0:T(1,128)} %copy.105), calls=%async_computation | async-start | bytes 327680 | tf_op jit(solution)/shard_map/all_to_all | solution.py:123
  24.4 0.0 copy-done.6
  24.5 11.6 %all-to-all-done = f32[64,1,576]{2,1,0:T(1,128)S(1)} async-done(((f32[64,1,576]{2,1,0:T(1,128)}), f32[64,1,576]{2,1,0:T(1,128)S(1)}, u32[]{:S(2)}, u32[]{:S(2)}) %all-to-all-start) | async-done | bytes 147488 | tf_op jit(solution)/shard_map/all_to_all | solution.py:123
  36.2 0.1 fusion.73
  36.3 0.0 copy-done.3
  36.3 0.0 copy-done.4
  36.3 0.1 select_reduce_fusion.1
  36.5 0.6 fusion.15
  37.2 1.3 %collective-permute-start = (f32[64,2,256]{2,0,1:T(8,128)S(1)}, f32[64,2,256]{2,0,1:T(8,128)S(1)}, u32[]{:S(2)}, u32[]{:S(2)}) collective-permute-start(f32[64,2,256]{2,0,1:T(8,128)S(1)} %get-tuple-element.25), channel_id=1, source_target_pairs={{1,0},{2,1},{3,2},{5,4},{6,5},{7,6},{9,8},{10,9},{11,10},{13,12},{... | collective-permute-start | bytes 393224 | tf_op jit(solution)/shard_map/ppermute | solution.py:135
  38.5 4.0 %collective-permute-start.1 = (f32[64,2,256]{2,0,1:T(8,128)S(1)}, f32[64,2,256]{2,0,1:T(8,128)S(1)}, u32[]{:S(2)}, u32[]{:S(2)}) collective-permute-start(f32[64,2,256]{2,0,1:T(8,128)S(1)} %get-tuple-element.26), channel_id=1, source_target_pairs={{0,1},{1,2},{2,3},{4,5},{5,6},{6,7},{8,9},{9,10},{10,11},{12,13},{... | collective-permute-start | bytes 393224 | tf_op jit(solution)/shard_map/ppermute | solution.py:136
  42.5 1.3 %collective-permute-done = f32[64,2,256]{2,0,1:T(8,128)S(1)} collective-permute-done((f32[64,2,256]{2,0,1:T(8,128)S(1)}, f32[64,2,256]{2,0,1:T(8,128)S(1)}, u32[]{:S(2)}, u32[]{:S(2)}) %collective-permute-start) | collective-permute-done | bytes 131104 | tf_op jit(solution)/shard_map/ppermute | solution.py:135
  43.7 0.9 %collective-permute-done.1 = f32[64,2,256]{2,0,1:T(8,128)S(1)} collective-permute-done((f32[64,2,256]{2,0,1:T(8,128)S(1)}, f32[64,2,256]{2,0,1:T(8,128)S(1)}, u32[]{:S(2)}, u32[]{:S(2)}) %collective-permute-start.1) | collective-permute-done | bytes 131104 | tf_op jit(solution)/shard_map/ppermute | solution.py:136
  44.6 0.1 copy.110
  44.8 16.1 %all_to_all.17 = f32[64,2,256]{2,1,0:T(2,128)S(1)} all-to-all(f32[64,2,256]{2,1,0:T(2,128)S(1)} %copy.110), channel_id=1, replica_groups=mesh['mom'=64,'en'=4] {'mom'}, dimensions={0} | all-to-all | bytes 262144 | tf_op jit(solution)/shard_map/all_to_all | solution.py:138
  60.8 0.2 broadcast_in_dim_reshape.3
  61.0 0.7 %copy.111 = f32[1,2,64,2,128]{4,3,2,1,0:T(2,128)} copy(f32[1,2,64,2,128]{4,3,1,2,0:T(2,128)S(1)} %broadcast_in_dim_reshape.3) | data formatting | bytes 262144 | tf_op jit(solution)/shard_map/broadcast_in_dim;reshape | solution.py:140
  (42 shorter events, 0.7 us)
Async XLA Ops:
  0.0 1.2 %copy-start.2 = (f32[1,2,2,128]{3,2,1,0:T(2,128)S(1)}, f32[1,2,2,128]{3,2,1,0:T(2,128)}, u32[]{:S(2)}) copy-start(f32[1,2,2,128]{3,2,1,0:T(2,128)} %param.10) | copy-start | bytes 6148
  0.0 1.3 %copy-start = (f32[1,2,2,128,128]{4,3,2,1,0:T(8,128)S(1)}, f32[1,2,2,128,128]{4,3,2,1,0:T(8,128)}, u32[]{:S(2)}) copy-start(f32[1,2,2,128,128]{4,3,2,1,0:T(8,128)} %param.9) | copy-start | bytes 786436
  4.0 0.8 %copy-start.1 = (s32[2,128,32]{1,2,0:T(8,128)S(1)}, s32[2,128,32]{1,2,0:T(8,128)}, u32[]{:S(2)}) copy-start(s32[2,128,32]{1,2,0:T(8,128)} %param.11) | copy-start | bytes 98308
  9.1 1.4 %copy-start.5 = (s32[1,64]{1,0:T(1,128)S(1)}, s32[1,64]{1,0:T(1,128)}, u32[]{:S(2)}) copy-start(s32[1,64]{1,0:T(1,128)} %param.13) | copy-start | bytes 772
  10.0 14.5 %copy-start.6 = (s32[6]{0:T(128)S(1)}, s32[6]{0:T(128)}, u32[]{:S(2)}) copy-start(s32[6]{0:T(128)} %param.12) | copy-start | bytes 76
  10.6 25.7 %copy-start.3 = (f32[6]{0:T(128)S(1)}, f32[6]{0:T(128)}, u32[]{:S(2)}) copy-start(f32[6]{0:T(128)} %param.14) | copy-start | bytes 76
  10.6 25.7 %copy-start.4 = (f32[6]{0:T(128)S(1)}, f32[6]{0:T(128)}, u32[]{:S(2)}) copy-start(f32[6]{0:T(128)} %param.15) | copy-start | bytes 76
  11.4 24.6 %all-to-all-start = ((f32[64,1,576]{2,1,0:T(1,128)}), f32[64,1,576]{2,1,0:T(1,128)S(1)}, u32[]{:S(2)}, u32[]{:S(2)}) async-start(f32[64,1,576]{2,1,0:T(1,128)} %copy.105), calls=%async_computation | async-start | bytes 327680 | tf_op jit(solution)/shard_map/all_to_all | solution.py:123
  37.2 6.6 %collective-permute-start = (f32[64,2,256]{2,0,1:T(8,128)S(1)}, f32[64,2,256]{2,0,1:T(8,128)S(1)}, u32[]{:S(2)}, u32[]{:S(2)}) collective-permute-start(f32[64,2,256]{2,0,1:T(8,128)S(1)} %get-tuple-element.25), channel_id=1, source_target_pairs={{1,0},{2,1},{3,2},{5,4},{6,5},{7,6},{9,8},{10,9},{11,10},{13,12},{... | collective-permute-start | bytes 393224 | tf_op jit(solution)/shard_map/ppermute | solution.py:135
  38.5 6.2 %collective-permute-start.1 = (f32[64,2,256]{2,0,1:T(8,128)S(1)}, f32[64,2,256]{2,0,1:T(8,128)S(1)}, u32[]{:S(2)}, u32[]{:S(2)}) collective-permute-start(f32[64,2,256]{2,0,1:T(8,128)S(1)} %get-tuple-element.26), channel_id=1, source_target_pairs={{0,1},{1,2},{2,3},{4,5},{5,6},{6,7},{8,9},{9,10},{10,11},{12,13},{... | collective-permute-start | bytes 393224 | tf_op jit(solution)/shard_map/ppermute | solution.py:136

commit v15 on v14

--- a/solution.py
+++ b/solution.py
@@ -130,10 +130,13 @@
         [data[:, SHIFT_MAX + offset : SHIFT_MAX + offset + reach] for offset in OFFSETS]
     )
     part = jnp.einsum("kdj,djec->kec", weights, windows, precision=CHAIN)
-    down = [(i, i - 1) for i in range(1, groups)]
-    up = [(i, i + 1) for i in range(groups - 1)]
+    down = [(i, (i - 1) % groups) for i in range(groups)]
+    up = [(i, (i + 1) % groups) for i in range(groups)]
+    place = lax.axis_index("en")
     from_up = lax.ppermute(part[:, :SHIFT_MAX], "en", down)
+    from_up = jnp.where(place == groups - 1, 0.0, from_up)
     from_down = lax.ppermute(part[:, SHIFT_MAX + local :], "en", up)
+    from_down = jnp.where(place == 0, 0.0, from_down)
     own = part[:, SHIFT_MAX : SHIFT_MAX + local] + from_up + from_down
     back = lax.all_to_all(own, "mom", 0, 0)
     result = jnp.swapaxes(back, 0, 1).reshape(pairs.shape)

time: 62.4 us -> 62.9 us (level)
  waiting for transfers between devices: 13.8 us -> 17.2 us
  starting transfers between devices: 18.3 us -> 15.8 us
    ppermute x1, starting transfers between devices: 3.99 us -> 0.01 us  [shards(): from_down = lax.ppermute(part[:, SHIFT_MAX + local:], 'en', up)]
    ppermute x1, waiting for transfers between devices: 0.9 us -> 3.13 us  [shards(): from_down = lax.ppermute(part[:, SHIFT_MAX + local:], 'en', up)]
    ppermute x1, starting transfers between devices: 1.29 us -> 2.81 us  [shards(): from_up = lax.ppermute(part[:, :SHIFT_MAX], 'en', down)]
    ppermute x1, waiting for transfers between devices: 1.25 us -> 2.46 us  [shards(): from_up = lax.ppermute(part[:, :SHIFT_MAX], 'en', down)]
where the time goes in v15:
time: 62.9 us; the launch traced here: 62.6 us
  waiting for transfers between devices  17.2 us (27%)
  blocking collectives  16.1 us (26%)
  starting transfers between devices  15.8 us (25%)
  matrix products  7.08 us (11%)
  local copies, waits for them, and re-layouts  4.32 us (7%)
  other arithmetic  1.59 us (3%)
    all_to_all x1, blocking collectives, shards(): back = lax.all_to_all(own, 'mom', 0, 0)  16.1 us
    all_to_all x1, starting transfers between devices, shards(): sent = lax.all_to_all(jnp.concatenate([blocks, ids], axis=1), 'mom', 0, 0)  13 us
    all_to_all x1, waiting for transfers between devices, shards(): sent = lax.all_to_all(jnp.concatenate([blocks, ids], axis=1), 'mom', 0, 0)  11.6 us
    dot_general x1, matrix products, slab_pairs(): jnp.einsum('qesxoc,sojc->qesjxo', jnp.stack(pieces), selector, preferred_...  3.57 us
    ppermute x1, waiting for transfers between devices, shards(): from_down = lax.ppermute(part[:, SHIFT_MAX + local:], 'en', up)  3.13 us
    dot_general x7, matrix products, cmul(): jnp.einsum(spec, block(left), column(right, adjoint), precision=CHAIN)  2.89 us
    ppermute x1, starting transfers between devices, shards(): from_up = lax.ppermute(part[:, :SHIFT_MAX], 'en', down)  2.81 us
    ppermute x1, waiting for transfers between devices, shards(): from_up = lax.ppermute(part[:, :SHIFT_MAX], 'en', down)  2.46 us
  transfers between devices with their start and end apart: 3, of which 3 were waited for; matrix products, arithmetic and copies ran while one was open for 0% of the time, Pallas kernels for 0%

profile of v15, /device:TPU:1, one launch (start us, length us, event | category | flops | bytes accessed | tf_op | source)
XLA Modules:
  0.0 62.6 jit_solution(17735486958695747713)
XLA Ops:
  0.0 0.0 copy-start.2
  0.0 0.0 copy-start
  0.0 1.1 %copy.138 = f32[1,2,2,2,128,128]{5,4,1,3,2,0:T(8,128)S(1)} copy(f32[1,2,2,2,128,128]{5,4,3,2,1,0:T(8,128)} %param.8) | data formatting | bytes 1048576 | tf_op args[0]
  1.2 0.0 copy-done.2
  1.3 0.0 copy-done
  1.4 0.4 fusion.29
  1.8 0.4 fusion.45
  2.4 0.6 fusion.18
  3.1 0.4 fusion.37
  3.5 0.4 fusion.49
  4.0 0.0 copy-start.1
  4.1 0.4 fusion.57
  4.5 0.2 copy-done.1
  4.8 0.1 copy.90
  4.9 0.4 fusion.65
  5.3 0.2 reduce-precision_convert_fusion.1
  5.4 0.1 pad_maximum_fusion
  5.5 3.6 %fusion.4 = f32[3,2,2,32,2,128]{3,0,4,1,5,2:T(4,128)S(1)} fusion(s32[2,128,32]{2,1,0:T(8,128)S(1)} %copy.90, bf16[3,2,2,2,128,128]{5,4,3,2,1,0:T(8,128)(2,1)S(1)} %pad_maximum_fusion), kind=kOutput, calls=%fused_computation.4 | convolution fusion | flops 26214400 | bytes 1212416 | tf_op jit(solution)/shard_map/qesxoc,sojc->qesjxo/dot_general | solution.py:84
  9.1 0.0 copy-start.5
  9.1 0.8 %slice_add_fusion = f32[1,2,2,32,2,128]{3,0,4,1,5,2:T(1,128)S(1)} fusion(f32[3,2,2,32,2,128]{3,0,4,1,5,2:T(4,128)S(1)} %fusion.4), kind=kLoop, calls=%fused_computation.34 | loop fusion | flops 65536 | bytes 524288 | tf_op jit(solution)/shard_map/add | solution.py:87
  10.0 0.0 copy-start.6
  10.0 0.4 copy.103
  10.4 0.1 add.30
  10.5 0.0 copy-done.5
  10.6 0.0 copy-start.3
  10.6 0.0 copy-start.4
  10.6 0.8 %copy.105 = f32[64,1,576]{2,1,0:T(1,128)} copy(f32[64,1,576]{2,0,1:T(8,128)S(1)} %maximum_bitcast_fusion.2) | data formatting | bytes 294912 | tf_op jit(solution)/shard_map/all_to_all | solution.py:123
  11.4 13.0 %all-to-all-start = ((f32[64,1,576]{2,1,0:T(1,128)}), f32[64,1,576]{2,1,0:T(1,128)S(1)}, u32[]{:S(2)}, u32[]{:S(2)}) async-start(f32[64,1,576]{2,1,0:T(1,128)} %copy.105), calls=%async_computation | async-start | bytes 327680 | tf_op jit(solution)/shard_map/all_to_all | solution.py:123
  24.4 0.0 copy-done.6
  24.5 11.6 %all-to-all-done = f32[64,1,576]{2,1,0:T(1,128)S(1)} async-done(((f32[64,1,576]{2,1,0:T(1,128)}), f32[64,1,576]{2,1,0:T(1,128)S(1)}, u32[]{:S(2)}, u32[]{:S(2)}) %all-to-all-start) | async-done | bytes 147488 | tf_op jit(solution)/shard_map/all_to_all | solution.py:123
  36.2 0.1 fusion.73
  36.3 0.0 copy-done.3
  36.3 0.0 copy-done.4
  36.3 0.1 select_reduce_fusion.1
  36.5 0.6 fusion.15
  37.2 2.8 %collective-permute-start = (f32[64,2,256]{2,0,1:T(8,128)S(1)}, f32[64,2,256]{2,0,1:T(8,128)S(1)}, u32[]{:S(2)}, u32[]{:S(2)}) collective-permute-start(f32[64,2,256]{2,0,1:T(8,128)S(1)} %get-tuple-element.25), channel_id=1, source_target_pairs={{0,3},{1,0},{2,1},{3,2},{4,7},{5,4},{6,5},{7,6},{8,11},{9,8},{10,9... | collective-permute-start | bytes 393224 | tf_op jit(solution)/shard_map/ppermute | solution.py:136
  40.0 0.0 collective-permute-start.1
  40.0 2.5 %collective-permute-done = f32[64,2,256]{2,0,1:T(8,128)S(1)} collective-permute-done((f32[64,2,256]{2,0,1:T(8,128)S(1)}, f32[64,2,256]{2,0,1:T(8,128)S(1)}, u32[]{:S(2)}, u32[]{:S(2)}) %collective-permute-start) | collective-permute-done | bytes 131104 | tf_op jit(solution)/shard_map/ppermute | solution.py:136
  42.4 3.1 %collective-permute-done.1 = f32[64,2,256]{2,0,1:T(8,128)S(1)} collective-permute-done((f32[64,2,256]{2,0,1:T(8,128)S(1)}, f32[64,2,256]{2,0,1:T(8,128)S(1)}, u32[]{:S(2)}, u32[]{:S(2)}) %collective-permute-start.1) | collective-permute-done | bytes 131104 | tf_op jit(solution)/shard_map/ppermute | solution.py:138
  45.6 0.1 copy.110
  45.7 16.1 %all_to_all.17 = f32[64,2,256]{2,1,0:T(2,128)S(1)} all-to-all(f32[64,2,256]{2,1,0:T(2,128)S(1)} %copy.110), channel_id=1, replica_groups=mesh['mom'=64,'en'=4] {'mom'}, dimensions={0} | all-to-all | bytes 262144 | tf_op jit(solution)/shard_map/all_to_all | solution.py:141
  61.8 0.2 broadcast_in_dim_reshape.3
  61.9 0.7 %copy.111 = f32[1,2,64,2,128]{4,3,2,1,0:T(2,128)} copy(f32[1,2,64,2,128]{4,3,1,2,0:T(2,128)S(1)} %broadcast_in_dim_reshape.3) | data formatting | bytes 262144 | tf_op jit(solution)/shard_map/broadcast_in_dim;reshape | solution.py:143
  (42 shorter events, 0.7 us)
Async XLA Ops:
  0.0 1.2 %copy-start.2 = (f32[1,2,2,128]{3,2,1,0:T(2,128)S(1)}, f32[1,2,2,128]{3,2,1,0:T(2,128)}, u32[]{:S(2)}) copy-start(f32[1,2,2,128]{3,2,1,0:T(2,128)} %param.10) | copy-start | bytes 6148
  0.0 1.3 %copy-start = (f32[1,2,2,128,128]{4,3,2,1,0:T(8,128)S(1)}, f32[1,2,2,128,128]{4,3,2,1,0:T(8,128)}, u32[]{:S(2)}) copy-start(f32[1,2,2,128,128]{4,3,2,1,0:T(8,128)} %param.9) | copy-start | bytes 786436
  4.0 0.8 %copy-start.1 = (s32[2,128,32]{1,2,0:T(8,128)S(1)}, s32[2,128,32]{1,2,0:T(8,128)}, u32[]{:S(2)}) copy-start(s32[2,128,32]{1,2,0:T(8,128)} %param.11) | copy-start | bytes 98308
  9.1 1.4 %copy-start.5 = (s32[1,64]{1,0:T(1,128)S(1)}, s32[1,64]{1,0:T(1,128)}, u32[]{:S(2)}) copy-start(s32[1,64]{1,0:T(1,128)} %param.13) | copy-start | bytes 772
  10.0 14.5 %copy-start.6 = (s32[6]{0:T(128)S(1)}, s32[6]{0:T(128)}, u32[]{:S(2)}) copy-start(s32[6]{0:T(128)} %param.12) | copy-start | bytes 76
  10.6 25.7 %copy-start.3 = (f32[6]{0:T(128)S(1)}, f32[6]{0:T(128)}, u32[]{:S(2)}) copy-start(f32[6]{0:T(128)} %param.14) | copy-start | bytes 76
  10.6 25.7 %copy-start.4 = (f32[6]{0:T(128)S(1)}, f32[6]{0:T(128)}, u32[]{:S(2)}) copy-start(f32[6]{0:T(128)} %param.15) | copy-start | bytes 76
  11.4 24.6 %all-to-all-start = ((f32[64,1,576]{2,1,0:T(1,128)}), f32[64,1,576]{2,1,0:T(1,128)S(1)}, u32[]{:S(2)}, u32[]{:S(2)}) async-start(f32[64,1,576]{2,1,0:T(1,128)} %copy.105), calls=%async_computation | async-start | bytes 327680 | tf_op jit(solution)/shard_map/all_to_all | solution.py:123
  37.2 5.3 %collective-permute-start = (f32[64,2,256]{2,0,1:T(8,128)S(1)}, f32[64,2,256]{2,0,1:T(8,128)S(1)}, u32[]{:S(2)}, u32[]{:S(2)}) collective-permute-start(f32[64,2,256]{2,0,1:T(8,128)S(1)} %get-tuple-element.25), channel_id=1, source_target_pairs={{0,3},{1,0},{2,1},{3,2},{4,7},{5,4},{6,5},{7,6},{8,11},{9,8},{10,9... | collective-permute-start | bytes 393224 | tf_op jit(solution)/shard_map/ppermute | solution.py:136
  40.0 5.6 %collective-permute-start.1 = (f32[64,2,256]{2,0,1:T(8,128)S(1)}, f32[64,2,256]{2,0,1:T(8,128)S(1)}, u32[]{:S(2)}, u32[]{:S(2)}) collective-permute-start(f32[64,2,256]{2,0,1:T(8,128)S(1)} %get-tuple-element.26), channel_id=1, source_target_pairs={{0,1},{1,2},{2,3},{3,0},{4,5},{5,6},{6,7},{7,4},{8,9},{9,10},{10,1... | collective-permute-start | bytes 393224 | tf_op jit(solution)/shard_map/ppermute | solution.py:138

commit v16 on v14

--- a/solution.py
+++ b/solution.py
@@ -81,10 +81,9 @@
         rest = rest - piece
     columns = jnp.arange(orbitals, dtype=jnp.int32)
     selector = (neighbors[..., None] == columns).astype(jnp.bfloat16)
-    picked = jnp.einsum(
-        "qesxoc,sojc->qesjxo", jnp.stack(pieces), selector, preferred_element_type=jnp.float32
-    )
-    picked = picked[0] + picked[1] + picked[2]
+    selector = jnp.concatenate([selector] * len(pieces), axis=-1)
+    joined = jnp.concatenate(pieces, axis=-1)
+    picked = jnp.einsum("esxok,sojk->esjxo", joined, selector, preferred_element_type=jnp.float32)
     return picked.reshape(picked.shape[0], -1, picked.shape[3], picked.shape[4])
 
 

time: 62.4 us -> 64 us (1.026)
  local copies, waits for them, and re-layouts: 4.32 us -> 5.73 us
  other arithmetic: 1.59 us -> 2.79 us
  matrix products: 7.08 us -> 6.11 us
    eq x0 -> x1, other arithmetic: none -> 2 us  [slab_pairs(): selector = (neighbors[..., None] == columns).astype(jnp.bfloat16)]
    unnamed x21, local copies, waits for them, and re-layouts: 1.57 us -> 3.12 us
    dot_general x1, matrix products: 3.57 us -> 2.6 us  [slab_pairs(): jnp.einsum('esxok,sojk->esjxo', joined, selector, preferred_element_type=...]
    add x1 -> x0, other arithmetic: 0.81 us -> none  [slab_pairs(): picked = picked[0] + picked[1] + picked[2]]
where the time goes in v16:
time: 64 us; the launch traced here: 63.2 us
  starting transfers between devices  18.3 us (29%)
  blocking collectives  16.1 us (25%)
  waiting for transfers between devices  13.8 us (22%)
  matrix products  6.11 us (10%)
  local copies, waits for them, and re-layouts  5.73 us (9%)
  other arithmetic  2.79 us (4%)
    all_to_all x1, blocking collectives, shards(): back = lax.all_to_all(own, 'mom', 0, 0)  16.1 us
    all_to_all x1, starting transfers between devices, shards(): sent = lax.all_to_all(jnp.concatenate([blocks, ids], axis=1), 'mom', 0, 0)  13 us
    all_to_all x1, waiting for transfers between devices, shards(): sent = lax.all_to_all(jnp.concatenate([blocks, ids], axis=1), 'mom', 0, 0)  11.6 us
    ppermute x1, starting transfers between devices, shards(): from_down = lax.ppermute(part[:, SHIFT_MAX + local:], 'en', up)  3.99 us
    unnamed x21, local copies, waits for them, and re-layouts  3.12 us
    dot_general x7, matrix products, cmul(): jnp.einsum(spec, block(left), column(right, adjoint), precision=CHAIN)  2.89 us
    dot_general x1, matrix products, slab_pairs(): jnp.einsum('esxok,sojk->esjxo', joined, selector, preferred_element_type=...  2.6 us
    eq x1, other arithmetic, slab_pairs(): selector = (neighbors[..., None] == columns).astype(jnp.bfloat16)  2 us
  transfers between devices with their start and end apart: 3, of which 3 were waited for; matrix products, arithmetic and copies ran while one was open for 0% of the time, Pallas kernels for 0%

profile of v16, /device:TPU:1, one launch (start us, length us, event | category | flops | bytes accessed | tf_op | source)
XLA Modules:
  0.0 63.2 jit_solution(2872343812297583840)
XLA Ops:
  0.0 0.0 copy-start.2
  0.0 1.1 %copy.138 = f32[1,2,2,2,128,128]{5,4,1,3,2,0:T(8,128)S(1)} copy(f32[1,2,2,2,128,128]{5,4,3,2,1,0:T(8,128)} %param.8) | data formatting | bytes 1048576 | tf_op args[0]
  1.1 0.0 copy-start
  1.2 0.0 copy-done.2
  1.3 0.8 %copy-done = f32[1,2,2,128,128]{4,3,2,1,0:T(8,128)S(1)} copy-done((f32[1,2,2,128,128]{4,3,2,1,0:T(8,128)S(1)}, f32[1,2,2,128,128]{4,3,2,1,0:T(8,128)}, u32[]{:S(2)}) %copy-start) | copy-done | bytes 262168
  2.1 0.4 fusion.24
  2.6 0.4 fusion.40
  3.2 0.6 fusion.13
  3.9 0.4 fusion.32
  4.3 0.4 fusion.44
  4.9 0.0 copy-start.1
  4.9 0.4 fusion.52
  5.3 0.3 copy-done.1
  5.6 0.1 copy.90
  5.7 2.0 %iota_compare_fusion = pred[2,128,32,128]{3,2,1,0:T(32,128)(4,1)S(1)} fusion(s32[2,128,32]{2,1,0:T(8,128)S(1)} %copy.90), kind=kLoop, calls=%fused_computation.2 | loop fusion | flops 1048576 | bytes 1081344 | tf_op jit(solution)/shard_map/eq | solution.py:83
  7.7 0.4 fusion.60
  8.1 0.2 reduce-precision_convert_fusion.1
  8.3 0.1 pad_maximum_fusion
  8.4 2.6 %fusion.9 = f32[2,2,32,2,128]{2,3,0,4,1:T(2,128)S(1)} fusion(pred[2,128,32,128]{3,2,1,0:T(32,128)(4,1)S(1)} %iota_compare_fusion, bf16[2,2,2,128,384]{4,3,2,1,0:T(8,128)(2,1)S(1)} %pad_maximum_fusion), kind=kOutput, calls=%fused_computation.15 | convolution fusion | flops 31457280 | bytes 1966080 | tf_op jit(solution)/shard_map/esxok,sojk->esjxo/dot_general | solution.py:86
  11.0 0.0 copy-start.5
  11.0 0.0 copy-start.6
  11.0 0.3 copy.103
  11.3 0.1 reshape_reshape_reshape.3
  11.5 0.2 copy-done.5
  11.7 0.8 %copy.105 = f32[64,1,576]{2,1,0:T(1,128)} copy(f32[64,1,576]{2,0,1:T(8,128)S(1)} %maximum_bitcast_fusion.2) | data formatting | bytes 294912 | tf_op jit(solution)/shard_map/all_to_all | solution.py:122
  12.5 13.0 %all-to-all-start = ((f32[64,1,576]{2,1,0:T(1,128)}), f32[64,1,576]{2,1,0:T(1,128)S(1)}, u32[]{:S(2)}, u32[]{:S(2)}) async-start(f32[64,1,576]{2,1,0:T(1,128)} %copy.105), calls=%async_computation | async-start | bytes 327680 | tf_op jit(solution)/shard_map/all_to_all | solution.py:122
  25.5 0.0 copy-done.6
  25.5 11.6 %all-to-all-done = f32[64,1,576]{2,1,0:T(1,128)S(1)} async-done(((f32[64,1,576]{2,1,0:T(1,128)}), f32[64,1,576]{2,1,0:T(1,128)S(1)}, u32[]{:S(2)}, u32[]{:S(2)}) %all-to-all-start) | async-done | bytes 147488 | tf_op jit(solution)/shard_map/all_to_all | solution.py:122
  37.2 0.0 copy-start.3
  37.2 0.0 copy-start.4
  37.3 0.1 fusion.68
  37.4 0.5 copy-done.3
  37.9 0.0 copy-done.4
  37.9 0.1 select_reduce_fusion.1
  38.1 0.6 fusion.10
  38.7 1.3 %collective-permute-start = (f32[64,2,256]{2,0,1:T(8,128)S(1)}, f32[64,2,256]{2,0,1:T(8,128)S(1)}, u32[]{:S(2)}, u32[]{:S(2)}) collective-permute-start(f32[64,2,256]{2,0,1:T(8,128)S(1)} %get-tuple-element.25), channel_id=1, source_target_pairs={{1,0},{2,1},{3,2},{5,4},{6,5},{7,6},{9,8},{10,9},{11,10},{13,12},{... | collective-permute-start | bytes 393224 | tf_op jit(solution)/shard_map/ppermute | solution.py:134
  40.0 4.0 %collective-permute-start.1 = (f32[64,2,256]{2,0,1:T(8,128)S(1)}, f32[64,2,256]{2,0,1:T(8,128)S(1)}, u32[]{:S(2)}, u32[]{:S(2)}) collective-permute-start(f32[64,2,256]{2,0,1:T(8,128)S(1)} %get-tuple-element.26), channel_id=1, source_target_pairs={{0,1},{1,2},{2,3},{4,5},{5,6},{6,7},{8,9},{9,10},{10,11},{12,13},{... | collective-permute-start | bytes 393224 | tf_op jit(solution)/shard_map/ppermute | solution.py:135
  44.0 1.3 %collective-permute-done = f32[64,2,256]{2,0,1:T(8,128)S(1)} collective-permute-done((f32[64,2,256]{2,0,1:T(8,128)S(1)}, f32[64,2,256]{2,0,1:T(8,128)S(1)}, u32[]{:S(2)}, u32[]{:S(2)}) %collective-permute-start) | collective-permute-done | bytes 131104 | tf_op jit(solution)/shard_map/ppermute | solution.py:134
  45.3 0.9 %collective-permute-done.1 = f32[64,2,256]{2,0,1:T(8,128)S(1)} collective-permute-done((f32[64,2,256]{2,0,1:T(8,128)S(1)}, f32[64,2,256]{2,0,1:T(8,128)S(1)}, u32[]{:S(2)}, u32[]{:S(2)}) %collective-permute-start.1) | collective-permute-done | bytes 131104 | tf_op jit(solution)/shard_map/ppermute | solution.py:135
  46.2 0.1 copy.110
  46.3 16.1 %all_to_all.17 = f32[64,2,256]{2,1,0:T(2,128)S(1)} all-to-all(f32[64,2,256]{2,1,0:T(2,128)S(1)} %copy.110), channel_id=1, replica_groups=mesh['mom'=64,'en'=4] {'mom'}, dimensions={0} | all-to-all | bytes 262144 | tf_op jit(solution)/shard_map/all_to_all | solution.py:137
  62.4 0.2 broadcast_in_dim_reshape.3
  62.5 0.7 %copy.111 = f32[1,2,64,2,128]{4,3,2,1,0:T(2,128)} copy(f32[1,2,64,2,128]{4,3,1,2,0:T(2,128)S(1)} %broadcast_in_dim_reshape.3) | data formatting | bytes 262144 | tf_op jit(solution)/shard_map/broadcast_in_dim;reshape | solution.py:139
  (42 shorter events, 0.8 us)
Async XLA Ops:
  0.0 1.2 %copy-start.2 = (f32[1,2,2,128]{3,2,1,0:T(2,128)S(1)}, f32[1,2,2,128]{3,2,1,0:T(2,128)}, u32[]{:S(2)}) copy-start(f32[1,2,2,128]{3,2,1,0:T(2,128)} %param.10) | copy-start | bytes 6148
  1.1 1.0 %copy-start = (f32[1,2,2,128,128]{4,3,2,1,0:T(8,128)S(1)}, f32[1,2,2,128,128]{4,3,2,1,0:T(8,128)}, u32[]{:S(2)}) copy-start(f32[1,2,2,128,128]{4,3,2,1,0:T(8,128)} %param.9) | copy-start | bytes 786436
  4.9 0.8 %copy-start.1 = (s32[2,128,32]{1,2,0:T(8,128)S(1)}, s32[2,128,32]{1,2,0:T(8,128)}, u32[]{:S(2)}) copy-start(s32[2,128,32]{1,2,0:T(8,128)} %param.11) | copy-start | bytes 98308
  11.0 0.7 %copy-start.5 = (s32[1,64]{1,0:T(1,128)S(1)}, s32[1,64]{1,0:T(1,128)}, u32[]{:S(2)}) copy-start(s32[1,64]{1,0:T(1,128)} %param.13) | copy-start | bytes 772
  11.0 14.5 %copy-start.6 = (s32[6]{0:T(128)S(1)}, s32[6]{0:T(128)}, u32[]{:S(2)}) copy-start(s32[6]{0:T(128)} %param.12) | copy-start | bytes 76
  12.5 24.6 %all-to-all-start = ((f32[64,1,576]{2,1,0:T(1,128)}), f32[64,1,576]{2,1,0:T(1,128)S(1)}, u32[]{:S(2)}, u32[]{:S(2)}) async-start(f32[64,1,576]{2,1,0:T(1,128)} %copy.105), calls=%async_computation | async-start | bytes 327680 | tf_op jit(solution)/shard_map/all_to_all | solution.py:122
  37.2 0.7 %copy-start.3 = (f32[6]{0:T(128)S(1)}, f32[6]{0:T(128)}, u32[]{:S(2)}) copy-start(f32[6]{0:T(128)} %param.14) | copy-start | bytes 76
  37.2 0.7 %copy-start.4 = (f32[6]{0:T(128)S(1)}, f32[6]{0:T(128)}, u32[]{:S(2)}) copy-start(f32[6]{0:T(128)} %param.15) | copy-start | bytes 76
  38.7 6.6 %collective-permute-start = (f32[64,2,256]{2,0,1:T(8,128)S(1)}, f32[64,2,256]{2,0,1:T(8,128)S(1)}, u32[]{:S(2)}, u32[]{:S(2)}) collective-permute-start(f32[64,2,256]{2,0,1:T(8,128)S(1)} %get-tuple-element.25), channel_id=1, source_target_pairs={{1,0},{2,1},{3,2},{5,4},{6,5},{7,6},{9,8},{10,9},{11,10},{13,12},{... | collective-permute-start | bytes 393224 | tf_op jit(solution)/shard_map/ppermute | solution.py:134
  40.0 6.2 %collective-permute-start.1 = (f32[64,2,256]{2,0,1:T(8,128)S(1)}, f32[64,2,256]{2,0,1:T(8,128)S(1)}, u32[]{:S(2)}, u32[]{:S(2)}) collective-permute-start(f32[64,2,256]{2,0,1:T(8,128)S(1)} %get-tuple-element.26), channel_id=1, source_target_pairs={{0,1},{1,2},{2,3},{4,5},{5,6},{6,7},{8,9},{9,10},{10,11},{12,13},{... | collective-permute-start | bytes 393224 | tf_op jit(solution)/shard_map/ppermute | solution.py:135
